TPU v7x, 128 devices: a whole 4x4x4 slice. The times are simulated.
128 devices in a mesh: view: 4 (over y), block: 32 (over z, x, core).
Axes of the slice: x: 4, y: 4, z: 4, core: 2. Of those that a mesh axis runs over, the one named last changes fastest.
Arguments:
- estimate: float32 [512, 128, 256], P('block'), may hold values from 0.3 to 3
- observed: float32 [4, 512, 2, 128, 256], P('view', 'block'), may hold values from 0.2 to 5
- route_dest: int32 [4, 512], P('view', 'block'), may hold values from -1 to 31, as said below
- route_pos: int32 [4, 512], P('view', 'block'), may hold values from -1 to 15, as said below
- view_span: int32 [8, 2], P('view'), may hold values from 0 to 256, as said below
- view_count: int32 [256], P('block'), may hold values from 4 to 8, as said below
- psf_taps: float32 [8, 3, 31], P('view'), may hold values from 0 to 2, as said below
- view_weight: float32 [8], P('view'), may hold values from 1 to 4
Outputs:
- restored: float32 [512, 128, 256], P('block')
Inputs may be any that keep to these rules, and one draw needn't show every extreme that they name: `route_dest`: in each view group, every brick of one of its views that lies inside that view's sub-volume stands in exactly one slot of the group's devices, with its owner block and position (view of the group times 8 plus brick of the block); other slots hold -1. One device's slots send at most 1 bricks to one block, and some device sends 1 to some block. `route_pos`: position of the slot's brick as described for route_dest, -1 together with it. `view_span`: each sub-volume lies within the 256 bricks and holds at least 128 of them; the first view of each view group spans all of them. `view_count`: equals the number of views whose span holds the brick. `psf_taps`: each kernel is positive.
All inputs are finite; a program needn't handle non-finite values.
Results may differ from a plain program's by a relative error of at most 0.0003.
Values sent between devices are 32-bit elements; how exact they have to be, the bound alone decides.
No kernel may reach another device: no remote copies, remote signals or barrier semaphores. Data moves between devices by JAX's collectives and lax.ppermute only.
A program may use at most 128 MiB of HBM per device.

v0:
```python
import jax
import jax.numpy as jnp
from jax import lax
from jax.sharding import PartitionSpec as P

ITERS = 2


def with_halo(cells, sides, width):
    for axis, dim in sides:
        count = lax.axis_size(axis)
        ends = count - 1
        head = lax.slice_in_dim(cells, 0, width, axis=dim)
        tail = lax.slice_in_dim(cells, cells.shape[dim] - width, cells.shape[dim], axis=dim)
        cells = jnp.concatenate(
            [
                lax.ppermute(tail, axis, [(i, (i + 1) % count) for i in range(ends)]),
                cells,
                lax.ppermute(head, axis, [((i + 1) % count, i) for i in range(ends)]),
            ],
            axis=dim,
        )
    return cells


def banded_blur_matrix(filter_tap_values, row_count, col_count, offset_base, orientation):
    tap_count = filter_tap_values.shape[-1]
    grid_shape = (row_count, col_count, tap_count)
    row_index = lax.broadcasted_iota(jnp.int32, grid_shape, 0)
    col_index = lax.broadcasted_iota(jnp.int32, grid_shape, 1)
    tap_index = lax.broadcasted_iota(jnp.int32, grid_shape, 2)
    selected_entries = (orientation * (row_index - col_index) + offset_base == tap_index).astype(
        jnp.float32
    )
    return jnp.einsum(
        "ewq,gq->gew", selected_entries, filter_tap_values, precision=lax.Precision.HIGHEST
    )


def on_device(
    estimate, observed, route_dest, route_pos, view_span, view_count, psf_taps, view_weight
):
    highest = lax.Precision.HIGHEST
    blocks = lax.axis_size("block")
    slot_count = observed.shape[1]
    planes = observed.shape[2]
    ny_cells = observed.shape[3]
    nz_cells = observed.shape[4]
    per_group = view_span.shape[0]
    per_block = view_count.shape[0]
    capacity = max(1, slot_count // blocks)
    block_x = per_block * planes
    reach = psf_taps.shape[-1] // 2
    sources = observed[0]
    dest_list = route_dest[0]
    pos_list = route_pos[0]
    slot_index = jnp.arange(slot_count, dtype=jnp.int32)
    earlier = (dest_list[:, None] == dest_list[None, :]) & (
        slot_index[None, :] < slot_index[:, None]
    )
    rank_in_dest = jnp.sum(earlier.astype(jnp.int32), axis=1)
    target = jnp.where(dest_list >= 0, dest_list * capacity + rank_in_dest, blocks * capacity)
    outgoing = (
        jnp.zeros((blocks * capacity, planes, ny_cells, nz_cells), jnp.float32)
        .at[target]
        .set(sources, mode="drop")
    )
    out_pos = (
        jnp.full((blocks * capacity,), -1.0, jnp.float32)
        .at[target]
        .set(pos_list.astype(jnp.float32), mode="drop")
    )
    arrived, arrived_pos = (
        lax.all_to_all(
            outgoing.reshape(blocks, capacity, planes, ny_cells, nz_cells),
            "block",
            split_axis=0,
            concat_axis=0,
            tiled=True,
        ),
        lax.all_to_all(
            out_pos.reshape(blocks, capacity), "block", split_axis=0, concat_axis=0, tiled=True
        ),
    )
    places = arrived_pos.reshape(-1).astype(jnp.int32)
    places = jnp.where(places >= 0, places, per_group * per_block)
    placed = (
        jnp.zeros((per_group * per_block, planes, ny_cells, nz_cells), jnp.float32)
        .at[places]
        .set(arrived.reshape(-1, planes, ny_cells, nz_cells), mode="drop")
    )
    obs_views = placed.reshape(per_group, block_x, ny_cells, nz_cells)
    brick_index = lax.axis_index("block") * per_block + jnp.arange(per_block, dtype=jnp.int32)
    span_first = view_span[:, 0:1]
    span_length = view_span[:, 1:2]
    inside = (
        (brick_index[None, :] >= span_first) & (brick_index[None, :] < span_first + span_length)
    ).astype(jnp.float32)
    live_cells = jnp.repeat(inside, planes, axis=1)[:, :, None, None]
    counts = jnp.repeat(view_count.astype(jnp.float32), planes)[:, None, None]
    point_spread_kernels = psf_taps / jnp.sum(psf_taps, axis=-1, keepdims=True)
    fwd_x = banded_blur_matrix(point_spread_kernels[:, 0], block_x + 2 * reach, block_x, 0, 1)
    adj_x = banded_blur_matrix(
        point_spread_kernels[:, 0], block_x + 2 * reach, block_x, 2 * reach, -1
    )
    mat_y = banded_blur_matrix(point_spread_kernels[:, 1], ny_cells, ny_cells, reach, 1)
    mat_z = banded_blur_matrix(point_spread_kernels[:, 2], nz_cells, nz_cells, reach, 1)
    weights = view_weight[:, None, None, None]
    current = estimate
    for iteration in range(ITERS):
        padded = with_halo(current, (("block", 0),), reach)
        along_x = jnp.einsum("wyz,vwx->vxyz", padded, fwd_x, precision=highest)
        lateral_y_pass = jnp.einsum("vxyz,vyq->vxqz", along_x, mat_y, precision=highest)
        blurred = jnp.einsum("vxyz,vzq->vxyq", lateral_y_pass, mat_z, precision=highest)
        ratios = live_cells * (obs_views / blurred) + (1.0 - live_cells)
        back_z = jnp.einsum("vxyz,vqz->vxyq", ratios, mat_z, precision=highest)
        back_y = jnp.einsum("vxyz,vqy->vxqz", back_z, mat_y, precision=highest)
        rimmed = with_halo(back_y, (("block", 1),), reach)
        corrected = jnp.einsum("vwyz,vwx->vxyz", rimmed, adj_x, precision=highest)
        partial_logarithm = jnp.sum(live_cells * weights * jnp.log(corrected), axis=0)
        summed = lax.psum(partial_logarithm, "view")
        current = current * jnp.exp(summed / counts)
    return current


def solution(mesh):
    placed = (
        P("block", None, None),
        P("view", "block", None, None, None),
        P("view", "block"),
        P("view", "block"),
        P("view", None),
        P("block"),
        P("view", None, None),
        P("view"),
    )
    return jax.shard_map(
        on_device, mesh=mesh, in_specs=placed, out_specs=P("block", None, None), check_vma=False
    )
```

profile of v0, /device:TPU:64, one launch (start us, length us, event | category | flops | bytes accessed | tf_op | source)
XLA Modules:
  0.0 546.2 jit_solution(2459085685893780492)
XLA Ops:
  6.5 0.9 convert_reduce_fusion.1
  7.4 0.7 fusion.58
  8.1 0.7 convert_bitcast_fusion
  8.8 0.6 scatter_custom_fusion
  9.4 0.7 copy.91
  10.1 7.6 %all-to-all-start = ((f32[32,1,1]{2,1,0:T(1,128)}), f32[32,1,1]{2,1,0:T(1,128)S(1)}, u32[]{:S(2)}, u32[]{:S(2)}) async-start(f32[32,1,1]{2,1,0:T(1,128)} %copy.91), calls=%async_computation | async-start | bytes 32768 | tf_op jit(solution)/shard_map/all_to_all | solution.py:81
  17.7 4.2 broadcast_in_dim.37
  21.9 7.3 %scatter_fusion = f32[32,2,128,256]{3,2,1,0:T(8,128)} fusion(f32[32,2,128,256]{3,2,1,0:T(8,128)} %broadcast_in_dim.37, s32[16]{0:T(128)S(1)} %fusion.58, f32[16,2,128,256]{3,2,1,0:T(8,128)} %bitcast.92), kind=kCustom, calls=%fused_computation.1 | custom fusion | bytes 12582976 | tf_op jit(solution)/shard_map/scatter | solution.py:66
  29.3 8.0 %all-to-all-start.1 = ((f32[32,1,2,128,256]{4,3,2,1,0:T(8,128)}), f32[32,1,2,128,256]{4,3,2,1,0:T(8,128)}, u32[]{:S(2)}, u32[]{:S(2)}) async-start(f32[32,1,2,128,256]{4,3,2,1,0:T(8,128)} %bitcast.89), calls=%async_computation.1 | async-start | bytes 16777216 | tf_op jit(solution)/shard_map/all_to_all | solution.py:74
  37.3 2.3 fusion.70
  39.7 2.1 collective-permute-start
  41.8 6.0 %collective-permute-start.1 = (f32[15,128,256]{2,1,0:T(8,128)}, f32[15,128,256]{2,1,0:T(8,128)}, u32[]{:S(2)}, u32[]{:S(2)}) collective-permute-start(f32[15,128,256]{2,1,0:T(8,128)} %get-tuple-element.14), channel_id=1, source_target_pairs={{1,0},{2,1},{3,2},{4,3},{5,4},{6,5},{7,6},{8,7},{9,8},{10,9},{11,1... | collective-permute-start | bytes 5898248 | tf_op jit(solution)/shard_map/ppermute | solution.py:19
  47.9 2.5 copy.103
  50.4 0.1 reduce_sum.38
  50.6 0.8 fusion.42
  51.4 0.1 copy.118
  51.5 0.2 slice_reduce_fusion
  51.9 0.2 convolution_bitcast_fusion.2
  52.2 2.0 fusion.41
  54.3 0.7 convert_reduce_fusion
  54.9 99.5 %collective-permute-done = f32[15,128,256]{2,1,0:T(8,128)} collective-permute-done((f32[15,128,256]{2,1,0:T(8,128)}, f32[15,128,256]{2,1,0:T(8,128)}, u32[]{:S(2)}, u32[]{:S(2)}) %collective-permute-start) | collective-permute-done | bytes 1966112 | tf_op jit(solution)/shard_map/ppermute | solution.py:17
  154.5 2.7 copy.92
  157.2 2.7 copy.94
  159.9 4.7 fusion.5
  164.6 17.1 %fusion.29 = f32[2,128,16,256]{3,1,2,0:T(8,128)S(1)} fusion(f32[2,128,128,1]{1,2,3,0:T(8,128)S(1)} %copy.118, f32[2,16,128,256]{3,1,2,0:T(8,128)S(1)} %fusion.5), kind=kOutput, calls=%fused_computation.37 | convolution fusion | flops 1610612736 | bytes 8519680 | tf_op jit(solution)/shard_map/vxyz,vyq->vxqz/dot_general | solution.py:113
  181.7 4.9 fusion.17
  186.6 2.5 broadcast_in_dim.33
  189.1 13.5 %scatter_fusion.1 = f32[16,2,128,256]{3,2,1,0:T(8,128)} fusion(f32[16,2,128,256]{3,2,1,0:T(8,128)} %broadcast_in_dim.33, s32[32]{0:T(128)S(1)} %fusion.57, f32[32,2,128,256]{3,2,1,0:T(8,128)} %bitcast.15), kind=kCustom, calls=%fused_computation.2 | custom fusion | bytes 25165952 | tf_op jit(solution)/shard_map/scatter | solution.py:90
  202.6 6.4 %fusion.21 = f32[2,16,128,256]{3,2,1,0:T(8,128)S(1)} fusion(f32[2,16,128,256]{3,2,1,0:T(8,128)} %fusion.17, f32[2,16]{1,0:T(2,128)S(1)} %get-tuple-element.16, f32[2,16]{1,0:T(2,128)S(1)} %broadcast_in_dim_reshape.4, f32[2,256,256,1]{2,0,1,3:T(2,128)S(1)} %fusion.41, f32[2,16,128,256]{3,2,1,0:T(8,128)} %bitcast.90), kind=kOutput, calls=%fused_computation.31 | convolution fusion | flops 3224371200 | bytes 13107456 | tf_op jit(solution)/shard_map/vxyz,vqz->vxyq/dot_general | solution.py:116
  209.0 3.8 convolution_bitcast_fusion.1
  212.7 0.9 fusion.68
  213.7 2.6 collective-permute-start.2
  216.3 5.1 collective-permute-start.3
  221.4 0.2 convolution_bitcast_fusion.3
  221.6 41.2 %collective-permute-done.2 = f32[2,15,128,256]{3,2,1,0:T(8,128)S(1)} collective-permute-done((f32[2,15,128,256]{3,2,1,0:T(8,128)S(1)}, f32[2,15,128,256]{3,2,1,0:T(8,128)S(1)}, u32[]{:S(2)}, u32[]{:S(2)}) %collective-permute-start.2) | collective-permute-done | bytes 3932192 | tf_op jit(solution)/shard_map/ppermute | solution.py:17
  262.8 1.8 collective-permute-done.3
  264.6 2.7 pad_maximum_fusion
  267.3 13.2 %multiply_reduce_fusion.1 = f32[16,128,256]{2,0,1:T(8,128)} fusion(f32[2,46,128,256]{3,2,1,0:T(8,128)S(1)} %pad_maximum_fusion, f32[2,16]{1,0:T(2,128)S(1)} %get-tuple-element.15, f32[2,46,16,1]{1,0,2,3:T(2,128)S(1)} %convolution_bitcast_fusion.3), kind=kOutput, calls=%fused_computation.40 | convolution fusion | flops 580386816 | bytes 14161792 | tf_op jit(solution)/shard_map/vwyz,vwx->vxyz/dot_general | solution.py:119
  280.8 65.7 %all-reduce.3.cloned.1.call-done = f32[16,128,256]{2,0,1:T(8,128)} async-done(((f32[16,128,256]{2,0,1:T(8,128)}), f32[16,128,256]{2,0,1:T(8,128)}) %all-reduce.3.cloned.1.call-update) | async-done | bytes 2097168 | tf_op jit(solution)/shard_map/psum | solution.py:121
  346.4 3.6 exponential_multiply_fusion.1
  350.0 0.6 fusion.69
  350.6 1.1 copy.104
  351.7 1.9 collective-permute-start.4
  353.6 1.1 copy.105
  354.8 5.9 %collective-permute-start.5 = (f32[15,128,256]{2,1,0:T(8,128)S(1)}, f32[15,128,256]{2,1,0:T(8,128)S(1)}, u32[]{:S(2)}, u32[]{:S(2)}) collective-permute-start(f32[15,128,256]{2,1,0:T(8,128)S(1)} %copy.105), channel_id=1, source_target_pairs={{1,0},{2,1},{3,2},{4,3},{5,4},{6,5},{7,6},{8,7},{9,8},{10,9},{11,1... | collective-permute-start | bytes 5898248 | tf_op jit(solution)/shard_map/ppermute | solution.py:19
  360.7 19.1 %collective-permute-done.4 = f32[15,128,256]{2,1,0:T(8,128)S(1)} collective-permute-done((f32[15,128,256]{2,1,0:T(8,128)S(1)}, f32[15,128,256]{2,1,0:T(8,128)S(1)}, u32[]{:S(2)}, u32[]{:S(2)}) %collective-permute-start.4) | collective-permute-done | bytes 1966112 | tf_op jit(solution)/shard_map/ppermute | solution.py:17
  379.8 1.1 copy.106
  380.9 1.8 collective-permute-done.5
  382.7 1.1 copy.107
  383.8 4.7 fusion.10
  388.5 6.3 %fusion.27 = f32[2,128,16,256]{3,1,2,0:T(8,128)S(1)} fusion(f32[2,128,128,1]{1,2,3,0:T(8,128)S(1)} %copy.118, f32[2,16,128,256]{3,1,2,0:T(8,128)S(1)} %fusion.10), kind=kOutput, calls=%fused_computation.35 | convolution fusion | flops 1610612736 | bytes 8519680 | tf_op jit(solution)/shard_map/vxyz,vyq->vxqz/dot_general | solution.py:113
  394.9 3.7 fusion.15
  398.6 4.4 fusion.25
  403.0 4.0 convolution_bitcast_fusion
  407.0 0.9 fusion.67
  408.0 1.9 collective-permute-start.6
  409.9 5.9 %collective-permute-start.7 = (f32[2,15,128,256]{3,2,1,0:T(8,128)S(1)}, f32[2,15,128,256]{3,2,1,0:T(8,128)S(1)}, u32[]{:S(2)}, u32[]{:S(2)}) collective-permute-start(f32[2,15,128,256]{3,2,1,0:T(8,128)S(1)} %get-tuple-element.8), channel_id=1, source_target_pairs={{1,0},{2,1},{3,2},{4,3},{5,4},{6,5},{7,6},{8,7},{9,8},{10,9},{11,1... | collective-permute-start | bytes 11796488 | tf_op jit(solution)/shard_map/ppermute | solution.py:19
  415.8 41.4 %collective-permute-done.6 = f32[2,15,128,256]{3,2,1,0:T(8,128)S(1)} collective-permute-done((f32[2,15,128,256]{3,2,1,0:T(8,128)S(1)}, f32[2,15,128,256]{3,2,1,0:T(8,128)S(1)}, u32[]{:S(2)}, u32[]{:S(2)}) %collective-permute-start.6) | collective-permute-done | bytes 3932192 | tf_op jit(solution)/shard_map/ppermute | solution.py:17
  457.3 1.8 collective-permute-done.7
  459.0 2.5 pad_maximum_fusion.1
  461.5 13.2 %multiply_reduce_fusion = f32[16,128,256]{2,0,1:T(8,128)} fusion(f32[2,46,128,256]{3,2,1,0:T(8,128)S(1)} %pad_maximum_fusion.1, f32[2,16]{1,0:T(2,128)S(1)} %get-tuple-element.15, f32[2,46,16,1]{1,0,2,3:T(2,128)S(1)} %convolution_bitcast_fusion.3), kind=kOutput, calls=%fused_computation.39 | convolution fusion | flops 580386816 | bytes 14161792 | tf_op jit(solution)/shard_map/vwyz,vwx->vxyz/dot_general | solution.py:119
  474.8 59.5 %all-reduce.5.cloned.1.call-done = f32[16,128,256]{2,0,1:T(8,128)} async-done(((f32[16,128,256]{2,0,1:T(8,128)}), f32[16,128,256]{2,0,1:T(8,128)}) %all-reduce.5.cloned.1.call-update) | async-done | bytes 2097168 | tf_op jit(solution)/shard_map/psum | solution.py:121
  534.2 2.1 exponential_multiply_fusion
  536.4 2.5 copy.116
  (31 shorter events, 0.7 us)
Async XLA Ops:
  10.1 19.2 %all-to-all-start = ((f32[32,1,1]{2,1,0:T(1,128)}), f32[32,1,1]{2,1,0:T(1,128)S(1)}, u32[]{:S(2)}, u32[]{:S(2)}) async-start(f32[32,1,1]{2,1,0:T(1,128)} %copy.91), calls=%async_computation | async-start | bytes 32768 | tf_op jit(solution)/shard_map/all_to_all | solution.py:81
  29.3 8.1 %copy-start.1 = (f32[16,128,256]{2,1,0:T(8,128)S(1)}, f32[16,128,256]{2,1,0:T(8,128)}, u32[]{:S(2)}) copy-start(f32[16,128,256]{2,1,0:T(8,128)} %param.8) | copy-start | bytes 6291460
  29.3 157.4 %all-to-all-start.1 = ((f32[32,1,2,128,256]{4,3,2,1,0:T(8,128)}), f32[32,1,2,128,256]{4,3,2,1,0:T(8,128)}, u32[]{:S(2)}, u32[]{:S(2)}) async-start(f32[32,1,2,128,256]{4,3,2,1,0:T(8,128)} %bitcast.89), calls=%async_computation.1 | async-start | bytes 16777216 | tf_op jit(solution)/shard_map/all_to_all | solution.py:74
  37.3 13.1 %copy-start.3 = (f32[2,3,31]{2,0,1:T(2,128)S(1)}, f32[2,3,31]{2,0,1:T(2,128)}, u32[]{:S(2)}) copy-start(f32[2,3,31]{2,0,1:T(2,128)} %param.14) | copy-start | bytes 2236
  37.3 309.2 %all-reduce.3.cloned.1.call-start = ((), (), s32[]{:S(2)}) async-start(), calls=%async_computation.2 | async-start | bytes 4194304 | tf_op jit(solution)/shard_map/psum | solution.py:121
  39.7 11.8 %copy-start.4 = (s32[2,2]{1,0:T(2,128)S(1)}, s32[2,2]{1,0:T(2,128)}, u32[]{:S(2)}) copy-start(s32[2,2]{1,0:T(2,128)} %param.12) | copy-start | bytes 52
  39.7 12.4 %copy-start.5 = (f32[2]{0:T(128)S(1)}, f32[2]{0:T(128)}, u32[]{:S(2)}) copy-start(f32[2]{0:T(128)} %param.15) | copy-start | bytes 28
  39.7 114.8 %collective-permute-start = (f32[15,128,256]{2,1,0:T(8,128)}, f32[15,128,256]{2,1,0:T(8,128)}, u32[]{:S(2)}, u32[]{:S(2)}) collective-permute-start(f32[15,128,256]{2,1,0:T(8,128)} %get-tuple-element.13), channel_id=1, source_target_pairs={{0,1},{1,2},{2,3},{3,4},{4,5},{5,6},{6,7},{7,8},{8,9},{9,10},{10,1... | collective-permute-start | bytes 5898248 | tf_op jit(solution)/shard_map/ppermute | solution.py:17
  41.8 115.3 %collective-permute-start.1 = (f32[15,128,256]{2,1,0:T(8,128)}, f32[15,128,256]{2,1,0:T(8,128)}, u32[]{:S(2)}, u32[]{:S(2)}) collective-permute-start(f32[15,128,256]{2,1,0:T(8,128)} %get-tuple-element.14), channel_id=1, source_target_pairs={{1,0},{2,1},{3,2},{4,3},{5,4},{6,5},{7,6},{8,7},{9,8},{10,9},{11,1... | collective-permute-start | bytes 5898248 | tf_op jit(solution)/shard_map/ppermute | solution.py:19
  54.2 105.6 %copy-start.2 = (f32[16,128,256]{2,0,1:T(8,128)S(1)}, f32[16,128,256]{2,0,1:T(8,128)}, u32[]{:S(2)}) copy-start(f32[16,128,256]{2,0,1:T(8,128)} %copy.103) | copy-start | bytes 6291460
  213.7 49.1 %collective-permute-start.2 = (f32[2,15,128,256]{3,2,1,0:T(8,128)S(1)}, f32[2,15,128,256]{3,2,1,0:T(8,128)S(1)}, u32[]{:S(2)}, u32[]{:S(2)}) collective-permute-start(f32[2,15,128,256]{3,2,1,0:T(8,128)S(1)} %get-tuple-element.9), channel_id=1, source_target_pairs={{0,1},{1,2},{2,3},{3,4},{4,5},{5,6},{6,7},{7,8},{8,9},{9,10},{10,1... | collective-permute-start | bytes 11796488 | tf_op jit(solution)/shard_map/ppermute | solution.py:17
  216.3 48.3 %collective-permute-start.3 = (f32[2,15,128,256]{3,2,1,0:T(8,128)S(1)}, f32[2,15,128,256]{3,2,1,0:T(8,128)S(1)}, u32[]{:S(2)}, u32[]{:S(2)}) collective-permute-start(f32[2,15,128,256]{3,2,1,0:T(8,128)S(1)} %get-tuple-element.10), channel_id=1, source_target_pairs={{1,0},{2,1},{3,2},{4,3},{5,4},{6,5},{7,6},{8,7},{9,8},{10,9},{11,1... | collective-permute-start | bytes 11796488 | tf_op jit(solution)/shard_map/ppermute | solution.py:19
  267.3 13.3 %copy-start.6 = (s32[8]{0:T(128)S(1)}, s32[8]{0:T(128)}, u32[]{:S(2)}) copy-start(s32[8]{0:T(128)} %param.13) | copy-start | bytes 100
  280.5 253.7 %all-reduce.5.cloned.1.call-start = ((), (), s32[]{:S(2)}) async-start(), calls=%async_computation.3 | async-start | bytes 4194304 | tf_op jit(solution)/shard_map/psum | solution.py:121
  351.7 28.1 %collective-permute-start.4 = (f32[15,128,256]{2,1,0:T(8,128)S(1)}, f32[15,128,256]{2,1,0:T(8,128)S(1)}, u32[]{:S(2)}, u32[]{:S(2)}) collective-permute-start(f32[15,128,256]{2,1,0:T(8,128)S(1)} %copy.104), channel_id=1, source_target_pairs={{0,1},{1,2},{2,3},{3,4},{4,5},{5,6},{6,7},{7,8},{8,9},{9,10},{10,1... | collective-permute-start | bytes 5898248 | tf_op jit(solution)/shard_map/ppermute | solution.py:17
  354.8 27.9 %collective-permute-start.5 = (f32[15,128,256]{2,1,0:T(8,128)S(1)}, f32[15,128,256]{2,1,0:T(8,128)S(1)}, u32[]{:S(2)}, u32[]{:S(2)}) collective-permute-start(f32[15,128,256]{2,1,0:T(8,128)S(1)} %copy.105), channel_id=1, source_target_pairs={{1,0},{2,1},{3,2},{4,3},{5,4},{6,5},{7,6},{8,7},{9,8},{10,9},{11,1... | collective-permute-start | bytes 5898248 | tf_op jit(solution)/shard_map/ppermute | solution.py:19
  394.9 3.7 copy-start
  408.0 49.3 %collective-permute-start.6 = (f32[2,15,128,256]{3,2,1,0:T(8,128)S(1)}, f32[2,15,128,256]{3,2,1,0:T(8,128)S(1)}, u32[]{:S(2)}, u32[]{:S(2)}) collective-permute-start(f32[2,15,128,256]{3,2,1,0:T(8,128)S(1)} %get-tuple-element.7), channel_id=1, source_target_pairs={{0,1},{1,2},{2,3},{3,4},{4,5},{5,6},{6,7},{7,8},{8,9},{9,10},{10,1... | collective-permute-start | bytes 11796488 | tf_op jit(solution)/shard_map/ppermute | solution.py:17
  409.9 49.1 %collective-permute-start.7 = (f32[2,15,128,256]{3,2,1,0:T(8,128)S(1)}, f32[2,15,128,256]{3,2,1,0:T(8,128)S(1)}, u32[]{:S(2)}, u32[]{:S(2)}) collective-permute-start(f32[2,15,128,256]{3,2,1,0:T(8,128)S(1)} %get-tuple-element.8), channel_id=1, source_target_pairs={{1,0},{2,1},{3,2},{4,3},{5,4},{6,5},{7,6},{8,7},{9,8},{10,9},{11,1... | collective-permute-start | bytes 11796488 | tf_op jit(solution)/shard_map/ppermute | solution.py:19
Sparse Core Ops, SparseCore 0:
  280.6 65.7 all-reduce.2
  474.9 59.3 all-reduce.4
where the time goes:
time: 551 us; the launch traced here: 546 us
  waiting for transfers between devices  332 us (60%)
  matrix products  89.7 us (16%)
  local copies, waits for them, and re-layouts  49.1 us (9%)
  starting transfers between devices  47.2 us (9%)
  other arithmetic  14.2 us (3%)
  between operations  14.2 us (3%)
    ppermute x4, waiting for transfers between devices, with_halo(): lax.ppermute(tail, axis, [(i, (i + 1) % count) for i in range(ends)])  201 us
    psum x2, waiting for transfers between devices, on_device(): summed = lax.psum(partial_logarithm, 'view')  125 us
    dot_general x2, matrix products, on_device(): corrected = jnp.einsum('vwyz,vwx->vxyz', rimmed, adj_x, precision=highest)  26.5 us
    dot_general x2, matrix products, on_device(): jnp.einsum('vxyz,vyq->vxqz', along_x, mat_y, precision=highest)  23.4 us
    ppermute x4, starting transfers between devices, with_halo(): lax.ppermute(head, axis, [((i + 1) % count, i) for i in range(ends)])  23 us
    scatter x1, local copies, waits for them, and re-layouts, on_device(): placed = jnp.zeros((per_group * per_block, planes, ny_cells, nz_cells), j...  13.5 us
  transfers between devices with their start and end apart: 12, of which 9 were waited for; matrix products, arithmetic and copies ran while one was open for 10% of the time, Pallas kernels for 0%

commit v1 on v0

--- a/solution.py
+++ b/solution.py
@@ -21,6 +21,32 @@
             axis=dim,
         )
     return cells
+
+
+def view_sum_update(partial, current, counts):
+    count = lax.axis_size("view")
+    me = lax.axis_index("view")
+    rows = partial.shape[0] // count
+
+    def piece(cells, index):
+        return lax.dynamic_slice_in_dim(cells, index * rows, rows, axis=0)
+
+    summed = piece(partial, me)
+    for shift in range(1, count):
+        sent = piece(partial, (me + shift) % count)
+        summed = summed + lax.ppermute(
+            sent, "view", [(i, (i + shift) % count) for i in range(count)]
+        )
+    updated = piece(current, me) * jnp.exp(summed / piece(counts, me))
+    gathered = lax.dynamic_update_slice_in_dim(current, updated, me * rows, axis=0)
+    for shift in range(1, count):
+        arrived = lax.ppermute(
+            updated, "view", [(i, (i + shift) % count) for i in range(count)]
+        )
+        gathered = lax.dynamic_update_slice_in_dim(
+            gathered, arrived, ((me - shift) % count) * rows, axis=0
+        )
+    return gathered
 
 
 def banded_blur_matrix(filter_tap_values, row_count, col_count, offset_base, orientation):
@@ -118,8 +144,7 @@
         rimmed = with_halo(back_y, (("block", 1),), reach)
         corrected = jnp.einsum("vwyz,vwx->vxyz", rimmed, adj_x, precision=highest)
         partial_logarithm = jnp.sum(live_cells * weights * jnp.log(corrected), axis=0)
-        summed = lax.psum(partial_logarithm, "view")
-        current = current * jnp.exp(summed / counts)
+        current = view_sum_update(partial_logarithm, current, counts)
     return current
 
 

time: 551 us -> 518 us (0.940)
  waiting for transfers between devices: 332 us -> 310 us
  between operations: 14.2 us -> 0.77 us
  matrix products: 89.7 us -> 76.7 us
  local copies, waits for them, and re-layouts: 49.1 us -> 58.4 us
  starting transfers between devices: 47.2 us -> 53.6 us
    ppermute x4, waiting for transfers between devices: 5.27 us -> 203 us  [with_halo(): lax.ppermute(head, axis, [((i + 1) % count, i) for i in range(ends)])]
    ppermute x4, waiting for transfers between devices: 201 us -> 18.7 us  [with_halo(): lax.ppermute(tail, axis, [(i, (i + 1) % count) for i in range(ends)])]
    psum x2 -> x0, waiting for transfers between devices: 125 us -> none  [on_device(): summed = lax.psum(partial_logarithm, 'view')]
    ppermute x0 -> x12, waiting for transfers between devices: none -> 88.3 us  [the longest x6 45.9 us: view_sum_update(): lax.ppermute(updated, 'view', [(i, (i + shift) % count) for i in range(co...]
    ppermute x0 -> x12, starting transfers between devices: none -> 13.8 us  [the longest x6 7.08 us: view_sum_update(): lax.ppermute(updated, 'view', [(i, (i + shift) % count) for i in range(co...]
    dot_general x2, matrix products: 23.4 us -> 12.9 us  [on_device(): jnp.einsum('vxyz,vyq->vxqz', along_x, mat_y, precision=highest)]
    ppermute x4, starting transfers between devices: 23 us -> 16.1 us  [with_halo(): lax.ppermute(head, axis, [((i + 1) % count, i) for i in range(ends)])]
    mul x2 -> x0, other arithmetic: 5.69 us -> none  [on_device(): current = current * jnp.exp(summed / counts)]
  transfers between devices with their start and end apart: 12 -> 22, of which waited for: 9 -> 15; matrix products, arithmetic and copies ran while one was open for 10% -> 9% of each run, Pallas kernels for 0% -> 0%
where the time goes in v1:
time: 518 us; the launch traced here: 514 us
  waiting for transfers between devices  310 us (60%)
  matrix products  76.7 us (15%)
  local copies, waits for them, and re-layouts  58.4 us (11%)
  starting transfers between devices  53.6 us (10%)
  other arithmetic  15 us (3%)
    ppermute x4, waiting for transfers between devices, with_halo(): lax.ppermute(head, axis, [((i + 1) % count, i) for i in range(ends)])  203 us
    ppermute x6, waiting for transfers between devices, view_sum_update(): lax.ppermute(updated, 'view', [(i, (i + shift) % count) for i in range(co...  45.9 us
    ppermute x6, waiting for transfers between devices, view_sum_update(): lax.ppermute(sent, 'view', [(i, (i + shift) % count) for i in range(count)])  42.3 us
    dot_general x2, matrix products, on_device(): corrected = jnp.einsum('vwyz,vwx->vxyz', rimmed, adj_x, precision=highest)  24 us
    ppermute x4, waiting for transfers between devices, with_halo(): lax.ppermute(tail, axis, [(i, (i + 1) % count) for i in range(ends)])  18.7 us
    ppermute x4, starting transfers between devices, with_halo(): lax.ppermute(head, axis, [((i + 1) % count, i) for i in range(ends)])  16.1 us
    scatter x1, local copies, waits for them, and re-layouts, on_device(): placed = jnp.zeros((per_group * per_block, planes, ny_cells, nz_cells), j...  14 us
    dot_general x2, matrix products, on_device(): jnp.einsum('vxyz,vyq->vxqz', along_x, mat_y, precision=highest)  12.9 us
  transfers between devices with their start and end apart: 22, of which 15 were waited for; matrix products, arithmetic and copies ran while one was open for 9% of the time, Pallas kernels for 0%

profile of v1, /device:TPU:64, one launch (start us, length us, event | category | flops | bytes accessed | tf_op | source)
XLA Modules:
  0.0 514.2 jit_solution(8920090750570905733)
XLA Ops:
  3.6 7.6 %all-to-all-start = ((f32[32,1,1]{2,1,0:T(1,128)}), f32[32,1,1]{2,1,0:T(1,128)S(1)}, u32[]{:S(2)}, u32[]{:S(2)}) async-start(f32[32,1,1]{2,1,0:T(1,128)} %copy.95), calls=%async_computation | async-start | bytes 32768 | tf_op jit(solution)/shard_map/all_to_all | solution.py:107
  11.2 4.3 broadcast_in_dim.37
  15.4 7.7 %scatter_fusion = f32[32,2,128,256]{3,2,1,0:T(8,128)} fusion(f32[32,2,128,256]{3,2,1,0:T(8,128)} %broadcast_in_dim.37, s32[16]{0:T(128)S(1)} %fusion.59, f32[16,2,128,256]{3,2,1,0:T(8,128)} %bitcast.94), kind=kCustom, calls=%fused_computation.1 | custom fusion | bytes 12582976 | tf_op jit(solution)/shard_map/scatter | solution.py:92
  23.1 7.8 %all-to-all-start.1 = ((f32[32,1,2,128,256]{4,3,2,1,0:T(8,128)}), f32[32,1,2,128,256]{4,3,2,1,0:T(8,128)}, u32[]{:S(2)}, u32[]{:S(2)}) async-start(f32[32,1,2,128,256]{4,3,2,1,0:T(8,128)} %bitcast.91), calls=%async_computation.1 | async-start | bytes 16777216 | tf_op jit(solution)/shard_map/all_to_all | solution.py:100
  30.9 2.5 fusion.71
  33.5 4.4 collective-permute-start.1
  37.9 2.1 collective-permute-start
  40.0 1.2 copy.107
  43.0 2.0 fusion.41
  45.8 102.0 %collective-permute-done.1 = f32[15,128,256]{2,1,0:T(8,128)} collective-permute-done((f32[15,128,256]{2,1,0:T(8,128)}, f32[15,128,256]{2,1,0:T(8,128)}, u32[]{:S(2)}, u32[]{:S(2)}) %collective-permute-start.1) | collective-permute-done | bytes 1966112 | tf_op jit(solution)/shard_map/ppermute | solution.py:19
  147.8 2.7 copy.98
  150.5 2.7 copy.96
  153.2 4.7 fusion.5
  157.9 6.6 %fusion.29 = f32[2,128,16,256]{3,1,2,0:T(8,128)S(1)} fusion(f32[2,128,128,1]{1,2,3,0:T(8,128)S(1)} %copy.122, f32[2,16,128,256]{3,1,2,0:T(8,128)S(1)} %fusion.5), kind=kOutput, calls=%fused_computation.37 | convolution fusion | flops 1610612736 | bytes 8519680 | tf_op jit(solution)/shard_map/vxyz,vyq->vxqz/dot_general | solution.py:139
  164.5 5.0 fusion.17
  169.5 2.5 broadcast_in_dim.33
  171.9 14.0 %scatter_fusion.1 = f32[16,2,128,256]{3,2,1,0:T(8,128)} fusion(f32[16,2,128,256]{3,2,1,0:T(8,128)} %broadcast_in_dim.33, s32[32]{0:T(128)S(1)} %fusion.57, f32[32,2,128,256]{3,2,1,0:T(8,128)} %bitcast.15), kind=kCustom, calls=%fused_computation.2 | custom fusion | bytes 25165952 | tf_op jit(solution)/shard_map/scatter | solution.py:116
  185.9 6.4 %fusion.21 = f32[2,16,128,256]{3,2,1,0:T(8,128)S(1)} fusion(f32[2,16,128,256]{3,2,1,0:T(8,128)} %fusion.17, f32[2,16]{1,0:T(2,128)S(1)} %get-tuple-element.26, f32[2,16]{1,0:T(2,128)S(1)} %broadcast_in_dim_reshape.6, f32[2,256,256,1]{2,0,1,3:T(2,128)S(1)} %fusion.41, f32[2,16,128,256]{3,2,1,0:T(8,128)} %bitcast.92), kind=kOutput, calls=%fused_computation.31 | convolution fusion | flops 3224371200 | bytes 13107456 | tf_op jit(solution)/shard_map/vxyz,vqz->vxyq/dot_general | solution.py:142
  192.4 3.8 convolution_bitcast_fusion.1
  196.1 4.4 fusion.69
  200.5 5.5 %collective-permute-start.3 = (f32[2,15,128,256]{3,2,1,0:T(8,128)}, f32[2,15,128,256]{3,2,1,0:T(8,128)}, u32[]{:S(2)}, u32[]{:S(2)}) collective-permute-start(f32[2,15,128,256]{3,2,1,0:T(8,128)} %get-tuple-element.14), channel_id=1, source_target_pairs={{1,0},{2,1},{3,2},{4,3},{5,4},{6,5},{7,6},{8,7},{9,8},{10,9},{11,1... | collective-permute-start | bytes 11796488 | tf_op jit(solution)/shard_map/ppermute | solution.py:19
  206.1 1.9 collective-permute-start.2
  208.2 41.3 %collective-permute-done.3 = f32[2,15,128,256]{3,2,1,0:T(8,128)} collective-permute-done((f32[2,15,128,256]{3,2,1,0:T(8,128)}, f32[2,15,128,256]{3,2,1,0:T(8,128)}, u32[]{:S(2)}, u32[]{:S(2)}) %collective-permute-start.3) | collective-permute-done | bytes 3932192 | tf_op jit(solution)/shard_map/ppermute | solution.py:19
  249.6 6.5 %collective-permute-done.2 = f32[2,15,128,256]{3,2,1,0:T(8,128)} collective-permute-done((f32[2,15,128,256]{3,2,1,0:T(8,128)}, f32[2,15,128,256]{3,2,1,0:T(8,128)}, u32[]{:S(2)}, u32[]{:S(2)}) %collective-permute-start.2) | collective-permute-done | bytes 3932192 | tf_op jit(solution)/shard_map/ppermute | solution.py:17
  256.0 5.7 %pad_maximum_fusion = f32[2,46,128,256]{3,2,1,0:T(8,128)S(1)} fusion(f32[2,15,128,256]{3,2,1,0:T(8,128)} %collective-permute-done.3, f32[2,16,128,256]{3,2,1,0:T(8,128)} %copy-done, f32[2,15,128,256]{3,2,1,0:T(8,128)} %collective-permute-done.2), kind=kLoop, calls=%fused_computation.7 | loop fusion | flops 6029312 | bytes 24117248 | tf_op jit(solution)/shard_map/concatenate | solution.py:15
  261.8 12.0 %multiply_reduce_fusion.1 = f32[16,128,256]{2,0,1:T(8,128)S(1)} fusion(f32[2,46,128,256]{3,2,1,0:T(8,128)S(1)} %pad_maximum_fusion, f32[2,16]{1,0:T(2,128)S(1)} %get-tuple-element.25, f32[2,46,16,1]{1,0,2,3:T(2,128)S(1)} %convolution_bitcast_fusion.3), kind=kOutput, calls=%fused_computation.40 | convolution fusion | flops 580386816 | bytes 14161792 | tf_op jit(solution)/shard_map/vwyz,vwx->vxyz/dot_general | solution.py:145
  273.8 1.3 copy-done.4
  275.1 1.4 constant_dynamic-slice_fusion.6
  276.5 2.6 collective-permute-start.6
  279.1 1.1 collective-permute-start.5
  280.9 17.7 %collective-permute-done.6 = f32[4,128,256]{2,0,1:T(4,128)} collective-permute-done((f32[4,128,256]{2,0,1:T(4,128)}, f32[4,128,256]{2,0,1:T(4,128)}, u32[]{:S(2)}, u32[]{:S(2)}) %collective-permute-start.6) | collective-permute-done | bytes 524320 | tf_op jit(solution)/shard_map/ppermute | solution.py:37
  298.5 3.7 collective-permute-done.4
  302.2 3.0 constant_dynamic-update-slice_fusion.7
  305.2 2.1 collective-permute-start.8
  307.3 1.7 collective-permute-start.9
  309.0 22.8 %collective-permute-done.7 = f32[4,128,256]{2,0,1:T(4,128)} collective-permute-done((f32[4,128,256]{2,0,1:T(4,128)}, f32[4,128,256]{2,0,1:T(4,128)}, u32[]{:S(2)}, u32[]{:S(2)}) %collective-permute-start.7) | collective-permute-done | bytes 524320 | tf_op jit(solution)/shard_map/ppermute | solution.py:43
  331.8 1.2 constant_dynamic-update-slice_fusion.6
  333.0 1.2 constant_dynamic-update-slice_fusion.5
  334.9 1.1 copy.109
  336.1 4.2 collective-permute-start.11
  340.3 1.1 copy.108
  341.4 1.9 collective-permute-start.10
  343.3 18.6 %collective-permute-done.11 = f32[15,128,256]{2,1,0:T(8,128)S(1)} collective-permute-done((f32[15,128,256]{2,1,0:T(8,128)S(1)}, f32[15,128,256]{2,1,0:T(8,128)S(1)}, u32[]{:S(2)}, u32[]{:S(2)}) %collective-permute-start.11) | collective-permute-done | bytes 1966112 | tf_op jit(solution)/shard_map/ppermute | solution.py:19
  362.0 1.1 copy.111
  363.1 6.3 %collective-permute-done.10 = f32[15,128,256]{2,1,0:T(8,128)S(1)} collective-permute-done((f32[15,128,256]{2,1,0:T(8,128)S(1)}, f32[15,128,256]{2,1,0:T(8,128)S(1)}, u32[]{:S(2)}, u32[]{:S(2)}) %collective-permute-start.10) | collective-permute-done | bytes 1966112 | tf_op jit(solution)/shard_map/ppermute | solution.py:17
  369.5 1.1 copy.110
  370.6 4.7 fusion.10
  375.3 6.3 %fusion.27 = f32[2,128,16,256]{3,1,2,0:T(8,128)S(1)} fusion(f32[2,128,128,1]{1,2,3,0:T(8,128)S(1)} %copy.122, f32[2,16,128,256]{3,1,2,0:T(8,128)S(1)} %fusion.10), kind=kOutput, calls=%fused_computation.35 | convolution fusion | flops 1610612736 | bytes 8519680 | tf_op jit(solution)/shard_map/vxyz,vyq->vxqz/dot_general | solution.py:139
  381.7 3.7 fusion.15
  385.4 4.4 fusion.25
  389.8 4.0 convolution_bitcast_fusion
  394.7 1.9 collective-permute-start.13
  396.6 2.4 collective-permute-start.12
  399.0 40.8 %collective-permute-done.13 = f32[2,15,128,256]{3,2,1,0:T(8,128)S(1)} collective-permute-done((f32[2,15,128,256]{3,2,1,0:T(8,128)S(1)}, f32[2,15,128,256]{3,2,1,0:T(8,128)S(1)}, u32[]{:S(2)}, u32[]{:S(2)}) %collective-permute-start.13) | collective-permute-done | bytes 3932192 | tf_op jit(solution)/shard_map/ppermute | solution.py:19
  439.8 5.9 %collective-permute-done.12 = f32[2,15,128,256]{3,2,1,0:T(8,128)S(1)} collective-permute-done((f32[2,15,128,256]{3,2,1,0:T(8,128)S(1)}, f32[2,15,128,256]{3,2,1,0:T(8,128)S(1)}, u32[]{:S(2)}, u32[]{:S(2)}) %collective-permute-start.12) | collective-permute-done | bytes 3932192 | tf_op jit(solution)/shard_map/ppermute | solution.py:17
  445.8 2.3 pad_maximum_fusion.1
  448.0 12.0 %multiply_reduce_fusion = f32[16,128,256]{2,0,1:T(8,128)S(1)} fusion(f32[2,46,128,256]{3,2,1,0:T(8,128)S(1)} %pad_maximum_fusion.1, f32[2,16]{1,0:T(2,128)S(1)} %get-tuple-element.25, f32[2,46,16,1]{1,0,2,3:T(2,128)S(1)} %convolution_bitcast_fusion.3), kind=kOutput, calls=%fused_computation.39 | convolution fusion | flops 580386816 | bytes 14161792 | tf_op jit(solution)/shard_map/vwyz,vwx->vxyz/dot_general | solution.py:145
  460.4 1.6 collective-permute-start.16
  463.0 12.3 %collective-permute-done.16 = f32[4,128,256]{2,0,1:T(4,128)S(1)} collective-permute-done((f32[4,128,256]{2,0,1:T(4,128)S(1)}, f32[4,128,256]{2,0,1:T(4,128)S(1)}, u32[]{:S(2)}, u32[]{:S(2)}) %collective-permute-start.16) | collective-permute-done | bytes 524320 | tf_op jit(solution)/shard_map/ppermute | solution.py:37
  475.3 3.1 collective-permute-done.15
  478.4 5.6 %collective-permute-done.14 = f32[4,128,256]{2,0,1:T(4,128)S(1)} collective-permute-done((f32[4,128,256]{2,0,1:T(4,128)S(1)}, f32[4,128,256]{2,0,1:T(4,128)S(1)}, u32[]{:S(2)}, u32[]{:S(2)}) %collective-permute-start.14) | collective-permute-done | bytes 524320 | tf_op jit(solution)/shard_map/ppermute | solution.py:37
  484.7 2.3 collective-permute-start.18
  487.9 22.8 %collective-permute-done.17 = f32[4,128,256]{2,0,1:T(4,128)S(1)} collective-permute-done((f32[4,128,256]{2,0,1:T(4,128)S(1)}, f32[4,128,256]{2,0,1:T(4,128)S(1)}, u32[]{:S(2)}, u32[]{:S(2)}) %collective-permute-start.17) | collective-permute-done | bytes 524320 | tf_op jit(solution)/shard_map/ppermute | solution.py:43
  511.4 2.5 copy.120
  (62 shorter events, 12.2 us)
Async XLA Ops:
  3.6 19.5 %all-to-all-start = ((f32[32,1,1]{2,1,0:T(1,128)}), f32[32,1,1]{2,1,0:T(1,128)S(1)}, u32[]{:S(2)}, u32[]{:S(2)}) async-start(f32[32,1,1]{2,1,0:T(1,128)} %copy.95), calls=%async_computation | async-start | bytes 32768 | tf_op jit(solution)/shard_map/all_to_all | solution.py:107
  23.1 7.8 %copy-start.2 = (f32[16,128,256]{2,1,0:T(8,128)S(1)}, f32[16,128,256]{2,1,0:T(8,128)}, u32[]{:S(2)}) copy-start(f32[16,128,256]{2,1,0:T(8,128)} %param.8) | copy-start | bytes 6291460
  23.1 146.4 %all-to-all-start.1 = ((f32[32,1,2,128,256]{4,3,2,1,0:T(8,128)}), f32[32,1,2,128,256]{4,3,2,1,0:T(8,128)}, u32[]{:S(2)}, u32[]{:S(2)}) async-start(f32[32,1,2,128,256]{4,3,2,1,0:T(8,128)} %bitcast.91), calls=%async_computation.1 | async-start | bytes 16777216 | tf_op jit(solution)/shard_map/all_to_all | solution.py:100
  30.9 9.1 %copy-start.3 = (f32[16,128,256]{2,1,0:T(8,128)S(1)}, f32[16,128,256]{2,1,0:T(8,128)}, u32[]{:S(2)}) copy-start(f32[16,128,256]{2,1,0:T(8,128)} %param.8) | copy-start | bytes 6291460
  30.9 10.3 %copy-start.5 = (f32[2,3,31]{2,0,1:T(2,128)S(1)}, f32[2,3,31]{2,0,1:T(2,128)}, u32[]{:S(2)}) copy-start(f32[2,3,31]{2,0,1:T(2,128)} %param.14) | copy-start | bytes 2236
  33.5 8.9 %copy-start.6 = (s32[2,2]{1,0:T(2,128)S(1)}, s32[2,2]{1,0:T(2,128)}, u32[]{:S(2)}) copy-start(s32[2,2]{1,0:T(2,128)} %param.12) | copy-start | bytes 52
  33.5 9.5 %copy-start.7 = (f32[2]{0:T(128)S(1)}, f32[2]{0:T(128)}, u32[]{:S(2)}) copy-start(f32[2]{0:T(128)} %param.15) | copy-start | bytes 28
  33.5 114.3 %collective-permute-start.1 = (f32[15,128,256]{2,1,0:T(8,128)}, f32[15,128,256]{2,1,0:T(8,128)}, u32[]{:S(2)}, u32[]{:S(2)}) collective-permute-start(f32[15,128,256]{2,1,0:T(8,128)} %get-tuple-element.24), channel_id=1, source_target_pairs={{1,0},{2,1},{3,2},{4,3},{5,4},{6,5},{7,6},{8,7},{9,8},{10,9},{11,1... | collective-permute-start | bytes 5898248 | tf_op jit(solution)/shard_map/ppermute | solution.py:19
  37.9 112.6 %collective-permute-start = (f32[15,128,256]{2,1,0:T(8,128)}, f32[15,128,256]{2,1,0:T(8,128)}, u32[]{:S(2)}, u32[]{:S(2)}) collective-permute-start(f32[15,128,256]{2,1,0:T(8,128)} %get-tuple-element.23), channel_id=1, source_target_pairs={{0,1},{1,2},{2,3},{3,4},{4,5},{5,6},{6,7},{7,8},{8,9},{9,10},{10,1... | collective-permute-start | bytes 5898248 | tf_op jit(solution)/shard_map/ppermute | solution.py:17
  196.1 4.4 copy-start
  200.5 49.0 %collective-permute-start.3 = (f32[2,15,128,256]{3,2,1,0:T(8,128)}, f32[2,15,128,256]{3,2,1,0:T(8,128)}, u32[]{:S(2)}, u32[]{:S(2)}) collective-permute-start(f32[2,15,128,256]{3,2,1,0:T(8,128)} %get-tuple-element.14), channel_id=1, source_target_pairs={{1,0},{2,1},{3,2},{4,3},{5,4},{6,5},{7,6},{8,7},{9,8},{10,9},{11,1... | collective-permute-start | bytes 11796488 | tf_op jit(solution)/shard_map/ppermute | solution.py:19
  206.1 50.0 %collective-permute-start.2 = (f32[2,15,128,256]{3,2,1,0:T(8,128)}, f32[2,15,128,256]{3,2,1,0:T(8,128)}, u32[]{:S(2)}, u32[]{:S(2)}) collective-permute-start(f32[2,15,128,256]{3,2,1,0:T(8,128)} %get-tuple-element.13), channel_id=1, source_target_pairs={{0,1},{1,2},{2,3},{3,4},{4,5},{5,6},{6,7},{7,8},{8,9},{9,10},{10,1... | collective-permute-start | bytes 11796488 | tf_op jit(solution)/shard_map/ppermute | solution.py:17
  261.8 18.9 %copy-start.8 = (s32[8]{0:T(128)S(1)}, s32[8]{0:T(128)}, u32[]{:S(2)}) copy-start(s32[8]{0:T(128)} %param.13) | copy-start | bytes 100
  273.8 1.3 copy-start.4
  276.5 22.1 %collective-permute-start.6 = (f32[4,128,256]{2,0,1:T(4,128)}, f32[4,128,256]{2,0,1:T(4,128)}, u32[]{:S(2)}, u32[]{:S(2)}) collective-permute-start(f32[4,128,256]{2,0,1:T(4,128)} %get-tuple-element.21), channel_id=1, source_target_pairs={{0,96},{32,0},{64,32},{96,64},{1,97},{33,1},{65,33},{97,65},{2,98}... | collective-permute-start | bytes 1572872 | tf_op jit(solution)/shard_map/ppermute | solution.py:37
  279.1 19.5 %collective-permute-start.5 = (f32[4,128,256]{2,0,1:T(4,128)}, f32[4,128,256]{2,0,1:T(4,128)}, u32[]{:S(2)}, u32[]{:S(2)}) collective-permute-start(f32[4,128,256]{2,0,1:T(4,128)} %get-tuple-element.22), channel_id=1, source_target_pairs={{0,64},{32,96},{64,0},{96,32},{1,65},{33,97},{65,1},{97,33},{2,66}... | collective-permute-start | bytes 1572872 | tf_op jit(solution)/shard_map/ppermute | solution.py:37
  280.2 22.1 %collective-permute-start.4 = (f32[4,128,256]{2,0,1:T(4,128)S(1)}, f32[4,128,256]{2,0,1:T(4,128)}, u32[]{:S(2)}, u32[]{:S(2)}) collective-permute-start(f32[4,128,256]{2,0,1:T(4,128)S(1)} %get-tuple-element.20), channel_id=1, source_target_pairs={{0,32},{32,64},{64,96},{96,0},{1,33},{33,65},{65,97},{97,1},{2,34}... | collective-permute-start | bytes 1572872 | tf_op jit(solution)/shard_map/ppermute | solution.py:37
  305.2 26.6 %collective-permute-start.7 = (f32[4,128,256]{2,0,1:T(4,128)}, f32[4,128,256]{2,0,1:T(4,128)}, u32[]{:S(2)}, u32[]{:S(2)}) collective-permute-start(f32[4,128,256]{2,0,1:T(4,128)} %get-tuple-element.10), channel_id=1, source_target_pairs={{0,32},{32,64},{64,96},{96,0},{1,33},{33,65},{65,97},{97,1},{2,34}... | collective-permute-start | bytes 1572872 | tf_op jit(solution)/shard_map/ppermute | solution.py:43
  305.2 27.8 %collective-permute-start.8 = (f32[4,128,256]{2,0,1:T(4,128)}, f32[4,128,256]{2,0,1:T(4,128)}, u32[]{:S(2)}, u32[]{:S(2)}) collective-permute-start(f32[4,128,256]{2,0,1:T(4,128)} %get-tuple-element.10), channel_id=1, source_target_pairs={{0,64},{32,96},{64,0},{96,32},{1,65},{33,97},{65,1},{97,33},{2,66}... | collective-permute-start | bytes 1572872 | tf_op jit(solution)/shard_map/ppermute | solution.py:43
  307.3 26.8 %collective-permute-start.9 = (f32[4,128,256]{2,0,1:T(4,128)}, f32[4,128,256]{2,0,1:T(4,128)S(1)}, u32[]{:S(2)}, u32[]{:S(2)}) collective-permute-start(f32[4,128,256]{2,0,1:T(4,128)} %get-tuple-element.10), channel_id=1, source_target_pairs={{0,96},{32,0},{64,32},{96,64},{1,97},{33,1},{65,33},{97,65},{2,98}... | collective-permute-start | bytes 1572872 | tf_op jit(solution)/shard_map/ppermute | solution.py:43
  336.1 25.9 %collective-permute-start.11 = (f32[15,128,256]{2,1,0:T(8,128)S(1)}, f32[15,128,256]{2,1,0:T(8,128)S(1)}, u32[]{:S(2)}, u32[]{:S(2)}) collective-permute-start(f32[15,128,256]{2,1,0:T(8,128)S(1)} %copy.109), channel_id=1, source_target_pairs={{1,0},{2,1},{3,2},{4,3},{5,4},{6,5},{7,6},{8,7},{9,8},{10,9},{11,1... | collective-permute-start | bytes 5898248 | tf_op jit(solution)/shard_map/ppermute | solution.py:19
  341.4 28.1 %collective-permute-start.10 = (f32[15,128,256]{2,1,0:T(8,128)S(1)}, f32[15,128,256]{2,1,0:T(8,128)S(1)}, u32[]{:S(2)}, u32[]{:S(2)}) collective-permute-start(f32[15,128,256]{2,1,0:T(8,128)S(1)} %copy.108), channel_id=1, source_target_pairs={{0,1},{1,2},{2,3},{3,4},{4,5},{5,6},{6,7},{7,8},{8,9},{9,10},{10,1... | collective-permute-start | bytes 5898248 | tf_op jit(solution)/shard_map/ppermute | solution.py:17
  381.7 3.7 copy-start.1
  394.7 45.1 %collective-permute-start.13 = (f32[2,15,128,256]{3,2,1,0:T(8,128)S(1)}, f32[2,15,128,256]{3,2,1,0:T(8,128)S(1)}, u32[]{:S(2)}, u32[]{:S(2)}) collective-permute-start(f32[2,15,128,256]{3,2,1,0:T(8,128)S(1)} %get-tuple-element.12), channel_id=1, source_target_pairs={{1,0},{2,1},{3,2},{4,3},{5,4},{6,5},{7,6},{8,7},{9,8},{10,9},{11,1... | collective-permute-start | bytes 11796488 | tf_op jit(solution)/shard_map/ppermute | solution.py:19
  396.6 49.1 %collective-permute-start.12 = (f32[2,15,128,256]{3,2,1,0:T(8,128)S(1)}, f32[2,15,128,256]{3,2,1,0:T(8,128)S(1)}, u32[]{:S(2)}, u32[]{:S(2)}) collective-permute-start(f32[2,15,128,256]{3,2,1,0:T(8,128)S(1)} %get-tuple-element.11), channel_id=1, source_target_pairs={{0,1},{1,2},{2,3},{3,4},{4,5},{5,6},{6,7},{7,8},{8,9},{9,10},{10,1... | collective-permute-start | bytes 11796488 | tf_op jit(solution)/shard_map/ppermute | solution.py:17
  460.4 14.9 %collective-permute-start.16 = (f32[4,128,256]{2,0,1:T(4,128)S(1)}, f32[4,128,256]{2,0,1:T(4,128)S(1)}, u32[]{:S(2)}, u32[]{:S(2)}) collective-permute-start(f32[4,128,256]{2,0,1:T(4,128)S(1)} %get-tuple-element.16), channel_id=1, source_target_pairs={{0,96},{32,0},{64,32},{96,64},{1,97},{33,1},{65,33},{97,65},{2,98}... | collective-permute-start | bytes 1572872 | tf_op jit(solution)/shard_map/ppermute | solution.py:37
  462.1 16.3 %collective-permute-start.15 = (f32[4,128,256]{2,0,1:T(4,128)S(1)}, f32[4,128,256]{2,0,1:T(4,128)S(1)}, u32[]{:S(2)}, u32[]{:S(2)}) collective-permute-start(f32[4,128,256]{2,0,1:T(4,128)S(1)} %get-tuple-element.17), channel_id=1, source_target_pairs={{0,64},{32,96},{64,0},{96,32},{1,65},{33,97},{65,1},{97,33},{2,66}... | collective-permute-start | bytes 1572872 | tf_op jit(solution)/shard_map/ppermute | solution.py:37
  462.1 21.9 %collective-permute-start.14 = (f32[4,128,256]{2,0,1:T(4,128)S(1)}, f32[4,128,256]{2,0,1:T(4,128)S(1)}, u32[]{:S(2)}, u32[]{:S(2)}) collective-permute-start(f32[4,128,256]{2,0,1:T(4,128)S(1)} %get-tuple-element.15), channel_id=1, source_target_pairs={{0,32},{32,64},{64,96},{96,0},{1,33},{33,65},{65,97},{97,1},{2,34}... | collective-permute-start | bytes 1572872 | tf_op jit(solution)/shard_map/ppermute | solution.py:37
  484.6 26.1 %collective-permute-start.17 = (f32[4,128,256]{2,0,1:T(4,128)S(1)}, f32[4,128,256]{2,0,1:T(4,128)S(1)}, u32[]{:S(2)}, u32[]{:S(2)}) collective-permute-start(f32[4,128,256]{2,0,1:T(4,128)S(1)} %get-tuple-element.8), channel_id=1, source_target_pairs={{0,32},{32,64},{64,96},{96,0},{1,33},{33,65},{65,97},{97,1},{2,34}... | collective-permute-start | bytes 1572872 | tf_op jit(solution)/shard_map/ppermute | solution.py:43
  484.7 26.1 %collective-permute-start.18 = (f32[4,128,256]{2,0,1:T(4,128)S(1)}, f32[4,128,256]{2,0,1:T(4,128)S(1)}, u32[]{:S(2)}, u32[]{:S(2)}) collective-permute-start(f32[4,128,256]{2,0,1:T(4,128)S(1)} %get-tuple-element.8), channel_id=1, source_target_pairs={{0,64},{32,96},{64,0},{96,32},{1,65},{33,97},{65,1},{97,33},{2,66}... | collective-permute-start | bytes 1572872 | tf_op jit(solution)/shard_map/ppermute | solution.py:43
  487.0 24.3 %collective-permute-start.19 = (f32[4,128,256]{2,0,1:T(4,128)S(1)}, f32[4,128,256]{2,0,1:T(4,128)S(1)}, u32[]{:S(2)}, u32[]{:S(2)}) collective-permute-start(f32[4,128,256]{2,0,1:T(4,128)S(1)} %get-tuple-element.8), channel_id=1, source_target_pairs={{0,96},{32,0},{64,32},{96,64},{1,97},{33,1},{65,33},{97,65},{2,98}... | collective-permute-start | bytes 1572872 | tf_op jit(solution)/shard_map/ppermute | solution.py:43

commit v2 on v1

--- a/solution.py
+++ b/solution.py
@@ -132,20 +132,41 @@
     mat_y = banded_blur_matrix(point_spread_kernels[:, 1], ny_cells, ny_cells, reach, 1)
     mat_z = banded_blur_matrix(point_spread_kernels[:, 2], nz_cells, nz_cells, reach, 1)
     weights = view_weight[:, None, None, None]
-    current = estimate
-    for iteration in range(ITERS):
-        padded = with_halo(current, (("block", 0),), reach)
+    chunk_count = 4
+    rows = ny_cells // chunk_count
+
+    def forward_chunk(cells):
+        padded = with_halo(cells, (("block", 0),), reach)
         along_x = jnp.einsum("wyz,vwx->vxyz", padded, fwd_x, precision=highest)
-        lateral_y_pass = jnp.einsum("vxyz,vyq->vxqz", along_x, mat_y, precision=highest)
-        blurred = jnp.einsum("vxyz,vzq->vxyq", lateral_y_pass, mat_z, precision=highest)
-        ratios = live_cells * (obs_views / blurred) + (1.0 - live_cells)
-        back_z = jnp.einsum("vxyz,vqz->vxyq", ratios, mat_z, precision=highest)
-        back_y = jnp.einsum("vxyz,vqy->vxqz", back_z, mat_y, precision=highest)
-        rimmed = with_halo(back_y, (("block", 1),), reach)
+        return jnp.einsum("vxyz,vzq->vxyq", along_x, mat_z, precision=highest)
+
+    def backward_chunk(back_y, cells, chunk):
+        back_z = jnp.einsum("vxyz,vqz->vxyq", back_y, mat_z, precision=highest)
+        rimmed = with_halo(back_z, (("block", 1),), reach)
         corrected = jnp.einsum("vwyz,vwx->vxyz", rimmed, adj_x, precision=highest)
         partial_logarithm = jnp.sum(live_cells * weights * jnp.log(corrected), axis=0)
-        current = view_sum_update(partial_logarithm, current, counts)
-    return current
+        return view_sum_update(partial_logarithm, cells, counts)
+
+    pieces = [
+        lax.slice_in_dim(estimate, c * rows, (c + 1) * rows, axis=1) for c in range(chunk_count)
+    ]
+    forward = [forward_chunk(cells) for cells in pieces]
+    for iteration in range(ITERS):
+        along_xz = jnp.concatenate(forward, axis=2)
+        blurred = jnp.einsum("vxyz,vyq->vxqz", along_xz, mat_y, precision=highest)
+        ratios = live_cells * (obs_views / blurred) + (1.0 - live_cells)
+        back_y = jnp.einsum("vxyz,vqy->vxqz", ratios, mat_y, precision=highest)
+        updated = []
+        forward = []
+        for c in range(chunk_count):
+            cells = backward_chunk(
+                lax.slice_in_dim(back_y, c * rows, (c + 1) * rows, axis=2), pieces[c], c
+            )
+            updated.append(cells)
+            if iteration + 1 < ITERS:
+                forward.append(forward_chunk(cells))
+        pieces = updated
+    return jnp.concatenate(pieces, axis=1)
 
 
 def solution(mesh):

time: 518 us -> 450 us (0.87)
  waiting for transfers between devices: 310 us -> 80.6 us
  starting transfers between devices: 53.6 us -> 212 us
  matrix products: 76.7 us -> 84.8 us
  other arithmetic: 15 us -> 7.81 us
    ppermute x4 -> x16, waiting for transfers between devices: 203 us -> 6.59 us  [with_halo(): lax.ppermute(head, axis, [((i + 1) % count, i) for i in range(ends)])]
    ppermute x4 -> x16, starting transfers between devices: 16.1 us -> 93.7 us  [with_halo(): lax.ppermute(head, axis, [((i + 1) % count, i) for i in range(ends)])]
    ppermute x4 -> x16, waiting for transfers between devices: 18.7 us -> 57.2 us  [with_halo(): lax.ppermute(tail, axis, [(i, (i + 1) % count) for i in range(ends)])]
    ppermute x6 -> x24, waiting for transfers between devices: 42.3 us -> 6.42 us  [view_sum_update(): lax.ppermute(sent, 'view', [(i, (i + shift) % count) for i in range(count)])]
    ppermute x6 -> x24, waiting for transfers between devices: 45.9 us -> 10.4 us  [view_sum_update(): lax.ppermute(updated, 'view', [(i, (i + shift) % count) for i in range(co...]
    ppermute x6 -> x24, starting transfers between devices: 7.08 us -> 35.2 us  [view_sum_update(): lax.ppermute(updated, 'view', [(i, (i + shift) % count) for i in range(co...]
    ppermute x4 -> x16, starting transfers between devices: 8.35 us -> 35.2 us  [with_halo(): lax.ppermute(tail, axis, [(i, (i + 1) % count) for i in range(ends)])]
    ppermute x6 -> x24, starting transfers between devices: 6.72 us -> 32.5 us  [view_sum_update(): lax.ppermute(sent, 'view', [(i, (i + shift) % count) for i in range(count)])]
  transfers between devices with their start and end apart: 22 -> 82, of which waited for: 15 -> 20; matrix products, arithmetic and copies ran while one was open for 9% -> 23% of each run, Pallas kernels for 0% -> 0%
where the time goes in v2:
time: 450 us; the launch traced here: 441 us
  starting transfers between devices  212 us (47%)
  matrix products  84.8 us (19%)
  waiting for transfers between devices  80.6 us (18%)
  local copies, waits for them, and re-layouts  54 us (12%)
  other arithmetic  7.81 us (2%)
    ppermute x16, starting transfers between devices, with_halo(): lax.ppermute(head, axis, [((i + 1) % count, i) for i in range(ends)])  93.7 us
    ppermute x16, waiting for transfers between devices, with_halo(): lax.ppermute(tail, axis, [(i, (i + 1) % count) for i in range(ends)])  57.2 us
    ppermute x24, starting transfers between devices, view_sum_update(): lax.ppermute(updated, 'view', [(i, (i + shift) % count) for i in range(co...  35.2 us
    ppermute x16, starting transfers between devices, with_halo(): lax.ppermute(tail, axis, [(i, (i + 1) % count) for i in range(ends)])  35.2 us
    ppermute x24, starting transfers between devices, view_sum_update(): lax.ppermute(sent, 'view', [(i, (i + shift) % count) for i in range(count)])  32.5 us
    dot_general x8, matrix products, backward_chunk(): corrected = jnp.einsum('vwyz,vwx->vxyz', rimmed, adj_x, precision=highest)  26.4 us
    unnamed x26, local copies, waits for them, and re-layouts  15.2 us
    scatter x1, local copies, waits for them, and re-layouts, on_device(): placed = jnp.zeros((per_group * per_block, planes, ny_cells, nz_cells), j...  13.6 us
  transfers between devices with their start and end apart: 82, of which 20 were waited for; matrix products, arithmetic and copies ran while one was open for 23% of the time, Pallas kernels for 0%

profile of v2, /device:TPU:64, one launch (start us, length us, event | category | flops | bytes accessed | tf_op | source)
XLA Modules:
  0.0 441.3 jit_solution(12225013723534158116)
XLA Ops:
  3.6 7.6 %all-to-all-start = ((f32[32,1,1]{2,1,0:T(1,128)}), f32[32,1,1]{2,1,0:T(1,128)S(1)}, u32[]{:S(2)}, u32[]{:S(2)}) async-start(f32[32,1,1]{2,1,0:T(1,128)} %copy.194), calls=%async_computation | async-start | bytes 32768 | tf_op jit(solution)/shard_map/all_to_all | solution.py:107
  11.2 4.3 broadcast_in_dim.37
  15.5 7.7 %scatter_fusion = f32[32,2,128,256]{3,2,1,0:T(8,128)} fusion(f32[32,2,128,256]{3,2,1,0:T(8,128)} %broadcast_in_dim.37, s32[16]{0:T(128)S(1)} %fusion.241, f32[16,2,128,256]{3,2,1,0:T(8,128)} %bitcast.146), kind=kCustom, calls=%fused_computation.1 | custom fusion | bytes 12582976 | tf_op jit(solution)/shard_map/scatter | solution.py:92
  23.2 7.9 %all-to-all-start.1 = ((f32[32,1,2,128,256]{4,3,2,1,0:T(8,128)}), f32[32,1,2,128,256]{4,3,2,1,0:T(8,128)}, u32[]{:S(2)}, u32[]{:S(2)}) async-start(f32[32,1,2,128,256]{4,3,2,1,0:T(8,128)} %bitcast.143), calls=%async_computation.1 | async-start | bytes 16777216 | tf_op jit(solution)/shard_map/all_to_all | solution.py:100
  33.6 2.1 collective-permute-start.4
  36.8 5.6 %collective-permute-start.5 = (f32[15,32,256]{2,0,1:T(8,128)}, f32[15,32,256]{2,0,1:T(8,128)}, u32[]{:S(2)}, u32[]{:S(2)}) collective-permute-start(f32[15,32,256]{2,0,1:T(8,128)} %copy.375), channel_id=1, source_target_pairs={{1,0},{2,1},{3,2},{4,3},{5,4},{6,5},{7,6},{8,7},{9,8},{10,9},{11,1... | collective-permute-start | bytes 1474568 | tf_op jit(solution)/shard_map/ppermute | solution.py:19
  46.6 5.7 %collective-permute-start.3 = (f32[15,32,256]{2,0,1:T(8,128)}, f32[15,32,256]{2,0,1:T(8,128)}, u32[]{:S(2)}, u32[]{:S(2)}) collective-permute-start(f32[15,32,256]{2,0,1:T(8,128)} %copy.372), channel_id=1, source_target_pairs={{1,0},{2,1},{3,2},{4,3},{5,4},{6,5},{7,6},{8,7},{9,8},{10,9},{11,1... | collective-permute-start | bytes 1474568 | tf_op jit(solution)/shard_map/ppermute | solution.py:19
  63.3 2.1 copy.369
  65.7 2.1 copy.376
  67.8 2.1 copy.378
  71.3 57.1 %collective-permute-done.4 = f32[15,32,256]{2,0,1:T(8,128)} collective-permute-done((f32[15,32,256]{2,0,1:T(8,128)}, f32[15,32,256]{2,0,1:T(8,128)}, u32[]{:S(2)}, u32[]{:S(2)}) %collective-permute-start.4) | collective-permute-done | bytes 491552 | tf_op jit(solution)/shard_map/ppermute | solution.py:17
  130.3 2.2 collective-permute-done.5
  132.5 5.8 %collective-permute-start.6 = (f32[15,32,256]{2,0,1:T(8,128)}, f32[15,32,256]{2,0,1:T(8,128)S(1)}, u32[]{:S(2)}, u32[]{:S(2)}) collective-permute-start(f32[15,32,256]{2,0,1:T(8,128)} %copy.376), channel_id=1, source_target_pairs={{0,1},{1,2},{2,3},{3,4},{4,5},{5,6},{6,7},{7,8},{8,9},{9,10},{10,1... | collective-permute-start | bytes 1474568 | tf_op jit(solution)/shard_map/ppermute | solution.py:17
  138.4 2.3 fusion.65
  140.7 10.9 %collective-permute-start.7 = (f32[15,32,256]{2,0,1:T(8,128)}, f32[15,32,256]{2,0,1:T(8,128)S(1)}, u32[]{:S(2)}, u32[]{:S(2)}) collective-permute-start(f32[15,32,256]{2,0,1:T(8,128)} %copy.378), channel_id=1, source_target_pairs={{1,0},{2,1},{3,2},{4,3},{5,4},{6,5},{7,6},{8,7},{9,8},{10,9},{11,1... | collective-permute-start | bytes 1474568 | tf_op jit(solution)/shard_map/ppermute | solution.py:19
  151.6 2.3 fusion.60
  154.0 2.2 fusion.55
  156.2 2.4 collective-permute-done.7
  166.5 5.3 %fusion.1 = f32[2,128,16,256]{3,1,2,0:T(8,128)} fusion(f32[2,128,128,1]{1,2,3,0:T(8,128)S(1)} %copy.267, f32[2,16,32,256]{3,2,1,0:T(8,128)S(1)} %fusion.193, f32[2,16,32,256]{3,2,1,0:T(8,128)S(1)} %fusion.195, f32[2,16,32,256]{3,2,1,0:T(8,128)S(1)} %fusion.197, f32[2,16,32,256]{3,2,1,0:T(8,128)S(1)} %fusion.199), kind=kOutput, calls=%fused_computation.5 | convolution fusion | flops 1613758464 | bytes 8519680 | tf_op jit(solution)/shard_map/vxyz,vyq->vxqz/dot_general | solution.py:156
  171.8 2.6 broadcast_in_dim.33
  174.3 13.6 %scatter_fusion.1 = f32[16,2,128,256]{3,2,1,0:T(8,128)} fusion(f32[16,2,128,256]{3,2,1,0:T(8,128)} %broadcast_in_dim.33, s32[32]{0:T(128)S(1)} %fusion.239, f32[32,2,128,256]{3,2,1,0:T(8,128)} %bitcast.15), kind=kCustom, calls=%fused_computation.2 | custom fusion | bytes 25165952 | tf_op jit(solution)/shard_map/scatter | solution.py:116
  187.9 6.7 %fusion.44 = f32[2,16,128,256]{3,2,1,0:T(8,128)S(1)} fusion(f32[2,128,16,256]{3,1,2,0:T(8,128)} %fusion.1, f32[2,16]{1,0:T(2,128)S(1)} %get-tuple-element.84, f32[2,16]{1,0:T(2,128)S(1)} %broadcast_in_dim_reshape.6, f32[2,128,128,1]{2,0,1,3:T(2,128)S(1)} %fusion.168, f32[2,16,128,256]{3,2,1,0:T(8,128)} %bitcast.144), kind=kOutput, calls=%fused_computation.56 | convolution fusion | flops 1613758464 | bytes 12714240 | tf_op jit(solution)/shard_map/vxyz,vqy->vxqz/dot_general | solution.py:158
  199.0 5.8 %collective-permute-start.39 = (f32[2,15,32,256]{3,2,1,0:T(8,128)S(1)}, f32[2,15,32,256]{3,2,1,0:T(8,128)S(1)}, u32[]{:S(2)}, u32[]{:S(2)}) collective-permute-start(f32[2,15,32,256]{3,2,1,0:T(8,128)S(1)} %get-tuple-element.50), channel_id=1, source_target_pairs={{1,0},{2,1},{3,2},{4,3},{5,4},{6,5},{7,6},{8,7},{9,8},{10,9},{11,1... | collective-permute-start | bytes 2949128 | tf_op jit(solution)/shard_map/ppermute | solution.py:19
  208.1 5.8 %collective-permute-start.19 = (f32[2,15,32,256]{3,2,1,0:T(8,128)S(1)}, f32[2,15,32,256]{3,2,1,0:T(8,128)S(1)}, u32[]{:S(2)}, u32[]{:S(2)}) collective-permute-start(f32[2,15,32,256]{3,2,1,0:T(8,128)S(1)} %get-tuple-element.46), channel_id=1, source_target_pairs={{1,0},{2,1},{3,2},{4,3},{5,4},{6,5},{7,6},{8,7},{9,8},{10,9},{11,1... | collective-permute-start | bytes 2949128 | tf_op jit(solution)/shard_map/ppermute | solution.py:19
  217.4 5.8 %collective-permute-start.9 = (f32[2,15,32,256]{3,2,1,0:T(8,128)S(1)}, f32[2,15,32,256]{3,2,1,0:T(8,128)S(1)}, u32[]{:S(2)}, u32[]{:S(2)}) collective-permute-start(f32[2,15,32,256]{3,2,1,0:T(8,128)S(1)} %get-tuple-element.44), channel_id=1, source_target_pairs={{1,0},{2,1},{3,2},{4,3},{5,4},{6,5},{7,6},{8,7},{9,8},{10,9},{11,1... | collective-permute-start | bytes 2949128 | tf_op jit(solution)/shard_map/ppermute | solution.py:19
  223.1 2.1 collective-permute-start.28
  225.7 3.3 fusion.155
  229.0 5.8 %collective-permute-start.29 = (f32[2,15,32,256]{3,2,1,0:T(8,128)S(1)}, f32[2,15,32,256]{3,2,1,0:T(8,128)S(1)}, u32[]{:S(2)}, u32[]{:S(2)}) collective-permute-start(f32[2,15,32,256]{3,2,1,0:T(8,128)S(1)} %get-tuple-element.48), channel_id=1, source_target_pairs={{1,0},{2,1},{3,2},{4,3},{5,4},{6,5},{7,6},{8,7},{9,8},{10,9},{11,1... | collective-permute-start | bytes 2949128 | tf_op jit(solution)/shard_map/ppermute | solution.py:19
  236.9 3.3 fusion.161
  240.3 3.0 collective-permute-start.41
  245.5 3.3 fusion.164
  255.7 2.1 collective-permute-done.20
  258.3 3.3 fusion.158
  263.4 2.8 collective-permute-start.32
  266.6 2.8 collective-permute-start.14
  272.3 2.3 collective-permute-start.24
  274.9 2.6 collective-permute-start.25
  278.0 2.3 collective-permute-start.34
  280.6 2.4 collective-permute-start.35
  286.2 3.0 collective-permute-start.45
  291.2 5.8 %collective-permute-start.17 = (f32[15,32,256]{2,0,1:T(8,128)S(1)}, f32[15,32,256]{2,0,1:T(8,128)S(1)}, u32[]{:S(2)}, u32[]{:S(2)}) collective-permute-start(f32[15,32,256]{2,0,1:T(8,128)S(1)} %get-tuple-element.64), channel_id=1, source_target_pairs={{1,0},{2,1},{3,2},{4,3},{5,4},{6,5},{7,6},{8,7},{9,8},{10,9},{11,1... | collective-permute-start | bytes 1474568 | tf_op jit(solution)/shard_map/ppermute | solution.py:19
  299.1 5.8 %collective-permute-start.27 = (f32[15,32,256]{2,0,1:T(8,128)S(1)}, f32[15,32,256]{2,0,1:T(8,128)S(1)}, u32[]{:S(2)}, u32[]{:S(2)}) collective-permute-start(f32[15,32,256]{2,0,1:T(8,128)S(1)} %get-tuple-element.69), channel_id=1, source_target_pairs={{1,0},{2,1},{3,2},{4,3},{5,4},{6,5},{7,6},{8,7},{9,8},{10,9},{11,1... | collective-permute-start | bytes 1474568 | tf_op jit(solution)/shard_map/ppermute | solution.py:19
  307.0 5.8 %collective-permute-start.37 = (f32[15,32,256]{2,0,1:T(8,128)S(1)}, f32[15,32,256]{2,0,1:T(8,128)S(1)}, u32[]{:S(2)}, u32[]{:S(2)}) collective-permute-start(f32[15,32,256]{2,0,1:T(8,128)S(1)} %get-tuple-element.74), channel_id=1, source_target_pairs={{1,0},{2,1},{3,2},{4,3},{5,4},{6,5},{7,6},{8,7},{9,8},{10,9},{11,1... | collective-permute-start | bytes 1474568 | tf_op jit(solution)/shard_map/ppermute | solution.py:19
  317.6 6.0 %collective-permute-start.47 = (f32[15,32,256]{2,0,1:T(8,128)S(1)}, f32[15,32,256]{2,0,1:T(8,128)S(1)}, u32[]{:S(2)}, u32[]{:S(2)}) collective-permute-start(f32[15,32,256]{2,0,1:T(8,128)S(1)} %get-tuple-element.79), channel_id=1, source_target_pairs={{1,0},{2,1},{3,2},{4,3},{5,4},{6,5},{7,6},{8,7},{9,8},{10,9},{11,1... | collective-permute-start | bytes 1474568 | tf_op jit(solution)/shard_map/ppermute | solution.py:19
  332.8 4.2 fusion.9
  337.0 4.3 fusion.47
  345.7 5.9 %collective-permute-start.65 = (f32[2,15,32,256]{3,2,1,0:T(8,128)S(1)}, f32[2,15,32,256]{3,2,1,0:T(8,128)S(1)}, u32[]{:S(2)}, u32[]{:S(2)}) collective-permute-start(f32[2,15,32,256]{3,2,1,0:T(8,128)S(1)} %get-tuple-element.40), channel_id=1, source_target_pairs={{1,0},{2,1},{3,2},{4,3},{5,4},{6,5},{7,6},{8,7},{9,8},{10,9},{11,1... | collective-permute-start | bytes 2949128 | tf_op jit(solution)/shard_map/ppermute | solution.py:19
  354.9 5.8 %collective-permute-start.73 = (f32[2,15,32,256]{3,2,1,0:T(8,128)S(1)}, f32[2,15,32,256]{3,2,1,0:T(8,128)S(1)}, u32[]{:S(2)}, u32[]{:S(2)}) collective-permute-start(f32[2,15,32,256]{3,2,1,0:T(8,128)S(1)} %get-tuple-element.42), channel_id=1, source_target_pairs={{1,0},{2,1},{3,2},{4,3},{5,4},{6,5},{7,6},{8,7},{9,8},{10,9},{11,1... | collective-permute-start | bytes 2949128 | tf_op jit(solution)/shard_map/ppermute | solution.py:19
  364.2 5.8 %collective-permute-start.49 = (f32[2,15,32,256]{3,2,1,0:T(8,128)S(1)}, f32[2,15,32,256]{3,2,1,0:T(8,128)S(1)}, u32[]{:S(2)}, u32[]{:S(2)}) collective-permute-start(f32[2,15,32,256]{3,2,1,0:T(8,128)S(1)} %get-tuple-element.36), channel_id=1, source_target_pairs={{1,0},{2,1},{3,2},{4,3},{5,4},{6,5},{7,6},{8,7},{9,8},{10,9},{11,1... | collective-permute-start | bytes 2949128 | tf_op jit(solution)/shard_map/ppermute | solution.py:19
  369.9 2.1 collective-permute-start.56
  372.4 3.3 fusion.146
  375.7 5.8 %collective-permute-start.57 = (f32[2,15,32,256]{3,2,1,0:T(8,128)S(1)}, f32[2,15,32,256]{3,2,1,0:T(8,128)S(1)}, u32[]{:S(2)}, u32[]{:S(2)}) collective-permute-start(f32[2,15,32,256]{3,2,1,0:T(8,128)S(1)} %get-tuple-element.38), channel_id=1, source_target_pairs={{1,0},{2,1},{3,2},{4,3},{5,4},{6,5},{7,6},{8,7},{9,8},{10,9},{11,1... | collective-permute-start | bytes 2949128 | tf_op jit(solution)/shard_map/ppermute | solution.py:19
  382.1 3.3 fusion.143
  387.1 2.3 collective-permute-start.68
  389.8 3.3 fusion.152
  396.4 2.6 collective-permute-start.76
  400.9 2.4 collective-permute-done.74
  403.4 3.3 fusion.149
  406.8 2.1 collective-permute-start.58
  409.0 2.6 collective-permute-start.60
  412.2 2.8 collective-permute-start.54
  419.6 3.1 collective-permute-start.62
  434.3 2.8 collective-permute-done.77
  438.3 2.5 copy.258
  (250 shorter events, 123.3 us)
Async XLA Ops:
  3.6 19.6 %all-to-all-start = ((f32[32,1,1]{2,1,0:T(1,128)}), f32[32,1,1]{2,1,0:T(1,128)S(1)}, u32[]{:S(2)}, u32[]{:S(2)}) async-start(f32[32,1,1]{2,1,0:T(1,128)} %copy.194), calls=%async_computation | async-start | bytes 32768 | tf_op jit(solution)/shard_map/all_to_all | solution.py:107
  23.2 148.6 %all-to-all-start.1 = ((f32[32,1,2,128,256]{4,3,2,1,0:T(8,128)}), f32[32,1,2,128,256]{4,3,2,1,0:T(8,128)}, u32[]{:S(2)}, u32[]{:S(2)}) async-start(f32[32,1,2,128,256]{4,3,2,1,0:T(8,128)} %bitcast.143), calls=%async_computation.1 | async-start | bytes 16777216 | tf_op jit(solution)/shard_map/all_to_all | solution.py:100
  33.6 94.8 %collective-permute-start.4 = (f32[15,32,256]{2,0,1:T(8,128)}, f32[15,32,256]{2,0,1:T(8,128)}, u32[]{:S(2)}, u32[]{:S(2)}) collective-permute-start(f32[15,32,256]{2,0,1:T(8,128)} %copy.373), channel_id=1, source_target_pairs={{0,1},{1,2},{2,3},{3,4},{4,5},{5,6},{6,7},{7,8},{8,9},{9,10},{10,1... | collective-permute-start | bytes 1474568 | tf_op jit(solution)/shard_map/ppermute | solution.py:17
  36.8 95.7 %collective-permute-start.5 = (f32[15,32,256]{2,0,1:T(8,128)}, f32[15,32,256]{2,0,1:T(8,128)}, u32[]{:S(2)}, u32[]{:S(2)}) collective-permute-start(f32[15,32,256]{2,0,1:T(8,128)} %copy.375), channel_id=1, source_target_pairs={{1,0},{2,1},{3,2},{4,3},{5,4},{6,5},{7,6},{8,7},{9,8},{10,9},{11,1... | collective-permute-start | bytes 1474568 | tf_op jit(solution)/shard_map/ppermute | solution.py:19
  43.6 97.2 %collective-permute-start.2 = (f32[15,32,256]{2,0,1:T(8,128)}, f32[15,32,256]{2,0,1:T(8,128)}, u32[]{:S(2)}, u32[]{:S(2)}) collective-permute-start(f32[15,32,256]{2,0,1:T(8,128)} %copy.370), channel_id=1, source_target_pairs={{0,1},{1,2},{2,3},{3,4},{4,5},{5,6},{6,7},{7,8},{8,9},{9,10},{10,1... | collective-permute-start | bytes 1474568 | tf_op jit(solution)/shard_map/ppermute | solution.py:17
  46.6 105.0 %collective-permute-start.3 = (f32[15,32,256]{2,0,1:T(8,128)}, f32[15,32,256]{2,0,1:T(8,128)}, u32[]{:S(2)}, u32[]{:S(2)}) collective-permute-start(f32[15,32,256]{2,0,1:T(8,128)} %copy.372), channel_id=1, source_target_pairs={{1,0},{2,1},{3,2},{4,3},{5,4},{6,5},{7,6},{8,7},{9,8},{10,9},{11,1... | collective-permute-start | bytes 1474568 | tf_op jit(solution)/shard_map/ppermute | solution.py:19
  53.4 100.6 %collective-permute-start = (f32[15,32,256]{2,0,1:T(8,128)}, f32[15,32,256]{2,0,1:T(8,128)}, u32[]{:S(2)}, u32[]{:S(2)}) collective-permute-start(f32[15,32,256]{2,0,1:T(8,128)} %copy.368), channel_id=1, source_target_pairs={{0,1},{1,2},{2,3},{3,4},{4,5},{5,6},{6,7},{7,8},{8,9},{9,10},{10,1... | collective-permute-start | bytes 1474568 | tf_op jit(solution)/shard_map/ppermute | solution.py:17
  128.4 25.6 %collective-permute-start.1 = (f32[15,32,256]{2,0,1:T(8,128)}, f32[15,32,256]{2,0,1:T(8,128)S(1)}, u32[]{:S(2)}, u32[]{:S(2)}) collective-permute-start(f32[15,32,256]{2,0,1:T(8,128)} %copy.369), channel_id=1, source_target_pairs={{1,0},{2,1},{3,2},{4,3},{5,4},{6,5},{7,6},{8,7},{9,8},{10,9},{11,1... | collective-permute-start | bytes 1474568 | tf_op jit(solution)/shard_map/ppermute | solution.py:19
  132.5 23.6 %collective-permute-start.6 = (f32[15,32,256]{2,0,1:T(8,128)}, f32[15,32,256]{2,0,1:T(8,128)S(1)}, u32[]{:S(2)}, u32[]{:S(2)}) collective-permute-start(f32[15,32,256]{2,0,1:T(8,128)} %copy.376), channel_id=1, source_target_pairs={{0,1},{1,2},{2,3},{3,4},{4,5},{5,6},{6,7},{7,8},{8,9},{9,10},{10,1... | collective-permute-start | bytes 1474568 | tf_op jit(solution)/shard_map/ppermute | solution.py:17
  140.7 17.9 %collective-permute-start.7 = (f32[15,32,256]{2,0,1:T(8,128)}, f32[15,32,256]{2,0,1:T(8,128)S(1)}, u32[]{:S(2)}, u32[]{:S(2)}) collective-permute-start(f32[15,32,256]{2,0,1:T(8,128)} %copy.378), channel_id=1, source_target_pairs={{1,0},{2,1},{3,2},{4,3},{5,4},{6,5},{7,6},{8,7},{9,8},{10,9},{11,1... | collective-permute-start | bytes 1474568 | tf_op jit(solution)/shard_map/ppermute | solution.py:19
  197.0 20.3 %collective-permute-start.38 = (f32[2,15,32,256]{3,2,1,0:T(8,128)S(1)}, f32[2,15,32,256]{3,2,1,0:T(8,128)S(1)}, u32[]{:S(2)}, u32[]{:S(2)}) collective-permute-start(f32[2,15,32,256]{3,2,1,0:T(8,128)S(1)} %get-tuple-element.49), channel_id=1, source_target_pairs={{0,1},{1,2},{2,3},{3,4},{4,5},{5,6},{6,7},{7,8},{8,9},{9,10},{10,1... | collective-permute-start | bytes 2949128 | tf_op jit(solution)/shard_map/ppermute | solution.py:17
  199.0 24.2 %collective-permute-start.39 = (f32[2,15,32,256]{3,2,1,0:T(8,128)S(1)}, f32[2,15,32,256]{3,2,1,0:T(8,128)S(1)}, u32[]{:S(2)}, u32[]{:S(2)}) collective-permute-start(f32[2,15,32,256]{3,2,1,0:T(8,128)S(1)} %get-tuple-element.50), channel_id=1, source_target_pairs={{1,0},{2,1},{3,2},{4,3},{5,4},{6,5},{7,6},{8,7},{9,8},{10,9},{11,1... | collective-permute-start | bytes 2949128 | tf_op jit(solution)/shard_map/ppermute | solution.py:19
  206.1 22.8 %collective-permute-start.18 = (f32[2,15,32,256]{3,2,1,0:T(8,128)S(1)}, f32[2,15,32,256]{3,2,1,0:T(8,128)S(1)}, u32[]{:S(2)}, u32[]{:S(2)}) collective-permute-start(f32[2,15,32,256]{3,2,1,0:T(8,128)S(1)} %get-tuple-element.45), channel_id=1, source_target_pairs={{0,1},{1,2},{2,3},{3,4},{4,5},{5,6},{6,7},{7,8},{8,9},{9,10},{10,1... | collective-permute-start | bytes 2949128 | tf_op jit(solution)/shard_map/ppermute | solution.py:17
  208.1 26.8 %collective-permute-start.19 = (f32[2,15,32,256]{3,2,1,0:T(8,128)S(1)}, f32[2,15,32,256]{3,2,1,0:T(8,128)S(1)}, u32[]{:S(2)}, u32[]{:S(2)}) collective-permute-start(f32[2,15,32,256]{3,2,1,0:T(8,128)S(1)} %get-tuple-element.46), channel_id=1, source_target_pairs={{1,0},{2,1},{3,2},{4,3},{5,4},{6,5},{7,6},{8,7},{9,8},{10,9},{11,1... | collective-permute-start | bytes 2949128 | tf_op jit(solution)/shard_map/ppermute | solution.py:19
  215.2 25.1 %collective-permute-start.8 = (f32[2,15,32,256]{3,2,1,0:T(8,128)S(1)}, f32[2,15,32,256]{3,2,1,0:T(8,128)S(1)}, u32[]{:S(2)}, u32[]{:S(2)}) collective-permute-start(f32[2,15,32,256]{3,2,1,0:T(8,128)S(1)} %get-tuple-element.43), channel_id=1, source_target_pairs={{0,1},{1,2},{2,3},{3,4},{4,5},{5,6},{6,7},{7,8},{8,9},{9,10},{10,1... | collective-permute-start | bytes 2949128 | tf_op jit(solution)/shard_map/ppermute | solution.py:17
  217.4 25.9 %collective-permute-start.9 = (f32[2,15,32,256]{3,2,1,0:T(8,128)S(1)}, f32[2,15,32,256]{3,2,1,0:T(8,128)S(1)}, u32[]{:S(2)}, u32[]{:S(2)}) collective-permute-start(f32[2,15,32,256]{3,2,1,0:T(8,128)S(1)} %get-tuple-element.44), channel_id=1, source_target_pairs={{1,0},{2,1},{3,2},{4,3},{5,4},{6,5},{7,6},{8,7},{9,8},{10,9},{11,1... | collective-permute-start | bytes 2949128 | tf_op jit(solution)/shard_map/ppermute | solution.py:19
  223.1 25.7 %collective-permute-start.28 = (f32[2,15,32,256]{3,2,1,0:T(8,128)S(1)}, f32[2,15,32,256]{3,2,1,0:T(8,128)S(1)}, u32[]{:S(2)}, u32[]{:S(2)}) collective-permute-start(f32[2,15,32,256]{3,2,1,0:T(8,128)S(1)} %get-tuple-element.47), channel_id=1, source_target_pairs={{0,1},{1,2},{2,3},{3,4},{4,5},{5,6},{6,7},{7,8},{8,9},{9,10},{10,1... | collective-permute-start | bytes 2949128 | tf_op jit(solution)/shard_map/ppermute | solution.py:17
  229.0 20.5 %collective-permute-start.29 = (f32[2,15,32,256]{3,2,1,0:T(8,128)S(1)}, f32[2,15,32,256]{3,2,1,0:T(8,128)S(1)}, u32[]{:S(2)}, u32[]{:S(2)}) collective-permute-start(f32[2,15,32,256]{3,2,1,0:T(8,128)S(1)} %get-tuple-element.48), channel_id=1, source_target_pairs={{1,0},{2,1},{3,2},{4,3},{5,4},{6,5},{7,6},{8,7},{9,8},{10,9},{11,1... | collective-permute-start | bytes 2949128 | tf_op jit(solution)/shard_map/ppermute | solution.py:19
  234.9 16.9 %collective-permute-start.40 = (f32[4,32,256]{2,0,1:T(4,128)S(1)}, f32[4,32,256]{2,0,1:T(4,128)S(1)}, u32[]{:S(2)}, u32[]{:S(2)}) collective-permute-start(f32[4,32,256]{2,0,1:T(4,128)S(1)} %get-tuple-element.80), channel_id=1, source_target_pairs={{0,32},{32,64},{64,96},{96,0},{1,33},{33,65},{65,97},{97,1},{2,34}... | collective-permute-start | bytes 393224 | tf_op jit(solution)/shard_map/ppermute | solution.py:37
  240.3 12.5 %collective-permute-start.41 = (f32[4,32,256]{2,0,1:T(4,128)S(1)}, f32[4,32,256]{2,0,1:T(4,128)S(1)}, u32[]{:S(2)}, u32[]{:S(2)}) collective-permute-start(f32[4,32,256]{2,0,1:T(4,128)S(1)} %get-tuple-element.82), channel_id=1, source_target_pairs={{0,64},{32,96},{64,0},{96,32},{1,65},{33,97},{65,1},{97,33},{2,66}... | collective-permute-start | bytes 393224 | tf_op jit(solution)/shard_map/ppermute | solution.py:37
  243.3 10.6 %collective-permute-start.42 = (f32[4,32,256]{2,0,1:T(4,128)S(1)}, f32[4,32,256]{2,0,1:T(4,128)S(1)}, u32[]{:S(2)}, u32[]{:S(2)}) collective-permute-start(f32[4,32,256]{2,0,1:T(4,128)S(1)} %get-tuple-element.81), channel_id=1, source_target_pairs={{0,96},{32,0},{64,32},{96,64},{1,97},{33,1},{65,33},{97,65},{2,98}... | collective-permute-start | bytes 393224 | tf_op jit(solution)/shard_map/ppermute | solution.py:37
  249.5 12.2 %collective-permute-start.21 = (f32[4,32,256]{2,0,1:T(4,128)S(1)}, f32[4,32,256]{2,0,1:T(4,128)S(1)}, u32[]{:S(2)}, u32[]{:S(2)}) collective-permute-start(f32[4,32,256]{2,0,1:T(4,128)S(1)} %get-tuple-element.72), channel_id=1, source_target_pairs={{0,64},{32,96},{64,0},{96,32},{1,65},{33,97},{65,1},{97,33},{2,66}... | collective-permute-start | bytes 393224 | tf_op jit(solution)/shard_map/ppermute | solution.py:37
  251.8 11.6 %collective-permute-start.22 = (f32[4,32,256]{2,0,1:T(4,128)S(1)}, f32[4,32,256]{2,0,1:T(4,128)S(1)}, u32[]{:S(2)}, u32[]{:S(2)}) collective-permute-start(f32[4,32,256]{2,0,1:T(4,128)S(1)} %get-tuple-element.71), channel_id=1, source_target_pairs={{0,96},{32,0},{64,32},{96,64},{1,97},{33,1},{65,33},{97,65},{2,98}... | collective-permute-start | bytes 393224 | tf_op jit(solution)/shard_map/ppermute | solution.py:37
  252.8 10.5 %collective-permute-start.10 = (f32[4,32,256]{2,0,1:T(4,128)S(1)}, f32[4,32,256]{2,0,1:T(4,128)S(1)}, u32[]{:S(2)}, u32[]{:S(2)}) collective-permute-start(f32[4,32,256]{2,0,1:T(4,128)S(1)} %get-tuple-element.65), channel_id=1, source_target_pairs={{0,32},{32,64},{64,96},{96,0},{1,33},{33,65},{65,97},{97,1},{2,34}... | collective-permute-start | bytes 393224 | tf_op jit(solution)/shard_map/ppermute | solution.py:37
  253.9 12.3 %collective-permute-start.11 = (f32[4,32,256]{2,0,1:T(4,128)S(1)}, f32[4,32,256]{2,0,1:T(4,128)S(1)}, u32[]{:S(2)}, u32[]{:S(2)}) collective-permute-start(f32[4,32,256]{2,0,1:T(4,128)S(1)} %get-tuple-element.67), channel_id=1, source_target_pairs={{0,64},{32,96},{64,0},{96,32},{1,65},{33,97},{65,1},{97,33},{2,66}... | collective-permute-start | bytes 393224 | tf_op jit(solution)/shard_map/ppermute | solution.py:37
  266.6 10.9 %collective-permute-start.14 = (f32[4,32,256]{2,0,1:T(4,128)S(1)}, f32[4,32,256]{2,0,1:T(4,128)S(1)}, u32[]{:S(2)}, u32[]{:S(2)}) collective-permute-start(f32[4,32,256]{2,0,1:T(4,128)S(1)} %get-tuple-element.16), channel_id=1, source_target_pairs={{0,64},{32,96},{64,0},{96,32},{1,65},{33,97},{65,1},{97,33},{2,66}... | collective-permute-start | bytes 393224 | tf_op jit(solution)/shard_map/ppermute | solution.py:43
  272.3 10.7 %collective-permute-start.24 = (f32[4,32,256]{2,0,1:T(4,128)S(1)}, f32[4,32,256]{2,0,1:T(4,128)S(1)}, u32[]{:S(2)}, u32[]{:S(2)}) collective-permute-start(f32[4,32,256]{2,0,1:T(4,128)S(1)} %get-tuple-element.90), channel_id=1, source_target_pairs={{0,64},{32,96},{64,0},{96,32},{1,65},{33,97},{65,1},{97,33},{2,66}... | collective-permute-start | bytes 393224 | tf_op jit(solution)/shard_map/ppermute | solution.py:43
  274.9 9.5 %collective-permute-start.25 = (f32[4,32,256]{2,0,1:T(4,128)S(1)}, f32[4,32,256]{2,0,1:T(4,128)S(1)}, u32[]{:S(2)}, u32[]{:S(2)}) collective-permute-start(f32[4,32,256]{2,0,1:T(4,128)S(1)} %get-tuple-element.90), channel_id=1, source_target_pairs={{0,96},{32,0},{64,32},{96,64},{1,97},{33,1},{65,33},{97,65},{2,98}... | collective-permute-start | bytes 393224 | tf_op jit(solution)/shard_map/ppermute | solution.py:43
  278.0 11.2 %collective-permute-start.34 = (f32[4,32,256]{2,0,1:T(4,128)S(1)}, f32[4,32,256]{2,0,1:T(4,128)S(1)}, u32[]{:S(2)}, u32[]{:S(2)}) collective-permute-start(f32[4,32,256]{2,0,1:T(4,128)S(1)} %get-tuple-element.20), channel_id=1, source_target_pairs={{0,64},{32,96},{64,0},{96,32},{1,65},{33,97},{65,1},{97,33},{2,66}... | collective-permute-start | bytes 393224 | tf_op jit(solution)/shard_map/ppermute | solution.py:43
  280.6 10.6 %collective-permute-start.35 = (f32[4,32,256]{2,0,1:T(4,128)S(1)}, f32[4,32,256]{2,0,1:T(4,128)S(1)}, u32[]{:S(2)}, u32[]{:S(2)}) collective-permute-start(f32[4,32,256]{2,0,1:T(4,128)S(1)} %get-tuple-element.20), channel_id=1, source_target_pairs={{0,96},{32,0},{64,32},{96,64},{1,97},{33,1},{65,33},{97,65},{2,98}... | collective-permute-start | bytes 393224 | tf_op jit(solution)/shard_map/ppermute | solution.py:43
  283.1 14.1 %collective-permute-start.43 = (f32[4,32,256]{2,0,1:T(4,128)S(1)}, f32[4,32,256]{2,0,1:T(4,128)S(1)}, u32[]{:S(2)}, u32[]{:S(2)}) collective-permute-start(f32[4,32,256]{2,0,1:T(4,128)S(1)} %get-tuple-element.92), channel_id=1, source_target_pairs={{0,32},{32,64},{64,96},{96,0},{1,33},{33,65},{65,97},{97,1},{2,34}... | collective-permute-start | bytes 393224 | tf_op jit(solution)/shard_map/ppermute | solution.py:43
  284.4 14.7 %collective-permute-start.44 = (f32[4,32,256]{2,0,1:T(4,128)S(1)}, f32[4,32,256]{2,0,1:T(4,128)S(1)}, u32[]{:S(2)}, u32[]{:S(2)}) collective-permute-start(f32[4,32,256]{2,0,1:T(4,128)S(1)} %get-tuple-element.92), channel_id=1, source_target_pairs={{0,64},{32,96},{64,0},{96,32},{1,65},{33,97},{65,1},{97,33},{2,66}... | collective-permute-start | bytes 393224 | tf_op jit(solution)/shard_map/ppermute | solution.py:43
  286.2 18.7 %collective-permute-start.45 = (f32[4,32,256]{2,0,1:T(4,128)S(1)}, f32[4,32,256]{2,0,1:T(4,128)S(1)}, u32[]{:S(2)}, u32[]{:S(2)}) collective-permute-start(f32[4,32,256]{2,0,1:T(4,128)S(1)} %get-tuple-element.92), channel_id=1, source_target_pairs={{0,96},{32,0},{64,32},{96,64},{1,97},{33,1},{65,33},{97,65},{2,98}... | collective-permute-start | bytes 393224 | tf_op jit(solution)/shard_map/ppermute | solution.py:43
  289.3 17.8 %collective-permute-start.16 = (f32[15,32,256]{2,0,1:T(8,128)S(1)}, f32[15,32,256]{2,0,1:T(8,128)S(1)}, u32[]{:S(2)}, u32[]{:S(2)}) collective-permute-start(f32[15,32,256]{2,0,1:T(8,128)S(1)} %get-tuple-element.63), channel_id=1, source_target_pairs={{0,1},{1,2},{2,3},{3,4},{4,5},{5,6},{6,7},{7,8},{8,9},{9,10},{10,1... | collective-permute-start | bytes 1474568 | tf_op jit(solution)/shard_map/ppermute | solution.py:17
  291.2 21.5 %collective-permute-start.17 = (f32[15,32,256]{2,0,1:T(8,128)S(1)}, f32[15,32,256]{2,0,1:T(8,128)S(1)}, u32[]{:S(2)}, u32[]{:S(2)}) collective-permute-start(f32[15,32,256]{2,0,1:T(8,128)S(1)} %get-tuple-element.64), channel_id=1, source_target_pairs={{1,0},{2,1},{3,2},{4,3},{5,4},{6,5},{7,6},{8,7},{9,8},{10,9},{11,1... | collective-permute-start | bytes 1474568 | tf_op jit(solution)/shard_map/ppermute | solution.py:19
  297.1 20.4 %collective-permute-start.26 = (f32[15,32,256]{2,0,1:T(8,128)S(1)}, f32[15,32,256]{2,0,1:T(8,128)S(1)}, u32[]{:S(2)}, u32[]{:S(2)}) collective-permute-start(f32[15,32,256]{2,0,1:T(8,128)S(1)} %get-tuple-element.68), channel_id=1, source_target_pairs={{0,1},{1,2},{2,3},{3,4},{4,5},{5,6},{6,7},{7,8},{8,9},{9,10},{10,1... | collective-permute-start | bytes 1474568 | tf_op jit(solution)/shard_map/ppermute | solution.py:17
  299.1 24.4 %collective-permute-start.27 = (f32[15,32,256]{2,0,1:T(8,128)S(1)}, f32[15,32,256]{2,0,1:T(8,128)S(1)}, u32[]{:S(2)}, u32[]{:S(2)}) collective-permute-start(f32[15,32,256]{2,0,1:T(8,128)S(1)} %get-tuple-element.69), channel_id=1, source_target_pairs={{1,0},{2,1},{3,2},{4,3},{5,4},{6,5},{7,6},{8,7},{9,8},{10,9},{11,1... | collective-permute-start | bytes 1474568 | tf_op jit(solution)/shard_map/ppermute | solution.py:19
  304.9 21.4 %collective-permute-start.36 = (f32[15,32,256]{2,0,1:T(8,128)S(1)}, f32[15,32,256]{2,0,1:T(8,128)S(1)}, u32[]{:S(2)}, u32[]{:S(2)}) collective-permute-start(f32[15,32,256]{2,0,1:T(8,128)S(1)} %get-tuple-element.73), channel_id=1, source_target_pairs={{0,1},{1,2},{2,3},{3,4},{4,5},{5,6},{6,7},{7,8},{8,9},{9,10},{10,1... | collective-permute-start | bytes 1474568 | tf_op jit(solution)/shard_map/ppermute | solution.py:17
  307.0 19.3 %collective-permute-start.37 = (f32[15,32,256]{2,0,1:T(8,128)S(1)}, f32[15,32,256]{2,0,1:T(8,128)S(1)}, u32[]{:S(2)}, u32[]{:S(2)}) collective-permute-start(f32[15,32,256]{2,0,1:T(8,128)S(1)} %get-tuple-element.74), channel_id=1, source_target_pairs={{1,0},{2,1},{3,2},{4,3},{5,4},{6,5},{7,6},{8,7},{9,8},{10,9},{11,1... | collective-permute-start | bytes 1474568 | tf_op jit(solution)/shard_map/ppermute | solution.py:19
  312.8 16.4 %collective-permute-start.46 = (f32[15,32,256]{2,0,1:T(8,128)S(1)}, f32[15,32,256]{2,0,1:T(8,128)S(1)}, u32[]{:S(2)}, u32[]{:S(2)}) collective-permute-start(f32[15,32,256]{2,0,1:T(8,128)S(1)} %get-tuple-element.78), channel_id=1, source_target_pairs={{0,1},{1,2},{2,3},{3,4},{4,5},{5,6},{6,7},{7,8},{8,9},{9,10},{10,1... | collective-permute-start | bytes 1474568 | tf_op jit(solution)/shard_map/ppermute | solution.py:17
  317.6 12.4 %collective-permute-start.47 = (f32[15,32,256]{2,0,1:T(8,128)S(1)}, f32[15,32,256]{2,0,1:T(8,128)S(1)}, u32[]{:S(2)}, u32[]{:S(2)}) collective-permute-start(f32[15,32,256]{2,0,1:T(8,128)S(1)} %get-tuple-element.79), channel_id=1, source_target_pairs={{1,0},{2,1},{3,2},{4,3},{5,4},{6,5},{7,6},{8,7},{9,8},{10,9},{11,1... | collective-permute-start | bytes 1474568 | tf_op jit(solution)/shard_map/ppermute | solution.py:19
  343.7 20.4 %collective-permute-start.64 = (f32[2,15,32,256]{3,2,1,0:T(8,128)S(1)}, f32[2,15,32,256]{3,2,1,0:T(8,128)S(1)}, u32[]{:S(2)}, u32[]{:S(2)}) collective-permute-start(f32[2,15,32,256]{3,2,1,0:T(8,128)S(1)} %get-tuple-element.39), channel_id=1, source_target_pairs={{0,1},{1,2},{2,3},{3,4},{4,5},{5,6},{6,7},{7,8},{8,9},{9,10},{10,1... | collective-permute-start | bytes 2949128 | tf_op jit(solution)/shard_map/ppermute | solution.py:17
  345.7 24.3 %collective-permute-start.65 = (f32[2,15,32,256]{3,2,1,0:T(8,128)S(1)}, f32[2,15,32,256]{3,2,1,0:T(8,128)S(1)}, u32[]{:S(2)}, u32[]{:S(2)}) collective-permute-start(f32[2,15,32,256]{3,2,1,0:T(8,128)S(1)} %get-tuple-element.40), channel_id=1, source_target_pairs={{1,0},{2,1},{3,2},{4,3},{5,4},{6,5},{7,6},{8,7},{9,8},{10,9},{11,1... | collective-permute-start | bytes 2949128 | tf_op jit(solution)/shard_map/ppermute | solution.py:19
  352.9 22.8 %collective-permute-start.72 = (f32[2,15,32,256]{3,2,1,0:T(8,128)S(1)}, f32[2,15,32,256]{3,2,1,0:T(8,128)S(1)}, u32[]{:S(2)}, u32[]{:S(2)}) collective-permute-start(f32[2,15,32,256]{3,2,1,0:T(8,128)S(1)} %get-tuple-element.41), channel_id=1, source_target_pairs={{0,1},{1,2},{2,3},{3,4},{4,5},{5,6},{6,7},{7,8},{8,9},{9,10},{10,1... | collective-permute-start | bytes 2949128 | tf_op jit(solution)/shard_map/ppermute | solution.py:17
  354.9 26.7 %collective-permute-start.73 = (f32[2,15,32,256]{3,2,1,0:T(8,128)S(1)}, f32[2,15,32,256]{3,2,1,0:T(8,128)S(1)}, u32[]{:S(2)}, u32[]{:S(2)}) collective-permute-start(f32[2,15,32,256]{3,2,1,0:T(8,128)S(1)} %get-tuple-element.42), channel_id=1, source_target_pairs={{1,0},{2,1},{3,2},{4,3},{5,4},{6,5},{7,6},{8,7},{9,8},{10,9},{11,1... | collective-permute-start | bytes 2949128 | tf_op jit(solution)/shard_map/ppermute | solution.py:19
  362.0 23.5 %collective-permute-start.48 = (f32[2,15,32,256]{3,2,1,0:T(8,128)S(1)}, f32[2,15,32,256]{3,2,1,0:T(8,128)S(1)}, u32[]{:S(2)}, u32[]{:S(2)}) collective-permute-start(f32[2,15,32,256]{3,2,1,0:T(8,128)S(1)} %get-tuple-element.35), channel_id=1, source_target_pairs={{0,1},{1,2},{2,3},{3,4},{4,5},{5,6},{6,7},{7,8},{8,9},{9,10},{10,1... | collective-permute-start | bytes 2949128 | tf_op jit(solution)/shard_map/ppermute | solution.py:17
  364.2 22.9 %collective-permute-start.49 = (f32[2,15,32,256]{3,2,1,0:T(8,128)S(1)}, f32[2,15,32,256]{3,2,1,0:T(8,128)S(1)}, u32[]{:S(2)}, u32[]{:S(2)}) collective-permute-start(f32[2,15,32,256]{3,2,1,0:T(8,128)S(1)} %get-tuple-element.36), channel_id=1, source_target_pairs={{1,0},{2,1},{3,2},{4,3},{5,4},{6,5},{7,6},{8,7},{9,8},{10,9},{11,1... | collective-permute-start | bytes 2949128 | tf_op jit(solution)/shard_map/ppermute | solution.py:19
  369.9 23.2 %collective-permute-start.56 = (f32[2,15,32,256]{3,2,1,0:T(8,128)S(1)}, f32[2,15,32,256]{3,2,1,0:T(8,128)S(1)}, u32[]{:S(2)}, u32[]{:S(2)}) collective-permute-start(f32[2,15,32,256]{3,2,1,0:T(8,128)S(1)} %get-tuple-element.37), channel_id=1, source_target_pairs={{0,1},{1,2},{2,3},{3,4},{4,5},{5,6},{6,7},{7,8},{8,9},{9,10},{10,1... | collective-permute-start | bytes 2949128 | tf_op jit(solution)/shard_map/ppermute | solution.py:17
  375.7 19.0 %collective-permute-start.57 = (f32[2,15,32,256]{3,2,1,0:T(8,128)S(1)}, f32[2,15,32,256]{3,2,1,0:T(8,128)S(1)}, u32[]{:S(2)}, u32[]{:S(2)}) collective-permute-start(f32[2,15,32,256]{3,2,1,0:T(8,128)S(1)} %get-tuple-element.38), channel_id=1, source_target_pairs={{1,0},{2,1},{3,2},{4,3},{5,4},{6,5},{7,6},{8,7},{9,8},{10,9},{11,1... | collective-permute-start | bytes 2949128 | tf_op jit(solution)/shard_map/ppermute | solution.py:19
  381.6 14.7 %collective-permute-start.66 = (f32[4,32,256]{2,0,1:T(4,128)S(1)}, f32[4,32,256]{2,0,1:T(4,128)S(1)}, u32[]{:S(2)}, u32[]{:S(2)}) collective-permute-start(f32[4,32,256]{2,0,1:T(4,128)S(1)} %get-tuple-element.57), channel_id=1, source_target_pairs={{0,32},{32,64},{64,96},{96,0},{1,33},{33,65},{65,97},{97,1},{2,34}... | collective-permute-start | bytes 393224 | tf_op jit(solution)/shard_map/ppermute | solution.py:37
  385.5 13.4 %collective-permute-start.67 = (f32[4,32,256]{2,0,1:T(4,128)S(1)}, f32[4,32,256]{2,0,1:T(4,128)S(1)}, u32[]{:S(2)}, u32[]{:S(2)}) collective-permute-start(f32[4,32,256]{2,0,1:T(4,128)S(1)} %get-tuple-element.59), channel_id=1, source_target_pairs={{0,64},{32,96},{64,0},{96,32},{1,65},{33,97},{65,1},{97,33},{2,66}... | collective-permute-start | bytes 393224 | tf_op jit(solution)/shard_map/ppermute | solution.py:37
  387.1 11.9 %collective-permute-start.68 = (f32[4,32,256]{2,0,1:T(4,128)S(1)}, f32[4,32,256]{2,0,1:T(4,128)S(1)}, u32[]{:S(2)}, u32[]{:S(2)}) collective-permute-start(f32[4,32,256]{2,0,1:T(4,128)S(1)} %get-tuple-element.58), channel_id=1, source_target_pairs={{0,96},{32,0},{64,32},{96,64},{1,97},{33,1},{65,33},{97,65},{2,98}... | collective-permute-start | bytes 393224 | tf_op jit(solution)/shard_map/ppermute | solution.py:37
  393.1 10.3 %collective-permute-start.74 = (f32[4,32,256]{2,0,1:T(4,128)S(1)}, f32[4,32,256]{2,0,1:T(4,128)S(1)}, u32[]{:S(2)}, u32[]{:S(2)}) collective-permute-start(f32[4,32,256]{2,0,1:T(4,128)S(1)} %get-tuple-element.60), channel_id=1, source_target_pairs={{0,32},{32,64},{64,96},{96,0},{1,33},{33,65},{65,97},{97,1},{2,34}... | collective-permute-start | bytes 393224 | tf_op jit(solution)/shard_map/ppermute | solution.py:37
  394.8 12.0 %collective-permute-start.75 = (f32[4,32,256]{2,0,1:T(4,128)S(1)}, f32[4,32,256]{2,0,1:T(4,128)S(1)}, u32[]{:S(2)}, u32[]{:S(2)}) collective-permute-start(f32[4,32,256]{2,0,1:T(4,128)S(1)} %get-tuple-element.62), channel_id=1, source_target_pairs={{0,64},{32,96},{64,0},{96,32},{1,65},{33,97},{65,1},{97,33},{2,66}... | collective-permute-start | bytes 393224 | tf_op jit(solution)/shard_map/ppermute | solution.py:37
  396.4 12.5 %collective-permute-start.76 = (f32[4,32,256]{2,0,1:T(4,128)S(1)}, f32[4,32,256]{2,0,1:T(4,128)S(1)}, u32[]{:S(2)}, u32[]{:S(2)}) collective-permute-start(f32[4,32,256]{2,0,1:T(4,128)S(1)} %get-tuple-element.61), channel_id=1, source_target_pairs={{0,96},{32,0},{64,32},{96,64},{1,97},{33,1},{65,33},{97,65},{2,98}... | collective-permute-start | bytes 393224 | tf_op jit(solution)/shard_map/ppermute | solution.py:37
  399.0 10.1 %collective-permute-start.50 = (f32[4,32,256]{2,0,1:T(4,128)S(1)}, f32[4,32,256]{2,0,1:T(4,128)S(1)}, u32[]{:S(2)}, u32[]{:S(2)}) collective-permute-start(f32[4,32,256]{2,0,1:T(4,128)S(1)} %get-tuple-element.51), channel_id=1, source_target_pairs={{0,32},{32,64},{64,96},{96,0},{1,33},{33,65},{65,97},{97,1},{2,34}... | collective-permute-start | bytes 393224 | tf_op jit(solution)/shard_map/ppermute | solution.py:37
  399.0 12.7 %collective-permute-start.51 = (f32[4,32,256]{2,0,1:T(4,128)S(1)}, f32[4,32,256]{2,0,1:T(4,128)S(1)}, u32[]{:S(2)}, u32[]{:S(2)}) collective-permute-start(f32[4,32,256]{2,0,1:T(4,128)S(1)} %get-tuple-element.53), channel_id=1, source_target_pairs={{0,64},{32,96},{64,0},{96,32},{1,65},{33,97},{65,1},{97,33},{2,66}... | collective-permute-start | bytes 393224 | tf_op jit(solution)/shard_map/ppermute | solution.py:37
  412.1 10.6 %collective-permute-start.53 = (f32[4,32,256]{2,0,1:T(4,128)S(1)}, f32[4,32,256]{2,0,1:T(4,128)S(1)}, u32[]{:S(2)}, u32[]{:S(2)}) collective-permute-start(f32[4,32,256]{2,0,1:T(4,128)S(1)} %get-tuple-element.8), channel_id=1, source_target_pairs={{0,32},{32,64},{64,96},{96,0},{1,33},{33,65},{65,97},{97,1},{2,34}... | collective-permute-start | bytes 393224 | tf_op jit(solution)/shard_map/ppermute | solution.py:43
  412.2 10.6 %collective-permute-start.54 = (f32[4,32,256]{2,0,1:T(4,128)S(1)}, f32[4,32,256]{2,0,1:T(4,128)S(1)}, u32[]{:S(2)}, u32[]{:S(2)}) collective-permute-start(f32[4,32,256]{2,0,1:T(4,128)S(1)} %get-tuple-element.8), channel_id=1, source_target_pairs={{0,64},{32,96},{64,0},{96,32},{1,65},{33,97},{65,1},{97,33},{2,66}... | collective-permute-start | bytes 393224 | tf_op jit(solution)/shard_map/ppermute | solution.py:43
  415.0 9.9 %collective-permute-start.55 = (f32[4,32,256]{2,0,1:T(4,128)S(1)}, f32[4,32,256]{2,0,1:T(4,128)S(1)}, u32[]{:S(2)}, u32[]{:S(2)}) collective-permute-start(f32[4,32,256]{2,0,1:T(4,128)S(1)} %get-tuple-element.8), channel_id=1, source_target_pairs={{0,96},{32,0},{64,32},{96,64},{1,97},{33,1},{65,33},{97,65},{2,98}... | collective-permute-start | bytes 393224 | tf_op jit(solution)/shard_map/ppermute | solution.py:43
  417.6 9.4 %collective-permute-start.61 = (f32[4,32,256]{2,0,1:T(4,128)S(1)}, f32[4,32,256]{2,0,1:T(4,128)S(1)}, u32[]{:S(2)}, u32[]{:S(2)}) collective-permute-start(f32[4,32,256]{2,0,1:T(4,128)S(1)} %get-tuple-element.10), channel_id=1, source_target_pairs={{0,32},{32,64},{64,96},{96,0},{1,33},{33,65},{65,97},{97,1},{2,34}... | collective-permute-start | bytes 393224 | tf_op jit(solution)/shard_map/ppermute | solution.py:43
  419.6 9.9 %collective-permute-start.62 = (f32[4,32,256]{2,0,1:T(4,128)S(1)}, f32[4,32,256]{2,0,1:T(4,128)S(1)}, u32[]{:S(2)}, u32[]{:S(2)}) collective-permute-start(f32[4,32,256]{2,0,1:T(4,128)S(1)} %get-tuple-element.10), channel_id=1, source_target_pairs={{0,64},{32,96},{64,0},{96,32},{1,65},{33,97},{65,1},{97,33},{2,66}... | collective-permute-start | bytes 393224 | tf_op jit(solution)/shard_map/ppermute | solution.py:43
  422.7 9.6 %collective-permute-start.69 = (f32[4,32,256]{2,0,1:T(4,128)S(1)}, f32[4,32,256]{2,0,1:T(4,128)S(1)}, u32[]{:S(2)}, u32[]{:S(2)}) collective-permute-start(f32[4,32,256]{2,0,1:T(4,128)S(1)} %get-tuple-element.88), channel_id=1, source_target_pairs={{0,32},{32,64},{64,96},{96,0},{1,33},{33,65},{65,97},{97,1},{2,34}... | collective-permute-start | bytes 393224 | tf_op jit(solution)/shard_map/ppermute | solution.py:43
  424.9 9.3 %collective-permute-start.70 = (f32[4,32,256]{2,0,1:T(4,128)S(1)}, f32[4,32,256]{2,0,1:T(4,128)S(1)}, u32[]{:S(2)}, u32[]{:S(2)}) collective-permute-start(f32[4,32,256]{2,0,1:T(4,128)S(1)} %get-tuple-element.88), channel_id=1, source_target_pairs={{0,64},{32,96},{64,0},{96,32},{1,65},{33,97},{65,1},{97,33},{2,66}... | collective-permute-start | bytes 393224 | tf_op jit(solution)/shard_map/ppermute | solution.py:43
  (25 other events, 254.2 us)

commit v3 on v2

--- a/solution.py
+++ b/solution.py
@@ -27,26 +27,15 @@
     count = lax.axis_size("view")
     me = lax.axis_index("view")
     rows = partial.shape[0] // count
-
-    def piece(cells, index):
-        return lax.dynamic_slice_in_dim(cells, index * rows, rows, axis=0)
-
-    summed = piece(partial, me)
-    for shift in range(1, count):
-        sent = piece(partial, (me + shift) % count)
-        summed = summed + lax.ppermute(
-            sent, "view", [(i, (i + shift) % count) for i in range(count)]
-        )
-    updated = piece(current, me) * jnp.exp(summed / piece(counts, me))
-    gathered = lax.dynamic_update_slice_in_dim(current, updated, me * rows, axis=0)
-    for shift in range(1, count):
-        arrived = lax.ppermute(
-            updated, "view", [(i, (i + shift) % count) for i in range(count)]
-        )
-        gathered = lax.dynamic_update_slice_in_dim(
-            gathered, arrived, ((me - shift) % count) * rows, axis=0
-        )
-    return gathered
+    quarters = partial.reshape((count, rows) + partial.shape[1:])
+    arrived = lax.all_to_all(quarters, "view", split_axis=0, concat_axis=0, tiled=True)
+    summed = jnp.sum(arrived, axis=0)
+    own = lax.dynamic_slice_in_dim(current, me * rows, rows, axis=0)
+    scale = lax.dynamic_slice_in_dim(counts, me * rows, rows, axis=0)
+    updated = own * jnp.exp(summed / scale)
+    copies = jnp.broadcast_to(updated[None], (count,) + updated.shape)
+    gathered = lax.all_to_all(copies, "view", split_axis=0, concat_axis=0, tiled=True)
+    return gathered.reshape(current.shape)
 
 
 def banded_blur_matrix(filter_tap_values, row_count, col_count, offset_base, orientation):

time: 450 us -> 552 us (1.23)
  blocking collectives: 0 us -> 34.6 us
  waiting for transfers between devices: 80.6 us -> 115 us
  local copies, waits for them, and re-layouts: 54 us -> 78 us
  other arithmetic: 7.81 us -> 24.2 us
  starting transfers between devices: 212 us -> 196 us
  matrix products: 84.8 us -> 92 us
    ppermute x48 -> x0, starting transfers between devices: 67.8 us -> none  [the longest x24 35.2 us: view_sum_update(): lax.ppermute(updated, 'view', [(i, (i + shift) % count) for i in range(co...]
    all_to_all x0 -> x13, starting transfers between devices: none -> 52.1 us  [the longest x8 33.4 us: view_sum_update(): lax.all_to_all(quarters, 'view', split_axis=0, concat_axis=0, tiled=True)]
    all_to_all x0 -> x13, waiting for transfers between devices: none -> 46.5 us  [the longest x5 26.8 us: view_sum_update(): lax.all_to_all(copies, 'view', split_axis=0, concat_axis=0, tiled=True)]
    all_to_all x0 -> x3, blocking collectives: none -> 34.6 us  [view_sum_update(): lax.all_to_all(copies, 'view', split_axis=0, concat_axis=0, tiled=True)]
    reshape x0 -> x20, local copies, waits for them, and re-layouts: none -> 18.3 us  [the longest x16 17.6 us: view_sum_update(): quarters = partial.reshape((count, rows) + partial.shape[1:])]
    ppermute x48 -> x0, waiting for transfers between devices: 16.9 us -> none  [the longest x24 10.4 us: view_sum_update(): lax.ppermute(updated, 'view', [(i, (i + shift) % count) for i in range(co...]
    slice x13, local copies, waits for them, and re-layouts: 3.41 us -> 13.8 us  [with_halo(): lax.slice_in_dim(cells, cells.shape[dim] - width, cells.shape[dim], axis=...]
    concatenate x8, other arithmetic: 3.09 us -> 12.5 us  [with_halo(): jnp.concatenate([lax.ppermute(tail, axis, [(i, (i + 1) % count) for i in...]
  transfers between devices with their start and end apart: 82 -> 47, of which waited for: 20 -> 12; matrix products, arithmetic and copies ran while one was open for 23% -> 26% of each run, Pallas kernels for 0% -> 0%
where the time goes in v3:
time: 552 us; the launch traced here: 541 us
  starting transfers between devices  196 us (36%)
  waiting for transfers between devices  115 us (21%)
  matrix products  92 us (17%)
  local copies, waits for them, and re-layouts  78 us (14%)
  blocking collectives  34.6 us (6%)
  other arithmetic  24.2 us (4%)
    ppermute x16, starting transfers between devices, with_halo(): lax.ppermute(head, axis, [((i + 1) % count, i) for i in range(ends)])  94.2 us
    ppermute x16, waiting for transfers between devices, with_halo(): lax.ppermute(tail, axis, [(i, (i + 1) % count) for i in range(ends)])  63.7 us
    all_to_all x3, blocking collectives, view_sum_update(): lax.all_to_all(copies, 'view', split_axis=0, concat_axis=0, tiled=True)  34.6 us
    ppermute x16, starting transfers between devices, with_halo(): lax.ppermute(tail, axis, [(i, (i + 1) % count) for i in range(ends)])  34.5 us
    all_to_all x8, starting transfers between devices, view_sum_update(): lax.all_to_all(quarters, 'view', split_axis=0, concat_axis=0, tiled=True)  33.4 us
    dot_general x8, matrix products, backward_chunk(): corrected = jnp.einsum('vwyz,vwx->vxyz', rimmed, adj_x, precision=highest)  29.6 us
    all_to_all x5, waiting for transfers between devices, view_sum_update(): lax.all_to_all(copies, 'view', split_axis=0, concat_axis=0, tiled=True)  26.8 us
    all_to_all x8, waiting for transfers between devices, view_sum_update(): lax.all_to_all(quarters, 'view', split_axis=0, concat_axis=0, tiled=True)  19.8 us
  transfers between devices with their start and end apart: 47, of which 12 were waited for; matrix products, arithmetic and copies ran while one was open for 26% of the time, Pallas kernels for 0%

profile of v3, /device:TPU:64, one launch (start us, length us, event | category | flops | bytes accessed | tf_op | source)
XLA Modules:
  0.0 541.1 jit_solution(5498812729982565133)
XLA Ops:
  3.6 7.6 %all-to-all-start = ((f32[32,1,1]{2,1,0:T(1,128)}), f32[32,1,1]{2,1,0:T(1,128)S(1)}, u32[]{:S(2)}, u32[]{:S(2)}) async-start(f32[32,1,1]{2,1,0:T(1,128)} %copy.281), calls=%async_computation | async-start | bytes 32768 | tf_op jit(solution)/shard_map/all_to_all | solution.py:96
  11.2 4.3 broadcast_in_dim.39
  15.4 8.0 %scatter_fusion = f32[32,2,128,256]{3,2,1,0:T(8,128)} fusion(f32[32,2,128,256]{3,2,1,0:T(8,128)} %broadcast_in_dim.39, s32[16]{0:T(128)S(1)} %fusion.241, f32[16,2,128,256]{3,2,1,0:T(8,128)} %bitcast.174), kind=kCustom, calls=%fused_computation.1 | custom fusion | bytes 12582976 | tf_op jit(solution)/shard_map/scatter | solution.py:81
  23.5 7.1 %all-to-all-start.1 = ((f32[32,1,2,128,256]{4,3,2,1,0:T(8,128)}), f32[32,1,2,128,256]{4,3,2,1,0:T(8,128)}, u32[]{:S(2)}, u32[]{:S(2)}) async-start(f32[32,1,2,128,256]{4,3,2,1,0:T(8,128)} %bitcast.171), calls=%async_computation.1 | async-start | bytes 16777216 | tf_op jit(solution)/shard_map/all_to_all | solution.py:89
  36.3 5.6 %collective-permute-start.5 = (f32[15,32,256]{2,0,1:T(8,128)}, f32[15,32,256]{2,0,1:T(8,128)}, u32[]{:S(2)}, u32[]{:S(2)}) collective-permute-start(f32[15,32,256]{2,0,1:T(8,128)} %copy.477), channel_id=1, source_target_pairs={{1,0},{2,1},{3,2},{4,3},{5,4},{6,5},{7,6},{8,7},{9,8},{10,9},{11,1... | collective-permute-start | bytes 1474568 | tf_op jit(solution)/shard_map/ppermute | solution.py:19
  46.0 5.7 %collective-permute-start.3 = (f32[15,32,256]{2,0,1:T(8,128)}, f32[15,32,256]{2,0,1:T(8,128)}, u32[]{:S(2)}, u32[]{:S(2)}) collective-permute-start(f32[15,32,256]{2,0,1:T(8,128)} %copy.474), channel_id=1, source_target_pairs={{1,0},{2,1},{3,2},{4,3},{5,4},{6,5},{7,6},{8,7},{9,8},{10,9},{11,1... | collective-permute-start | bytes 1474568 | tf_op jit(solution)/shard_map/ppermute | solution.py:19
  64.3 63.6 %collective-permute-done.4 = f32[15,32,256]{2,0,1:T(8,128)} collective-permute-done((f32[15,32,256]{2,0,1:T(8,128)}, f32[15,32,256]{2,0,1:T(8,128)}, u32[]{:S(2)}, u32[]{:S(2)}) %collective-permute-start.4) | collective-permute-done | bytes 491552 | tf_op jit(solution)/shard_map/ppermute | solution.py:17
  129.8 2.2 collective-permute-done.5
  132.0 5.6 %collective-permute-start.6 = (f32[15,32,256]{2,0,1:T(8,128)}, f32[15,32,256]{2,0,1:T(8,128)S(1)}, u32[]{:S(2)}, u32[]{:S(2)}) collective-permute-start(f32[15,32,256]{2,0,1:T(8,128)} %copy.478), channel_id=1, source_target_pairs={{0,1},{1,2},{2,3},{3,4},{4,5},{5,6},{6,7},{7,8},{8,9},{9,10},{10,1... | collective-permute-start | bytes 1474568 | tf_op jit(solution)/shard_map/ppermute | solution.py:17
  137.6 2.3 fusion.65
  140.0 10.9 %collective-permute-start.7 = (f32[15,32,256]{2,0,1:T(8,128)}, f32[15,32,256]{2,0,1:T(8,128)S(1)}, u32[]{:S(2)}, u32[]{:S(2)}) collective-permute-start(f32[15,32,256]{2,0,1:T(8,128)} %copy.480), channel_id=1, source_target_pairs={{1,0},{2,1},{3,2},{4,3},{5,4},{6,5},{7,6},{8,7},{9,8},{10,9},{11,1... | collective-permute-start | bytes 1474568 | tf_op jit(solution)/shard_map/ppermute | solution.py:19
  150.9 2.3 fusion.60
  155.4 2.4 collective-permute-done.7
  165.7 5.5 %fusion.1 = f32[2,128,16,256]{3,1,2,0:T(8,128)} fusion(f32[2,128,128,1]{1,2,3,0:T(8,128)S(1)} %copy.369, f32[2,16,32,256]{3,2,1,0:T(8,128)S(1)} %fusion.193, f32[2,16,32,256]{3,2,1,0:T(8,128)S(1)} %fusion.195, f32[2,16,32,256]{3,2,1,0:T(8,128)S(1)} %fusion.197, f32[2,16,32,256]{3,2,1,0:T(8,128)S(1)} %fusion.199), kind=kOutput, calls=%fused_computation.5 | convolution fusion | flops 1613758464 | bytes 8519680 | tf_op jit(solution)/shard_map/vxyz,vyq->vxqz/dot_general | solution.py:145
  171.2 2.5 broadcast_in_dim.35
  173.7 14.2 %scatter_fusion.1 = f32[16,2,128,256]{3,2,1,0:T(8,128)} fusion(f32[16,2,128,256]{3,2,1,0:T(8,128)} %broadcast_in_dim.35, s32[32]{0:T(128)S(1)} %fusion.240, f32[32,2,128,256]{3,2,1,0:T(8,128)} %bitcast.15), kind=kCustom, calls=%fused_computation.2 | custom fusion | bytes 25165952 | tf_op jit(solution)/shard_map/scatter | solution.py:105
  187.9 6.7 %fusion.44 = f32[2,16,128,256]{3,2,1,0:T(8,128)S(1)} fusion(f32[2,128,16,256]{3,1,2,0:T(8,128)} %fusion.1, f32[2,16]{1,0:T(2,128)S(1)} %get-tuple-element.44, f32[2,16]{1,0:T(2,128)S(1)} %broadcast_in_dim_reshape.6, f32[2,128,128,1]{2,0,1,3:T(2,128)S(1)} %fusion.168, f32[2,16,128,256]{3,2,1,0:T(8,128)} %bitcast.172), kind=kOutput, calls=%fused_computation.56 | convolution fusion | flops 1613758464 | bytes 12714240 | tf_op jit(solution)/shard_map/vxyz,vqy->vxqz/dot_general | solution.py:147
  199.0 6.0 %collective-permute-start.13 = (f32[2,15,32,256]{3,2,1,0:T(8,128)S(1)}, f32[2,15,32,256]{3,2,1,0:T(8,128)S(1)}, u32[]{:S(2)}, u32[]{:S(2)}) collective-permute-start(f32[2,15,32,256]{3,2,1,0:T(8,128)S(1)} %get-tuple-element.30), channel_id=1, source_target_pairs={{1,0},{2,1},{3,2},{4,3},{5,4},{6,5},{7,6},{8,7},{9,8},{10,9},{11,1... | collective-permute-start | bytes 2949128 | tf_op jit(solution)/shard_map/ppermute | solution.py:19
  209.3 5.8 %collective-permute-start.17 = (f32[2,15,32,256]{3,2,1,0:T(8,128)}, f32[2,15,32,256]{3,2,1,0:T(8,128)}, u32[]{:S(2)}, u32[]{:S(2)}) collective-permute-start(f32[2,15,32,256]{3,2,1,0:T(8,128)} %get-tuple-element.32), channel_id=1, source_target_pairs={{1,0},{2,1},{3,2},{4,3},{5,4},{6,5},{7,6},{8,7},{9,8},{10,9},{11,1... | collective-permute-start | bytes 2949128 | tf_op jit(solution)/shard_map/ppermute | solution.py:19
  219.6 5.8 %collective-permute-start.21 = (f32[2,15,32,256]{3,2,1,0:T(8,128)}, f32[2,15,32,256]{3,2,1,0:T(8,128)}, u32[]{:S(2)}, u32[]{:S(2)}) collective-permute-start(f32[2,15,32,256]{3,2,1,0:T(8,128)} %get-tuple-element.34), channel_id=1, source_target_pairs={{1,0},{2,1},{3,2},{4,3},{5,4},{6,5},{7,6},{8,7},{9,8},{10,9},{11,1... | collective-permute-start | bytes 2949128 | tf_op jit(solution)/shard_map/ppermute | solution.py:19
  229.3 5.9 %collective-permute-start.9 = (f32[2,15,32,256]{3,2,1,0:T(8,128)}, f32[2,15,32,256]{3,2,1,0:T(8,128)}, u32[]{:S(2)}, u32[]{:S(2)}) collective-permute-start(f32[2,15,32,256]{3,2,1,0:T(8,128)} %get-tuple-element.28), channel_id=1, source_target_pairs={{1,0},{2,1},{3,2},{4,3},{5,4},{6,5},{7,6},{8,7},{9,8},{10,9},{11,1... | collective-permute-start | bytes 2949128 | tf_op jit(solution)/shard_map/ppermute | solution.py:19
  235.2 4.1 fusion.161
  243.2 4.7 all-to-all-start.4
  247.9 2.2 pad_maximum_fusion.2
  250.1 4.1 fusion.158
  258.1 4.8 all-to-all-start.6
  264.8 3.3 fusion.155
  271.1 3.7 all-to-all-start.8
  276.7 3.3 fusion.164
  282.8 3.5 all-to-all-start.2
  289.0 5.3 all-to-all-done.2
  295.9 12.4 %all_to_all.94 = f32[4,4,32,256]{3,1,2,0:T(4,128)S(1)} all-to-all(f32[4,4,32,256]{3,1,2,0:T(4,128)S(1)} %broadcast_in_dim.41), channel_id=1, replica_groups=mesh['view'=4,'block'=32] {'view'}, dimensions={0} | all-to-all | bytes 1048576 | tf_op jit(solution)/shard_map/all_to_all | solution.py:37
  308.4 11.7 %all_to_all.95 = f32[4,4,32,256]{3,1,2,0:T(4,128)S(1)} all-to-all(f32[4,4,32,256]{3,1,2,0:T(4,128)S(1)} %broadcast_in_dim.42), channel_id=1, replica_groups=mesh['view'=4,'block'=32] {'view'}, dimensions={0} | all-to-all | bytes 1048576 | tf_op jit(solution)/shard_map/all_to_all | solution.py:37
  321.0 3.5 all-to-all-start.7
  327.7 5.8 %collective-permute-start.11 = (f32[15,32,256]{2,0,1:T(8,128)}, f32[15,32,256]{2,0,1:T(8,128)}, u32[]{:S(2)}, u32[]{:S(2)}) collective-permute-start(f32[15,32,256]{2,0,1:T(8,128)} %get-tuple-element.36), channel_id=1, source_target_pairs={{1,0},{2,1},{3,2},{4,3},{5,4},{6,5},{7,6},{8,7},{9,8},{10,9},{11,1... | collective-permute-start | bytes 1474568 | tf_op jit(solution)/shard_map/ppermute | solution.py:19
  334.7 4.8 all-to-all-start.9
  342.5 5.8 %collective-permute-start.15 = (f32[15,32,256]{2,0,1:T(8,128)}, f32[15,32,256]{2,0,1:T(8,128)}, u32[]{:S(2)}, u32[]{:S(2)}) collective-permute-start(f32[15,32,256]{2,0,1:T(8,128)} %get-tuple-element.38), channel_id=1, source_target_pairs={{1,0},{2,1},{3,2},{4,3},{5,4},{6,5},{7,6},{8,7},{9,8},{10,9},{11,1... | collective-permute-start | bytes 1474568 | tf_op jit(solution)/shard_map/ppermute | solution.py:19
  352.0 5.8 %collective-permute-start.19 = (f32[15,32,256]{2,0,1:T(8,128)}, f32[15,32,256]{2,0,1:T(8,128)S(1)}, u32[]{:S(2)}, u32[]{:S(2)}) collective-permute-start(f32[15,32,256]{2,0,1:T(8,128)} %get-tuple-element.40), channel_id=1, source_target_pairs={{1,0},{2,1},{3,2},{4,3},{5,4},{6,5},{7,6},{8,7},{9,8},{10,9},{11,1... | collective-permute-start | bytes 1474568 | tf_op jit(solution)/shard_map/ppermute | solution.py:19
  359.7 2.3 fusion.75
  363.7 6.2 %collective-permute-start.23 = (f32[15,32,256]{2,0,1:T(8,128)S(1)}, f32[15,32,256]{2,0,1:T(8,128)S(1)}, u32[]{:S(2)}, u32[]{:S(2)}) collective-permute-start(f32[15,32,256]{2,0,1:T(8,128)S(1)} %get-tuple-element.42), channel_id=1, source_target_pairs={{1,0},{2,1},{3,2},{4,3},{5,4},{6,5},{7,6},{8,7},{9,8},{10,9},{11,1... | collective-permute-start | bytes 1474568 | tf_op jit(solution)/shard_map/ppermute | solution.py:19
  369.9 2.3 fusion.80
  380.7 4.3 fusion.9
  385.0 4.6 fusion.47
  394.0 5.8 %collective-permute-start.27 = (f32[2,15,32,256]{3,2,1,0:T(8,128)S(1)}, f32[2,15,32,256]{3,2,1,0:T(8,128)S(1)}, u32[]{:S(2)}, u32[]{:S(2)}) collective-permute-start(f32[2,15,32,256]{3,2,1,0:T(8,128)S(1)} %get-tuple-element.22), channel_id=1, source_target_pairs={{1,0},{2,1},{3,2},{4,3},{5,4},{6,5},{7,6},{8,7},{9,8},{10,9},{11,1... | collective-permute-start | bytes 2949128 | tf_op jit(solution)/shard_map/ppermute | solution.py:19
  404.0 5.8 %collective-permute-start.29 = (f32[2,15,32,256]{3,2,1,0:T(8,128)}, f32[2,15,32,256]{3,2,1,0:T(8,128)}, u32[]{:S(2)}, u32[]{:S(2)}) collective-permute-start(f32[2,15,32,256]{3,2,1,0:T(8,128)} %get-tuple-element.24), channel_id=1, source_target_pairs={{1,0},{2,1},{3,2},{4,3},{5,4},{6,5},{7,6},{8,7},{9,8},{10,9},{11,1... | collective-permute-start | bytes 2949128 | tf_op jit(solution)/shard_map/ppermute | solution.py:19
  414.3 5.8 %collective-permute-start.31 = (f32[2,15,32,256]{3,2,1,0:T(8,128)}, f32[2,15,32,256]{3,2,1,0:T(8,128)}, u32[]{:S(2)}, u32[]{:S(2)}) collective-permute-start(f32[2,15,32,256]{3,2,1,0:T(8,128)} %get-tuple-element.26), channel_id=1, source_target_pairs={{1,0},{2,1},{3,2},{4,3},{5,4},{6,5},{7,6},{8,7},{9,8},{10,9},{11,1... | collective-permute-start | bytes 2949128 | tf_op jit(solution)/shard_map/ppermute | solution.py:19
  423.9 6.0 %collective-permute-start.25 = (f32[2,15,32,256]{3,2,1,0:T(8,128)}, f32[2,15,32,256]{3,2,1,0:T(8,128)}, u32[]{:S(2)}, u32[]{:S(2)}) collective-permute-start(f32[2,15,32,256]{3,2,1,0:T(8,128)} %get-tuple-element.20), channel_id=1, source_target_pairs={{1,0},{2,1},{3,2},{4,3},{5,4},{6,5},{7,6},{8,7},{9,8},{10,9},{11,1... | collective-permute-start | bytes 2949128 | tf_op jit(solution)/shard_map/ppermute | solution.py:19
  429.9 4.1 fusion.149
  436.0 4.8 all-to-all-start.12
  440.8 2.2 pad_maximum_fusion.6
  443.0 4.1 fusion.146
  451.0 4.8 all-to-all-start.14
  457.6 3.3 fusion.143
  464.0 3.7 all-to-all-start.16
  469.6 3.3 fusion.152
  475.7 3.5 all-to-all-start.10
  480.6 6.6 %all-to-all-done.10 = f32[4,4,32,256]{3,1,2,0:T(4,128)S(1)} async-done(((f32[4,4,32,256]{3,1,2,0:T(4,128)}), f32[4,4,32,256]{3,1,2,0:T(4,128)S(1)}, u32[]{:S(2)}, u32[]{:S(2)}) %all-to-all-start.10) | async-done | bytes 524320 | tf_op jit(solution)/shard_map/all_to_all | solution.py:31
  489.6 3.5 all-to-all-start.11
  493.1 8.1 %all-to-all-done.11 = f32[4,4,32,256]{3,2,1,0:T(8,128)S(1)} async-done(((f32[4,4,32,256]{3,2,1,0:T(8,128)}), f32[4,4,32,256]{3,2,1,0:T(8,128)S(1)}, u32[]{:S(2)}, u32[]{:S(2)}) %all-to-all-start.11) | async-done | bytes 524320 | tf_op jit(solution)/shard_map/all_to_all | solution.py:37
  502.1 3.5 all-to-all-start.13
  505.6 9.3 %all-to-all-done.13 = f32[4,4,32,256]{3,2,1,0:T(8,128)S(1)} async-done(((f32[4,4,32,256]{3,2,1,0:T(8,128)}), f32[4,4,32,256]{3,2,1,0:T(8,128)S(1)}, u32[]{:S(2)}, u32[]{:S(2)}) %all-to-all-start.13) | async-done | bytes 524320 | tf_op jit(solution)/shard_map/all_to_all | solution.py:37
  515.7 3.5 all-to-all-start.15
  519.3 9.4 %all-to-all-done.15 = f32[4,4,32,256]{3,2,1,0:T(8,128)S(1)} async-done(((f32[4,4,32,256]{3,2,1,0:T(8,128)}), f32[4,4,32,256]{3,2,1,0:T(8,128)S(1)}, u32[]{:S(2)}, u32[]{:S(2)}) %all-to-all-start.15) | async-done | bytes 524320 | tf_op jit(solution)/shard_map/all_to_all | solution.py:37
  528.7 10.5 %all_to_all.96 = f32[4,4,32,256]{3,2,1,0:T(8,128)S(1)} all-to-all(f32[4,4,32,256]{3,2,1,0:T(8,128)S(1)} %broadcast_in_dim.48), channel_id=1, replica_groups=mesh['view'=4,'block'=32] {'view'}, dimensions={0} | all-to-all | bytes 1048576 | tf_op jit(solution)/shard_map/all_to_all | solution.py:37
  (218 shorter events, 139.5 us)
Async XLA Ops:
  3.6 19.9 %all-to-all-start = ((f32[32,1,1]{2,1,0:T(1,128)}), f32[32,1,1]{2,1,0:T(1,128)S(1)}, u32[]{:S(2)}, u32[]{:S(2)}) async-start(f32[32,1,1]{2,1,0:T(1,128)} %copy.281), calls=%async_computation | async-start | bytes 32768 | tf_op jit(solution)/shard_map/all_to_all | solution.py:96
  23.5 7.1 %copy-start.1 = (f32[16,128,256]{2,1,0:T(8,128)S(1)}, f32[16,128,256]{2,1,0:T(8,128)}, u32[]{:S(2)}) copy-start(f32[16,128,256]{2,1,0:T(8,128)} %param.8) | copy-start | bytes 6291460
  23.5 147.8 %all-to-all-start.1 = ((f32[32,1,2,128,256]{4,3,2,1,0:T(8,128)}), f32[32,1,2,128,256]{4,3,2,1,0:T(8,128)}, u32[]{:S(2)}, u32[]{:S(2)}) async-start(f32[32,1,2,128,256]{4,3,2,1,0:T(8,128)} %bitcast.171), calls=%async_computation.1 | async-start | bytes 16777216 | tf_op jit(solution)/shard_map/all_to_all | solution.py:89
  31.9 22.9 %copy-start.16 = (f32[2,3,31]{2,0,1:T(2,128)S(1)}, f32[2,3,31]{2,0,1:T(2,128)}, u32[]{:S(2)}) copy-start(f32[2,3,31]{2,0,1:T(2,128)} %param.14) | copy-start | bytes 2236
  31.9 23.0 %copy-start.17 = (s32[2,2]{1,0:T(2,128)S(1)}, s32[2,2]{1,0:T(2,128)}, u32[]{:S(2)}) copy-start(s32[2,2]{1,0:T(2,128)} %param.12) | copy-start | bytes 52
  33.0 23.2 %copy-start.18 = (f32[2]{0:T(128)S(1)}, f32[2]{0:T(128)}, u32[]{:S(2)}) copy-start(f32[2]{0:T(128)} %param.15) | copy-start | bytes 28
  33.0 94.9 %collective-permute-start.4 = (f32[15,32,256]{2,0,1:T(8,128)}, f32[15,32,256]{2,0,1:T(8,128)}, u32[]{:S(2)}, u32[]{:S(2)}) collective-permute-start(f32[15,32,256]{2,0,1:T(8,128)} %copy.475), channel_id=1, source_target_pairs={{0,1},{1,2},{2,3},{3,4},{4,5},{5,6},{6,7},{7,8},{8,9},{9,10},{10,1... | collective-permute-start | bytes 1474568 | tf_op jit(solution)/shard_map/ppermute | solution.py:17
  36.3 95.8 %collective-permute-start.5 = (f32[15,32,256]{2,0,1:T(8,128)}, f32[15,32,256]{2,0,1:T(8,128)}, u32[]{:S(2)}, u32[]{:S(2)}) collective-permute-start(f32[15,32,256]{2,0,1:T(8,128)} %copy.477), channel_id=1, source_target_pairs={{1,0},{2,1},{3,2},{4,3},{5,4},{6,5},{7,6},{8,7},{9,8},{10,9},{11,1... | collective-permute-start | bytes 1474568 | tf_op jit(solution)/shard_map/ppermute | solution.py:19
  43.0 96.9 %collective-permute-start.2 = (f32[15,32,256]{2,0,1:T(8,128)}, f32[15,32,256]{2,0,1:T(8,128)}, u32[]{:S(2)}, u32[]{:S(2)}) collective-permute-start(f32[15,32,256]{2,0,1:T(8,128)} %copy.472), channel_id=1, source_target_pairs={{0,1},{1,2},{2,3},{3,4},{4,5},{5,6},{6,7},{7,8},{8,9},{9,10},{10,1... | collective-permute-start | bytes 1474568 | tf_op jit(solution)/shard_map/ppermute | solution.py:17
  46.0 104.8 %collective-permute-start.3 = (f32[15,32,256]{2,0,1:T(8,128)}, f32[15,32,256]{2,0,1:T(8,128)}, u32[]{:S(2)}, u32[]{:S(2)}) collective-permute-start(f32[15,32,256]{2,0,1:T(8,128)} %copy.474), channel_id=1, source_target_pairs={{1,0},{2,1},{3,2},{4,3},{5,4},{6,5},{7,6},{8,7},{9,8},{10,9},{11,1... | collective-permute-start | bytes 1474568 | tf_op jit(solution)/shard_map/ppermute | solution.py:19
  52.9 100.3 %collective-permute-start = (f32[15,32,256]{2,0,1:T(8,128)}, f32[15,32,256]{2,0,1:T(8,128)}, u32[]{:S(2)}, u32[]{:S(2)}) collective-permute-start(f32[15,32,256]{2,0,1:T(8,128)} %copy.470), channel_id=1, source_target_pairs={{0,1},{1,2},{2,3},{3,4},{4,5},{5,6},{6,7},{7,8},{8,9},{9,10},{10,1... | collective-permute-start | bytes 1474568 | tf_op jit(solution)/shard_map/ppermute | solution.py:17
  56.2 131.7 %copy-start.14 = (f32[2,128,128,1]{2,0,1,3:T(2,128)}, f32[2,128,128,1]{2,0,1,3:T(2,128)S(1)}, u32[]{:S(2)}) copy-start(f32[2,128,128,1]{2,0,1,3:T(2,128)S(1)} %fusion.168) | copy-start | bytes 393220
  59.3 91.5 %copy-start.7 = (f32[16,32,256]{2,0,1:T(8,128)}, f32[16,32,256]{2,0,1:T(8,128)S(1)}, u32[]{:S(2)}) copy-start(f32[16,32,256]{2,0,1:T(8,128)S(1)} %copy.473) | copy-start | bytes 1572868
  60.8 92.5 %copy-start.8 = (f32[16,32,256]{2,0,1:T(8,128)}, f32[16,32,256]{2,0,1:T(8,128)S(1)}, u32[]{:S(2)}) copy-start(f32[16,32,256]{2,0,1:T(8,128)S(1)} %copy.469) | copy-start | bytes 1572868
  63.3 94.6 %copy-start.9 = (f32[16,32,256]{2,0,1:T(8,128)}, f32[16,32,256]{2,0,1:T(8,128)S(1)}, u32[]{:S(2)}) copy-start(f32[16,32,256]{2,0,1:T(8,128)S(1)} %copy.479) | copy-start | bytes 1572868
  127.9 25.3 %collective-permute-start.1 = (f32[15,32,256]{2,0,1:T(8,128)}, f32[15,32,256]{2,0,1:T(8,128)S(1)}, u32[]{:S(2)}, u32[]{:S(2)}) collective-permute-start(f32[15,32,256]{2,0,1:T(8,128)} %copy.471), channel_id=1, source_target_pairs={{1,0},{2,1},{3,2},{4,3},{5,4},{6,5},{7,6},{8,7},{9,8},{10,9},{11,1... | collective-permute-start | bytes 1474568 | tf_op jit(solution)/shard_map/ppermute | solution.py:19
  132.0 23.4 %collective-permute-start.6 = (f32[15,32,256]{2,0,1:T(8,128)}, f32[15,32,256]{2,0,1:T(8,128)S(1)}, u32[]{:S(2)}, u32[]{:S(2)}) collective-permute-start(f32[15,32,256]{2,0,1:T(8,128)} %copy.478), channel_id=1, source_target_pairs={{0,1},{1,2},{2,3},{3,4},{4,5},{5,6},{6,7},{7,8},{8,9},{9,10},{10,1... | collective-permute-start | bytes 1474568 | tf_op jit(solution)/shard_map/ppermute | solution.py:17
  140.0 17.9 %collective-permute-start.7 = (f32[15,32,256]{2,0,1:T(8,128)}, f32[15,32,256]{2,0,1:T(8,128)S(1)}, u32[]{:S(2)}, u32[]{:S(2)}) collective-permute-start(f32[15,32,256]{2,0,1:T(8,128)} %copy.480), channel_id=1, source_target_pairs={{1,0},{2,1},{3,2},{4,3},{5,4},{6,5},{7,6},{8,7},{9,8},{10,9},{11,1... | collective-permute-start | bytes 1474568 | tf_op jit(solution)/shard_map/ppermute | solution.py:19
  196.9 9.4 %copy-start.2 = (f32[2,16,32,256]{3,2,1,0:T(8,128)}, f32[2,16,32,256]{3,2,1,0:T(8,128)S(1)}, u32[]{:S(2)}) copy-start(f32[2,16,32,256]{3,2,1,0:T(8,128)S(1)} %fusion.179) | copy-start | bytes 3145732
  197.1 22.5 %collective-permute-start.12 = (f32[2,15,32,256]{3,2,1,0:T(8,128)S(1)}, f32[2,15,32,256]{3,2,1,0:T(8,128)S(1)}, u32[]{:S(2)}, u32[]{:S(2)}) collective-permute-start(f32[2,15,32,256]{3,2,1,0:T(8,128)S(1)} %get-tuple-element.29), channel_id=1, source_target_pairs={{0,1},{1,2},{2,3},{3,4},{4,5},{5,6},{6,7},{7,8},{8,9},{9,10},{10,1... | collective-permute-start | bytes 2949128 | tf_op jit(solution)/shard_map/ppermute | solution.py:17
  199.0 27.9 %collective-permute-start.13 = (f32[2,15,32,256]{3,2,1,0:T(8,128)S(1)}, f32[2,15,32,256]{3,2,1,0:T(8,128)S(1)}, u32[]{:S(2)}, u32[]{:S(2)}) collective-permute-start(f32[2,15,32,256]{3,2,1,0:T(8,128)S(1)} %get-tuple-element.30), channel_id=1, source_target_pairs={{1,0},{2,1},{3,2},{4,3},{5,4},{6,5},{7,6},{8,7},{9,8},{10,9},{11,1... | collective-permute-start | bytes 2949128 | tf_op jit(solution)/shard_map/ppermute | solution.py:19
  207.4 21.9 %collective-permute-start.16 = (f32[2,15,32,256]{3,2,1,0:T(8,128)S(1)}, f32[2,15,32,256]{3,2,1,0:T(8,128)}, u32[]{:S(2)}, u32[]{:S(2)}) collective-permute-start(f32[2,15,32,256]{3,2,1,0:T(8,128)S(1)} %get-tuple-element.31), channel_id=1, source_target_pairs={{0,1},{1,2},{2,3},{3,4},{4,5},{5,6},{6,7},{7,8},{8,9},{9,10},{10,1... | collective-permute-start | bytes 2949128 | tf_op jit(solution)/shard_map/ppermute | solution.py:17
  209.3 38.6 %collective-permute-start.17 = (f32[2,15,32,256]{3,2,1,0:T(8,128)}, f32[2,15,32,256]{3,2,1,0:T(8,128)}, u32[]{:S(2)}, u32[]{:S(2)}) collective-permute-start(f32[2,15,32,256]{3,2,1,0:T(8,128)} %get-tuple-element.32), channel_id=1, source_target_pairs={{1,0},{2,1},{3,2},{4,3},{5,4},{6,5},{7,6},{8,7},{9,8},{10,9},{11,1... | collective-permute-start | bytes 2949128 | tf_op jit(solution)/shard_map/ppermute | solution.py:19
  216.6 46.3 %collective-permute-start.20 = (f32[2,15,32,256]{3,2,1,0:T(8,128)}, f32[2,15,32,256]{3,2,1,0:T(8,128)}, u32[]{:S(2)}, u32[]{:S(2)}) collective-permute-start(f32[2,15,32,256]{3,2,1,0:T(8,128)} %get-tuple-element.33), channel_id=1, source_target_pairs={{0,1},{1,2},{2,3},{3,4},{4,5},{5,6},{6,7},{7,8},{8,9},{9,10},{10,1... | collective-permute-start | bytes 2949128 | tf_op jit(solution)/shard_map/ppermute | solution.py:17
  219.6 43.3 %collective-permute-start.21 = (f32[2,15,32,256]{3,2,1,0:T(8,128)}, f32[2,15,32,256]{3,2,1,0:T(8,128)}, u32[]{:S(2)}, u32[]{:S(2)}) collective-permute-start(f32[2,15,32,256]{3,2,1,0:T(8,128)} %get-tuple-element.34), channel_id=1, source_target_pairs={{1,0},{2,1},{3,2},{4,3},{5,4},{6,5},{7,6},{8,7},{9,8},{10,9},{11,1... | collective-permute-start | bytes 2949128 | tf_op jit(solution)/shard_map/ppermute | solution.py:19
  227.0 47.9 %collective-permute-start.8 = (f32[2,15,32,256]{3,2,1,0:T(8,128)}, f32[2,15,32,256]{3,2,1,0:T(8,128)}, u32[]{:S(2)}, u32[]{:S(2)}) collective-permute-start(f32[2,15,32,256]{3,2,1,0:T(8,128)} %get-tuple-element.27), channel_id=1, source_target_pairs={{0,1},{1,2},{2,3},{3,4},{4,5},{5,6},{6,7},{7,8},{8,9},{9,10},{10,1... | collective-permute-start | bytes 2949128 | tf_op jit(solution)/shard_map/ppermute | solution.py:17
  229.3 45.5 %collective-permute-start.9 = (f32[2,15,32,256]{3,2,1,0:T(8,128)}, f32[2,15,32,256]{3,2,1,0:T(8,128)}, u32[]{:S(2)}, u32[]{:S(2)}) collective-permute-start(f32[2,15,32,256]{3,2,1,0:T(8,128)} %get-tuple-element.28), channel_id=1, source_target_pairs={{1,0},{2,1},{3,2},{4,3},{5,4},{6,5},{7,6},{8,7},{9,8},{10,9},{11,1... | collective-permute-start | bytes 2949128 | tf_op jit(solution)/shard_map/ppermute | solution.py:19
  243.2 14.9 %all-to-all-start.4 = ((f32[4,4,32,256]{3,1,2,0:T(4,128)}), f32[4,4,32,256]{3,1,2,0:T(4,128)}, u32[]{:S(2)}, u32[]{:S(2)}) async-start(f32[4,4,32,256]{3,1,2,0:T(4,128)} %copy.318), calls=%async_computation.4 | async-start | bytes 1048576 | tf_op jit(solution)/shard_map/all_to_all | solution.py:31
  258.1 13.0 %all-to-all-start.6 = ((f32[4,4,32,256]{3,1,2,0:T(4,128)}), f32[4,4,32,256]{3,1,2,0:T(4,128)}, u32[]{:S(2)}, u32[]{:S(2)}) async-start(f32[4,4,32,256]{3,1,2,0:T(4,128)} %copy.326), calls=%async_computation.6 | async-start | bytes 1048576 | tf_op jit(solution)/shard_map/all_to_all | solution.py:31
  271.1 11.7 %all-to-all-start.8 = ((f32[4,4,32,256]{3,1,2,0:T(4,128)}), f32[4,4,32,256]{3,1,2,0:T(4,128)S(1)}, u32[]{:S(2)}, u32[]{:S(2)}) async-start(f32[4,4,32,256]{3,1,2,0:T(4,128)} %copy.334), calls=%async_computation.8 | async-start | bytes 1048576 | tf_op jit(solution)/shard_map/all_to_all | solution.py:31
  276.7 9.6 %copy-start.19 = (s32[8]{0:T(128)S(1)}, s32[8]{0:T(128)}, u32[]{:S(2)}) copy-start(s32[8]{0:T(128)} %param.13) | copy-start | bytes 100
  282.8 11.5 %all-to-all-start.2 = ((f32[4,4,32,256]{3,1,2,0:T(4,128)}), f32[4,4,32,256]{3,1,2,0:T(4,128)S(1)}, u32[]{:S(2)}, u32[]{:S(2)}) async-start(f32[4,4,32,256]{3,1,2,0:T(4,128)} %copy.310), calls=%async_computation.2 | async-start | bytes 1048576 | tf_op jit(solution)/shard_map/all_to_all | solution.py:31
  321.0 12.8 %all-to-all-start.7 = ((f32[4,4,32,256]{3,1,2,0:T(4,128)}), f32[4,4,32,256]{3,1,2,0:T(4,128)S(1)}, u32[]{:S(2)}, u32[]{:S(2)}) async-start(f32[4,4,32,256]{3,1,2,0:T(4,128)} %broadcast_in_dim.43), calls=%async_computation.7 | async-start | bytes 1048576 | tf_op jit(solution)/shard_map/all_to_all | solution.py:37
  325.8 26.2 %collective-permute-start.10 = (f32[15,32,256]{2,0,1:T(8,128)}, f32[15,32,256]{2,0,1:T(8,128)}, u32[]{:S(2)}, u32[]{:S(2)}) collective-permute-start(f32[15,32,256]{2,0,1:T(8,128)} %get-tuple-element.35), channel_id=1, source_target_pairs={{0,1},{1,2},{2,3},{3,4},{4,5},{5,6},{6,7},{7,8},{8,9},{9,10},{10,1... | collective-permute-start | bytes 1474568 | tf_op jit(solution)/shard_map/ppermute | solution.py:17
  327.7 30.0 %collective-permute-start.11 = (f32[15,32,256]{2,0,1:T(8,128)}, f32[15,32,256]{2,0,1:T(8,128)}, u32[]{:S(2)}, u32[]{:S(2)}) collective-permute-start(f32[15,32,256]{2,0,1:T(8,128)} %get-tuple-element.36), channel_id=1, source_target_pairs={{1,0},{2,1},{3,2},{4,3},{5,4},{6,5},{7,6},{8,7},{9,8},{10,9},{11,1... | collective-permute-start | bytes 1474568 | tf_op jit(solution)/shard_map/ppermute | solution.py:19
  333.8 36.1 %copy-start.4 = (f32[16,32,256]{2,0,1:T(8,128)}, f32[16,32,256]{2,0,1:T(8,128)S(1)}, u32[]{:S(2)}) copy-start(f32[16,32,256]{2,0,1:T(8,128)S(1)} %reshape.175) | copy-start | bytes 1572868
  334.7 16.9 %all-to-all-start.9 = ((f32[4,4,32,256]{3,1,2,0:T(4,128)}), f32[4,4,32,256]{3,1,2,0:T(4,128)S(1)}, u32[]{:S(2)}, u32[]{:S(2)}) async-start(f32[4,4,32,256]{3,1,2,0:T(4,128)} %broadcast_in_dim.44), calls=%async_computation.9 | async-start | bytes 1048576 | tf_op jit(solution)/shard_map/all_to_all | solution.py:37
  340.6 23.2 %collective-permute-start.14 = (f32[15,32,256]{2,0,1:T(8,128)}, f32[15,32,256]{2,0,1:T(8,128)}, u32[]{:S(2)}, u32[]{:S(2)}) collective-permute-start(f32[15,32,256]{2,0,1:T(8,128)} %get-tuple-element.37), channel_id=1, source_target_pairs={{0,1},{1,2},{2,3},{3,4},{4,5},{5,6},{6,7},{7,8},{8,9},{9,10},{10,1... | collective-permute-start | bytes 1474568 | tf_op jit(solution)/shard_map/ppermute | solution.py:17
  342.5 27.4 %collective-permute-start.15 = (f32[15,32,256]{2,0,1:T(8,128)}, f32[15,32,256]{2,0,1:T(8,128)}, u32[]{:S(2)}, u32[]{:S(2)}) collective-permute-start(f32[15,32,256]{2,0,1:T(8,128)} %get-tuple-element.38), channel_id=1, source_target_pairs={{1,0},{2,1},{3,2},{4,3},{5,4},{6,5},{7,6},{8,7},{9,8},{10,9},{11,1... | collective-permute-start | bytes 1474568 | tf_op jit(solution)/shard_map/ppermute | solution.py:19
  348.5 25.5 %copy-start.5 = (f32[16,32,256]{2,0,1:T(8,128)}, f32[16,32,256]{2,0,1:T(8,128)S(1)}, u32[]{:S(2)}) copy-start(f32[16,32,256]{2,0,1:T(8,128)S(1)} %reshape.177) | copy-start | bytes 1572868
  349.7 24.2 %collective-permute-start.18 = (f32[15,32,256]{2,0,1:T(8,128)}, f32[15,32,256]{2,0,1:T(8,128)}, u32[]{:S(2)}, u32[]{:S(2)}) collective-permute-start(f32[15,32,256]{2,0,1:T(8,128)} %get-tuple-element.39), channel_id=1, source_target_pairs={{0,1},{1,2},{2,3},{3,4},{4,5},{5,6},{6,7},{7,8},{8,9},{9,10},{10,1... | collective-permute-start | bytes 1474568 | tf_op jit(solution)/shard_map/ppermute | solution.py:17
  351.9 26.0 %copy-start.6 = (f32[16,32,256]{2,0,1:T(8,128)}, f32[16,32,256]{2,0,1:T(8,128)S(1)}, u32[]{:S(2)}) copy-start(f32[16,32,256]{2,0,1:T(8,128)S(1)} %reshape.179) | copy-start | bytes 1572868
  352.0 22.0 %collective-permute-start.19 = (f32[15,32,256]{2,0,1:T(8,128)}, f32[15,32,256]{2,0,1:T(8,128)S(1)}, u32[]{:S(2)}, u32[]{:S(2)}) collective-permute-start(f32[15,32,256]{2,0,1:T(8,128)} %get-tuple-element.40), channel_id=1, source_target_pairs={{1,0},{2,1},{3,2},{4,3},{5,4},{6,5},{7,6},{8,7},{9,8},{10,9},{11,1... | collective-permute-start | bytes 1474568 | tf_op jit(solution)/shard_map/ppermute | solution.py:19
  357.8 20.1 %collective-permute-start.22 = (f32[15,32,256]{2,0,1:T(8,128)S(1)}, f32[15,32,256]{2,0,1:T(8,128)S(1)}, u32[]{:S(2)}, u32[]{:S(2)}) collective-permute-start(f32[15,32,256]{2,0,1:T(8,128)S(1)} %get-tuple-element.41), channel_id=1, source_target_pairs={{0,1},{1,2},{2,3},{3,4},{4,5},{5,6},{6,7},{7,8},{8,9},{9,10},{10,1... | collective-permute-start | bytes 1474568 | tf_op jit(solution)/shard_map/ppermute | solution.py:17
  363.7 14.1 %collective-permute-start.23 = (f32[15,32,256]{2,0,1:T(8,128)S(1)}, f32[15,32,256]{2,0,1:T(8,128)S(1)}, u32[]{:S(2)}, u32[]{:S(2)}) collective-permute-start(f32[15,32,256]{2,0,1:T(8,128)S(1)} %get-tuple-element.42), channel_id=1, source_target_pairs={{1,0},{2,1},{3,2},{4,3},{5,4},{6,5},{7,6},{8,7},{9,8},{10,9},{11,1... | collective-permute-start | bytes 1474568 | tf_op jit(solution)/shard_map/ppermute | solution.py:19
  380.7 4.3 copy-start
  380.7 4.3 copy-start.15
  391.8 9.2 %copy-start.3 = (f32[2,16,32,256]{3,2,1,0:T(8,128)}, f32[2,16,32,256]{3,2,1,0:T(8,128)S(1)}, u32[]{:S(2)}) copy-start(f32[2,16,32,256]{3,2,1,0:T(8,128)S(1)} %fusion.171) | copy-start | bytes 3145732
  392.1 22.2 %collective-permute-start.26 = (f32[2,15,32,256]{3,2,1,0:T(8,128)S(1)}, f32[2,15,32,256]{3,2,1,0:T(8,128)S(1)}, u32[]{:S(2)}, u32[]{:S(2)}) collective-permute-start(f32[2,15,32,256]{3,2,1,0:T(8,128)S(1)} %get-tuple-element.21), channel_id=1, source_target_pairs={{0,1},{1,2},{2,3},{3,4},{4,5},{5,6},{6,7},{7,8},{8,9},{9,10},{10,1... | collective-permute-start | bytes 2949128 | tf_op jit(solution)/shard_map/ppermute | solution.py:17
  394.0 27.7 %collective-permute-start.27 = (f32[2,15,32,256]{3,2,1,0:T(8,128)S(1)}, f32[2,15,32,256]{3,2,1,0:T(8,128)S(1)}, u32[]{:S(2)}, u32[]{:S(2)}) collective-permute-start(f32[2,15,32,256]{3,2,1,0:T(8,128)S(1)} %get-tuple-element.22), channel_id=1, source_target_pairs={{1,0},{2,1},{3,2},{4,3},{5,4},{6,5},{7,6},{8,7},{9,8},{10,9},{11,1... | collective-permute-start | bytes 2949128 | tf_op jit(solution)/shard_map/ppermute | solution.py:19
  402.1 21.8 %collective-permute-start.28 = (f32[2,15,32,256]{3,2,1,0:T(8,128)S(1)}, f32[2,15,32,256]{3,2,1,0:T(8,128)S(1)}, u32[]{:S(2)}, u32[]{:S(2)}) collective-permute-start(f32[2,15,32,256]{3,2,1,0:T(8,128)S(1)} %get-tuple-element.23), channel_id=1, source_target_pairs={{0,1},{1,2},{2,3},{3,4},{4,5},{5,6},{6,7},{7,8},{8,9},{9,10},{10,1... | collective-permute-start | bytes 2949128 | tf_op jit(solution)/shard_map/ppermute | solution.py:17
  404.0 36.8 %collective-permute-start.29 = (f32[2,15,32,256]{3,2,1,0:T(8,128)}, f32[2,15,32,256]{3,2,1,0:T(8,128)}, u32[]{:S(2)}, u32[]{:S(2)}) collective-permute-start(f32[2,15,32,256]{3,2,1,0:T(8,128)} %get-tuple-element.24), channel_id=1, source_target_pairs={{1,0},{2,1},{3,2},{4,3},{5,4},{6,5},{7,6},{8,7},{9,8},{10,9},{11,1... | collective-permute-start | bytes 2949128 | tf_op jit(solution)/shard_map/ppermute | solution.py:19
  411.3 44.5 %collective-permute-start.30 = (f32[2,15,32,256]{3,2,1,0:T(8,128)}, f32[2,15,32,256]{3,2,1,0:T(8,128)}, u32[]{:S(2)}, u32[]{:S(2)}) collective-permute-start(f32[2,15,32,256]{3,2,1,0:T(8,128)} %get-tuple-element.25), channel_id=1, source_target_pairs={{0,1},{1,2},{2,3},{3,4},{4,5},{5,6},{6,7},{7,8},{8,9},{9,10},{10,1... | collective-permute-start | bytes 2949128 | tf_op jit(solution)/shard_map/ppermute | solution.py:17
  414.3 41.4 %collective-permute-start.31 = (f32[2,15,32,256]{3,2,1,0:T(8,128)}, f32[2,15,32,256]{3,2,1,0:T(8,128)}, u32[]{:S(2)}, u32[]{:S(2)}) collective-permute-start(f32[2,15,32,256]{3,2,1,0:T(8,128)} %get-tuple-element.26), channel_id=1, source_target_pairs={{1,0},{2,1},{3,2},{4,3},{5,4},{6,5},{7,6},{8,7},{9,8},{10,9},{11,1... | collective-permute-start | bytes 2949128 | tf_op jit(solution)/shard_map/ppermute | solution.py:19
  421.7 46.0 %collective-permute-start.24 = (f32[2,15,32,256]{3,2,1,0:T(8,128)}, f32[2,15,32,256]{3,2,1,0:T(8,128)}, u32[]{:S(2)}, u32[]{:S(2)}) collective-permute-start(f32[2,15,32,256]{3,2,1,0:T(8,128)} %get-tuple-element.19), channel_id=1, source_target_pairs={{0,1},{1,2},{2,3},{3,4},{4,5},{5,6},{6,7},{7,8},{8,9},{9,10},{10,1... | collective-permute-start | bytes 2949128 | tf_op jit(solution)/shard_map/ppermute | solution.py:17
  423.9 6.0 %copy-start.13 = (f32[2,15,32,256]{3,2,1,0:T(8,128)}, f32[2,15,32,256]{3,2,1,0:T(8,128)S(1)}, u32[]{:S(2)}) copy-start(f32[2,15,32,256]{3,2,1,0:T(8,128)S(1)} %collective-permute-done.28) | copy-start | bytes 2949124
  423.9 43.8 %collective-permute-start.25 = (f32[2,15,32,256]{3,2,1,0:T(8,128)}, f32[2,15,32,256]{3,2,1,0:T(8,128)}, u32[]{:S(2)}, u32[]{:S(2)}) collective-permute-start(f32[2,15,32,256]{3,2,1,0:T(8,128)} %get-tuple-element.20), channel_id=1, source_target_pairs={{1,0},{2,1},{3,2},{4,3},{5,4},{6,5},{7,6},{8,7},{9,8},{10,9},{11,1... | collective-permute-start | bytes 2949128 | tf_op jit(solution)/shard_map/ppermute | solution.py:19
  436.0 15.0 %all-to-all-start.12 = ((f32[4,4,32,256]{3,1,2,0:T(4,128)}), f32[4,4,32,256]{3,1,2,0:T(4,128)S(1)}, u32[]{:S(2)}, u32[]{:S(2)}) async-start(f32[4,4,32,256]{3,1,2,0:T(4,128)} %copy.349), calls=%async_computation.12 | async-start | bytes 1048576 | tf_op jit(solution)/shard_map/all_to_all | solution.py:31
  451.0 13.0 %all-to-all-start.14 = ((f32[4,4,32,256]{3,1,2,0:T(4,128)}), f32[4,4,32,256]{3,1,2,0:T(4,128)}, u32[]{:S(2)}, u32[]{:S(2)}) async-start(f32[4,4,32,256]{3,1,2,0:T(4,128)} %copy.354), calls=%async_computation.14 | async-start | bytes 1048576 | tf_op jit(solution)/shard_map/all_to_all | solution.py:31
  464.0 11.8 %all-to-all-start.16 = ((f32[4,4,32,256]{3,1,2,0:T(4,128)}), f32[4,4,32,256]{3,1,2,0:T(4,128)S(1)}, u32[]{:S(2)}, u32[]{:S(2)}) async-start(f32[4,4,32,256]{3,1,2,0:T(4,128)} %copy.359), calls=%async_computation.16 | async-start | bytes 1048576 | tf_op jit(solution)/shard_map/all_to_all | solution.py:31
  475.7 11.5 %all-to-all-start.10 = ((f32[4,4,32,256]{3,1,2,0:T(4,128)}), f32[4,4,32,256]{3,1,2,0:T(4,128)S(1)}, u32[]{:S(2)}, u32[]{:S(2)}) async-start(f32[4,4,32,256]{3,1,2,0:T(4,128)} %copy.344), calls=%async_computation.10 | async-start | bytes 1048576 | tf_op jit(solution)/shard_map/all_to_all | solution.py:31
  489.6 11.6 %all-to-all-start.11 = ((f32[4,4,32,256]{3,2,1,0:T(8,128)}), f32[4,4,32,256]{3,2,1,0:T(8,128)S(1)}, u32[]{:S(2)}, u32[]{:S(2)}) async-start(f32[4,4,32,256]{3,2,1,0:T(8,128)} %broadcast_in_dim.45), calls=%async_computation.11 | async-start | bytes 1048576 | tf_op jit(solution)/shard_map/all_to_all | solution.py:37
  502.1 12.8 %all-to-all-start.13 = ((f32[4,4,32,256]{3,2,1,0:T(8,128)}), f32[4,4,32,256]{3,2,1,0:T(8,128)S(1)}, u32[]{:S(2)}, u32[]{:S(2)}) async-start(f32[4,4,32,256]{3,2,1,0:T(8,128)} %broadcast_in_dim.46), calls=%async_computation.13 | async-start | bytes 1048576 | tf_op jit(solution)/shard_map/all_to_all | solution.py:37
  515.7 12.9 %all-to-all-start.15 = ((f32[4,4,32,256]{3,2,1,0:T(8,128)}), f32[4,4,32,256]{3,2,1,0:T(8,128)S(1)}, u32[]{:S(2)}, u32[]{:S(2)}) async-start(f32[4,4,32,256]{3,2,1,0:T(8,128)} %broadcast_in_dim.47), calls=%async_computation.15 | async-start | bytes 1048576 | tf_op jit(solution)/shard_map/all_to_all | solution.py:37
  (3 other events, 6.7 us)

commit v4 on v2

--- a/solution.py
+++ b/solution.py
@@ -132,7 +132,7 @@
     mat_y = banded_blur_matrix(point_spread_kernels[:, 1], ny_cells, ny_cells, reach, 1)
     mat_z = banded_blur_matrix(point_spread_kernels[:, 2], nz_cells, nz_cells, reach, 1)
     weights = view_weight[:, None, None, None]
-    chunk_count = 4
+    chunk_count = 2
     rows = ny_cells // chunk_count
 
     def forward_chunk(cells):

time: 450 us -> 456 us (1.013)
  the two profiles are of different devices: /device:TPU:64 before, /device:TPU:38 now
where the time goes in v4:
time: 456 us; the launch traced here: 453 us
  waiting for transfers between devices  189 us (41%)
  starting transfers between devices  104 us (23%)
  matrix products  80 us (18%)
  local copies, waits for them, and re-layouts  61.7 us (14%)
  other arithmetic  16.7 us (4%)
    ppermute x8, waiting for transfers between devices, with_halo(): lax.ppermute(tail, axis, [(i, (i + 1) % count) for i in range(ends)])  137 us
    ppermute x8, starting transfers between devices, with_halo(): lax.ppermute(head, axis, [((i + 1) % count, i) for i in range(ends)])  32.5 us
    ppermute x12, waiting for transfers between devices, view_sum_update(): lax.ppermute(updated, 'view', [(i, (i + shift) % count) for i in range(co...  26.7 us
    dot_general x4, matrix products, backward_chunk(): corrected = jnp.einsum('vwyz,vwx->vxyz', rimmed, adj_x, precision=highest)  26 us
    ppermute x12, starting transfers between devices, view_sum_update(): lax.ppermute(sent, 'view', [(i, (i + shift) % count) for i in range(count)])  22 us
    ppermute x12, starting transfers between devices, view_sum_update(): lax.ppermute(updated, 'view', [(i, (i + shift) % count) for i in range(co...  18.1 us
    ppermute x12, waiting for transfers between devices, view_sum_update(): lax.ppermute(sent, 'view', [(i, (i + shift) % count) for i in range(count)])  17.2 us
    ppermute x8, starting transfers between devices, with_halo(): lax.ppermute(tail, axis, [(i, (i + 1) % count) for i in range(ends)])  15.4 us
  transfers between devices with their start and end apart: 42, of which 24 were waited for; matrix products, arithmetic and copies ran while one was open for 23% of the time, Pallas kernels for 0%

profile of v4, /device:TPU:38, one launch (start us, length us, event | category | flops | bytes accessed | tf_op | source)
XLA Modules:
  0.0 452.8 jit_solution(4189570816403117465)
XLA Ops:
  3.6 8.0 %all-to-all-start = ((f32[32,1,1]{2,1,0:T(1,128)}), f32[32,1,1]{2,1,0:T(1,128)S(1)}, u32[]{:S(2)}, u32[]{:S(2)}) async-start(f32[32,1,1]{2,1,0:T(1,128)} %copy.154), calls=%async_computation | async-start | bytes 32768 | tf_op jit(solution)/shard_map/all_to_all | solution.py:107
  11.5 4.3 broadcast_in_dim.37
  15.8 7.9 %scatter_fusion = f32[32,2,128,256]{3,2,1,0:T(8,128)} fusion(f32[32,2,128,256]{3,2,1,0:T(8,128)} %broadcast_in_dim.37, s32[16]{0:T(128)S(1)} %fusion.109, f32[16,2,128,256]{3,2,1,0:T(8,128)} %bitcast.118), kind=kCustom, calls=%fused_computation.1 | custom fusion | bytes 12582976 | tf_op jit(solution)/shard_map/scatter | solution.py:92
  23.7 7.6 %all-to-all-start.1 = ((f32[32,1,2,128,256]{4,3,2,1,0:T(8,128)}), f32[32,1,2,128,256]{4,3,2,1,0:T(8,128)}, u32[]{:S(2)}, u32[]{:S(2)}) async-start(f32[32,1,2,128,256]{4,3,2,1,0:T(8,128)} %bitcast.115), calls=%async_computation.1 | async-start | bytes 16777216 | tf_op jit(solution)/shard_map/all_to_all | solution.py:100
  31.4 2.0 fusion.126
  35.4 3.5 collective-permute-start.1
  40.9 3.9 collective-permute-start.3
  47.9 2.0 fusion.83
  50.7 94.7 %collective-permute-done = f32[15,64,256]{2,1,0:T(8,128)} collective-permute-done((f32[15,64,256]{2,1,0:T(8,128)}, f32[15,64,256]{2,1,0:T(8,128)}, u32[]{:S(2)}, u32[]{:S(2)}) %collective-permute-start) | collective-permute-done | bytes 983072 | tf_op jit(solution)/shard_map/ppermute | solution.py:17
  149.0 7.0 %collective-permute-done.2 = f32[15,64,256]{2,1,0:T(8,128)} collective-permute-done((f32[15,64,256]{2,1,0:T(8,128)}, f32[15,64,256]{2,1,0:T(8,128)}, u32[]{:S(2)}, u32[]{:S(2)}) %collective-permute-start.2) | collective-permute-done | bytes 983072 | tf_op jit(solution)/shard_map/ppermute | solution.py:17
  159.5 2.2 fusion.28
  161.7 2.2 fusion.33
  163.9 3.4 fusion.68
  167.3 3.2 fusion.66
  170.5 5.6 %fusion.9 = f32[2,128,16,256]{3,1,2,0:T(8,128)} fusion(f32[2,128,128,1]{1,2,3,0:T(8,128)S(1)} %copy.201, f32[2,16,64,256]{3,2,1,0:T(8,128)S(1)} %fusion.66, f32[2,16,64,256]{3,2,1,0:T(8,128)S(1)} %fusion.68), kind=kOutput, calls=%fused_computation.17 | convolution fusion | flops 1611661312 | bytes 8519680 | tf_op jit(solution)/shard_map/vxyz,vyq->vxqz/dot_general | solution.py:156
  176.1 2.5 broadcast_in_dim.33
  178.6 14.0 %scatter_fusion.1 = f32[16,2,128,256]{3,2,1,0:T(8,128)} fusion(f32[16,2,128,256]{3,2,1,0:T(8,128)} %broadcast_in_dim.33, s32[32]{0:T(128)S(1)} %fusion.107, f32[32,2,128,256]{3,2,1,0:T(8,128)} %bitcast.15), kind=kCustom, calls=%fused_computation.2 | custom fusion | bytes 25165952 | tf_op jit(solution)/shard_map/scatter | solution.py:116
  192.6 6.8 %fusion.48 = f32[2,16,128,256]{3,2,1,0:T(8,128)S(1)} fusion(f32[2,128,16,256]{3,1,2,0:T(8,128)} %fusion.9, f32[2,16]{1,0:T(2,128)S(1)} %get-tuple-element.46, f32[2,16]{1,0:T(2,128)S(1)} %broadcast_in_dim_reshape.6, f32[2,128,128,1]{2,0,1,3:T(2,128)S(1)} %fusion.84, f32[2,16,128,256]{3,2,1,0:T(8,128)} %bitcast.116), kind=kOutput, calls=%fused_computation.60 | convolution fusion | flops 1613758464 | bytes 12714240 | tf_op jit(solution)/shard_map/vxyz,vqy->vxqz/dot_general | solution.py:158
  201.3 2.6 fusion.125
  205.8 3.6 collective-permute-start.15
  211.5 2.6 fusion.124
  216.0 3.8 collective-permute-start.5
  220.1 10.1 %collective-permute-done.14 = f32[2,15,64,256]{3,2,1,0:T(8,128)} collective-permute-done((f32[2,15,64,256]{3,2,1,0:T(8,128)}, f32[2,15,64,256]{3,2,1,0:T(8,128)}, u32[]{:S(2)}, u32[]{:S(2)}) %collective-permute-start.14) | collective-permute-done | bytes 1966112 | tf_op jit(solution)/shard_map/ppermute | solution.py:17
  231.9 3.5 pad_maximum_fusion.1
  235.4 6.5 %multiply_reduce_fusion.2 = f32[16,64,256]{2,0,1:T(8,128)S(1)} fusion(f32[2,46,64,256]{3,2,1,0:T(8,128)S(1)} %pad_maximum_fusion.1, f32[2,16]{1,0:T(2,128)S(1)} %get-tuple-element.45, f32[2,46,16,1]{1,0,2,3:T(2,128)S(1)} %convolution_bitcast_fusion.1), kind=kOutput, calls=%fused_computation.81 | convolution fusion | flops 290193408 | bytes 7083904 | tf_op jit(solution)/shard_map/vwyz,vwx->vxyz/dot_general | solution.py:146
  243.6 3.1 collective-permute-start.17
  247.9 3.3 collective-permute-done.4
  253.0 3.0 pad_maximum_fusion
  256.0 6.5 %multiply_reduce_fusion.3 = f32[16,64,256]{2,0,1:T(8,128)S(1)} fusion(f32[2,46,64,256]{3,2,1,0:T(8,128)S(1)} %pad_maximum_fusion, f32[2,16]{1,0:T(2,128)S(1)} %get-tuple-element.45, f32[2,46,16,1]{1,0,2,3:T(2,128)S(1)} %convolution_bitcast_fusion.1), kind=kOutput, calls=%fused_computation.82 | convolution fusion | flops 290193408 | bytes 7083904 | tf_op jit(solution)/shard_map/vwyz,vwx->vxyz/dot_general | solution.py:146
  265.8 3.1 collective-permute-start.7
  270.9 3.9 collective-permute-done.6
  274.8 2.8 collective-permute-done.7
  277.6 3.0 constant_dynamic-update-slice_fusion.14
  287.8 5.8 %collective-permute-done.9 = f32[4,64,256]{2,0,1:T(4,128)} collective-permute-done((f32[4,64,256]{2,0,1:T(4,128)}, f32[4,64,256]{2,0,1:T(4,128)}, u32[]{:S(2)}, u32[]{:S(2)}) %collective-permute-start.9) | collective-permute-done | bytes 262176 | tf_op jit(solution)/shard_map/ppermute | solution.py:43
  294.7 2.6 collective-permute-done.10
  301.2 3.6 collective-permute-start.13
  308.4 6.5 %collective-permute-start.23 = (f32[15,64,256]{2,1,0:T(8,128)S(1)}, f32[15,64,256]{2,1,0:T(8,128)S(1)}, u32[]{:S(2)}, u32[]{:S(2)}) collective-permute-start(f32[15,64,256]{2,1,0:T(8,128)S(1)} %copy.182), channel_id=1, source_target_pairs={{1,0},{2,1},{3,2},{4,3},{5,4},{6,5},{7,6},{8,7},{9,8},{10,9},{11,1... | collective-permute-start | bytes 2949128 | tf_op jit(solution)/shard_map/ppermute | solution.py:19
  317.0 7.6 %collective-permute-done.22 = f32[15,64,256]{2,1,0:T(8,128)S(1)} collective-permute-done((f32[15,64,256]{2,1,0:T(8,128)S(1)}, f32[15,64,256]{2,1,0:T(8,128)S(1)}, u32[]{:S(2)}, u32[]{:S(2)}) %collective-permute-start.22) | collective-permute-done | bytes 983072 | tf_op jit(solution)/shard_map/ppermute | solution.py:17
  325.2 2.2 fusion.38
  327.4 3.2 fusion.64
  331.2 2.2 fusion.43
  333.4 3.4 fusion.62
  336.9 4.0 fusion.13
  340.9 4.6 %fusion.51 = f32[2,16,128,256]{3,2,1,0:T(8,128)S(1)} fusion(f32[2,128,16,256]{3,1,2,0:T(8,128)S(1)} %fusion.13, f32[2,16]{1,0:T(2,128)S(1)} %get-tuple-element.46, f32[2,16]{1,0:T(2,128)S(1)} %broadcast_in_dim_reshape.6, f32[2,128,128,1]{2,0,1,3:T(2,128)S(1)} %fusion.84, f32[2,16,128,256]{3,2,1,0:T(8,128)S(1)} %bitcast.117), kind=kOutput, calls=%fused_computation.61 | convolution fusion | flops 1613758464 | bytes 12714240 | tf_op jit(solution)/shard_map/vxyz,vqy->vxqz/dot_general | solution.py:158
  349.8 3.9 collective-permute-start.33
  355.7 2.5 fusion.122
  360.0 3.6 collective-permute-start.25
  363.7 10.2 %collective-permute-done.32 = f32[2,15,64,256]{3,2,1,0:T(8,128)S(1)} collective-permute-done((f32[2,15,64,256]{3,2,1,0:T(8,128)S(1)}, f32[2,15,64,256]{3,2,1,0:T(8,128)S(1)}, u32[]{:S(2)}, u32[]{:S(2)}) %collective-permute-start.32) | collective-permute-done | bytes 1966112 | tf_op jit(solution)/shard_map/ppermute | solution.py:17
  375.6 2.5 pad_maximum_fusion.3
  378.1 6.5 %multiply_reduce_fusion = f32[16,64,256]{2,0,1:T(8,128)S(1)} fusion(f32[2,46,64,256]{3,2,1,0:T(8,128)S(1)} %pad_maximum_fusion.3, f32[2,16]{1,0:T(2,128)S(1)} %get-tuple-element.45, f32[2,46,16,1]{1,0,2,3:T(2,128)S(1)} %convolution_bitcast_fusion.1), kind=kOutput, calls=%fused_computation.79 | convolution fusion | flops 290193408 | bytes 7083904 | tf_op jit(solution)/shard_map/vwyz,vwx->vxyz/dot_general | solution.py:146
  386.7 3.4 collective-permute-start.35
  390.3 4.6 %collective-permute-done.24 = f32[2,15,64,256]{3,2,1,0:T(8,128)S(1)} collective-permute-done((f32[2,15,64,256]{3,2,1,0:T(8,128)}, f32[2,15,64,256]{3,2,1,0:T(8,128)S(1)}, u32[]{:S(2)}, u32[]{:S(2)}) %collective-permute-start.24) | collective-permute-done | bytes 1966112 | tf_op jit(solution)/shard_map/ppermute | solution.py:17
  397.6 6.5 %multiply_reduce_fusion.1 = f32[16,64,256]{2,0,1:T(8,128)S(1)} fusion(f32[2,46,64,256]{3,2,1,0:T(8,128)S(1)} %pad_maximum_fusion.2, f32[2,16]{1,0:T(2,128)S(1)} %get-tuple-element.45, f32[2,46,16,1]{1,0,2,3:T(2,128)S(1)} %convolution_bitcast_fusion.1), kind=kOutput, calls=%fused_computation.80 | convolution fusion | flops 290193408 | bytes 7083904 | tf_op jit(solution)/shard_map/vwyz,vwx->vxyz/dot_general | solution.py:146
  406.2 3.4 collective-permute-start.27
  409.6 2.9 collective-permute-done.26
  412.5 6.7 %collective-permute-done.27 = f32[4,64,256]{2,0,1:T(4,128)S(1)} collective-permute-done((f32[4,64,256]{2,0,1:T(4,128)S(1)}, f32[4,64,256]{2,0,1:T(4,128)S(1)}, u32[]{:S(2)}, u32[]{:S(2)}) %collective-permute-start.27) | collective-permute-done | bytes 262176 | tf_op jit(solution)/shard_map/ppermute | solution.py:37
  420.6 2.6 collective-permute-start.29
  423.2 2.7 collective-permute-start.30
  428.7 2.1 collective-permute-done.29
  430.9 2.7 collective-permute-start.39
  433.6 5.0 %collective-permute-done.30 = f32[4,64,256]{2,0,1:T(4,128)S(1)} collective-permute-done((f32[4,64,256]{2,0,1:T(4,128)S(1)}, f32[4,64,256]{2,0,1:T(4,128)S(1)}, u32[]{:S(2)}, u32[]{:S(2)}) %collective-permute-start.30) | collective-permute-done | bytes 262176 | tf_op jit(solution)/shard_map/ppermute | solution.py:43
  438.8 3.3 collective-permute-done.37
  442.2 7.4 %collective-permute-done.38 = f32[4,64,256]{2,0,1:T(4,128)S(1)} collective-permute-done((f32[4,64,256]{2,0,1:T(4,128)S(1)}, f32[4,64,256]{2,0,1:T(4,128)S(1)}, u32[]{:S(2)}, u32[]{:S(2)}) %collective-permute-start.38) | collective-permute-done | bytes 262176 | tf_op jit(solution)/shard_map/ppermute | solution.py:43
  449.9 2.5 copy.196
  (138 shorter events, 78.8 us)
Async XLA Ops:
  3.6 20.2 %all-to-all-start = ((f32[32,1,1]{2,1,0:T(1,128)}), f32[32,1,1]{2,1,0:T(1,128)S(1)}, u32[]{:S(2)}, u32[]{:S(2)}) async-start(f32[32,1,1]{2,1,0:T(1,128)} %copy.154), calls=%async_computation | async-start | bytes 32768 | tf_op jit(solution)/shard_map/all_to_all | solution.py:107
  23.7 7.6 %copy-start.4 = (f32[16,128,256]{2,1,0:T(8,128)S(1)}, f32[16,128,256]{2,1,0:T(8,128)}, u32[]{:S(2)}) copy-start(f32[16,128,256]{2,1,0:T(8,128)} %param.8) | copy-start | bytes 6291460
  23.7 152.4 %all-to-all-start.1 = ((f32[32,1,2,128,256]{4,3,2,1,0:T(8,128)}), f32[32,1,2,128,256]{4,3,2,1,0:T(8,128)}, u32[]{:S(2)}, u32[]{:S(2)}) async-start(f32[32,1,2,128,256]{4,3,2,1,0:T(8,128)} %bitcast.115), calls=%async_computation.1 | async-start | bytes 16777216 | tf_op jit(solution)/shard_map/all_to_all | solution.py:100
  31.3 13.4 %copy-start.8 = (f32[2,3,31]{2,0,1:T(2,128)S(1)}, f32[2,3,31]{2,0,1:T(2,128)}, u32[]{:S(2)}) copy-start(f32[2,3,31]{2,0,1:T(2,128)} %param.14) | copy-start | bytes 2236
  31.3 13.5 %copy-start.9 = (s32[2,2]{1,0:T(2,128)S(1)}, s32[2,2]{1,0:T(2,128)}, u32[]{:S(2)}) copy-start(s32[2,2]{1,0:T(2,128)} %param.12) | copy-start | bytes 52
  33.4 112.0 %collective-permute-start = (f32[15,64,256]{2,1,0:T(8,128)}, f32[15,64,256]{2,1,0:T(8,128)}, u32[]{:S(2)}, u32[]{:S(2)}) collective-permute-start(f32[15,64,256]{2,1,0:T(8,128)} %get-tuple-element.23), channel_id=1, source_target_pairs={{0,1},{1,2},{2,3},{3,4},{4,5},{5,6},{6,7},{7,8},{8,9},{9,10},{10,1... | collective-permute-start | bytes 2949128 | tf_op jit(solution)/shard_map/ppermute | solution.py:17
  35.4 111.7 %collective-permute-start.1 = (f32[15,64,256]{2,1,0:T(8,128)}, f32[15,64,256]{2,1,0:T(8,128)}, u32[]{:S(2)}, u32[]{:S(2)}) collective-permute-start(f32[15,64,256]{2,1,0:T(8,128)} %get-tuple-element.24), channel_id=1, source_target_pairs={{1,0},{2,1},{3,2},{4,3},{5,4},{6,5},{7,6},{8,7},{9,8},{10,9},{11,1... | collective-permute-start | bytes 2949128 | tf_op jit(solution)/shard_map/ppermute | solution.py:19
  39.0 116.9 %collective-permute-start.2 = (f32[15,64,256]{2,1,0:T(8,128)}, f32[15,64,256]{2,1,0:T(8,128)}, u32[]{:S(2)}, u32[]{:S(2)}) collective-permute-start(f32[15,64,256]{2,1,0:T(8,128)} %get-tuple-element.26), channel_id=1, source_target_pairs={{0,1},{1,2},{2,3},{3,4},{4,5},{5,6},{6,7},{7,8},{8,9},{9,10},{10,1... | collective-permute-start | bytes 2949128 | tf_op jit(solution)/shard_map/ppermute | solution.py:17
  40.9 116.8 %collective-permute-start.3 = (f32[15,64,256]{2,1,0:T(8,128)}, f32[15,64,256]{2,1,0:T(8,128)}, u32[]{:S(2)}, u32[]{:S(2)}) collective-permute-start(f32[15,64,256]{2,1,0:T(8,128)} %get-tuple-element.25), channel_id=1, source_target_pairs={{1,0},{2,1},{3,2},{4,3},{5,4},{6,5},{7,6},{8,7},{9,8},{10,9},{11,1... | collective-permute-start | bytes 2949128 | tf_op jit(solution)/shard_map/ppermute | solution.py:19
  45.4 2.5 copy-start.10
  201.3 2.6 copy-start.3
  203.9 26.3 %collective-permute-start.14 = (f32[2,15,64,256]{3,2,1,0:T(8,128)}, f32[2,15,64,256]{3,2,1,0:T(8,128)}, u32[]{:S(2)}, u32[]{:S(2)}) collective-permute-start(f32[2,15,64,256]{3,2,1,0:T(8,128)} %get-tuple-element.21), channel_id=1, source_target_pairs={{0,1},{1,2},{2,3},{3,4},{4,5},{5,6},{6,7},{7,8},{8,9},{9,10},{10,1... | collective-permute-start | bytes 5898248 | tf_op jit(solution)/shard_map/ppermute | solution.py:17
  205.8 26.1 %collective-permute-start.15 = (f32[2,15,64,256]{3,2,1,0:T(8,128)}, f32[2,15,64,256]{3,2,1,0:T(8,128)}, u32[]{:S(2)}, u32[]{:S(2)}) collective-permute-start(f32[2,15,64,256]{3,2,1,0:T(8,128)} %get-tuple-element.22), channel_id=1, source_target_pairs={{1,0},{2,1},{3,2},{4,3},{5,4},{6,5},{7,6},{8,7},{9,8},{10,9},{11,1... | collective-permute-start | bytes 5898248 | tf_op jit(solution)/shard_map/ppermute | solution.py:19
  211.5 2.6 copy-start.1
  214.1 37.1 %collective-permute-start.4 = (f32[2,15,64,256]{3,2,1,0:T(8,128)}, f32[2,15,64,256]{3,2,1,0:T(8,128)}, u32[]{:S(2)}, u32[]{:S(2)}) collective-permute-start(f32[2,15,64,256]{3,2,1,0:T(8,128)} %get-tuple-element.19), channel_id=1, source_target_pairs={{0,1},{1,2},{2,3},{3,4},{4,5},{5,6},{6,7},{7,8},{8,9},{9,10},{10,1... | collective-permute-start | bytes 5898248 | tf_op jit(solution)/shard_map/ppermute | solution.py:17
  216.0 37.0 %collective-permute-start.5 = (f32[2,15,64,256]{3,2,1,0:T(8,128)}, f32[2,15,64,256]{3,2,1,0:T(8,128)}, u32[]{:S(2)}, u32[]{:S(2)}) collective-permute-start(f32[2,15,64,256]{3,2,1,0:T(8,128)} %get-tuple-element.20), channel_id=1, source_target_pairs={{1,0},{2,1},{3,2},{4,3},{5,4},{6,5},{7,6},{8,7},{9,8},{10,9},{11,1... | collective-permute-start | bytes 5898248 | tf_op jit(solution)/shard_map/ppermute | solution.py:19
  235.4 17.6 %copy-start.2 = (f32[2,16,64,256]{3,2,1,0:T(8,128)S(1)}, f32[2,16,64,256]{3,2,1,0:T(8,128)}, u32[]{:S(2)}) copy-start(f32[2,16,64,256]{3,2,1,0:T(8,128)} %copy-done.1) | copy-start | bytes 6291460
  241.9 9.3 %copy-start.5 = (f32[16,64,256]{2,0,1:T(8,128)}, f32[16,64,256]{2,0,1:T(8,128)S(1)}, u32[]{:S(2)}) copy-start(f32[16,64,256]{2,0,1:T(8,128)S(1)} %multiply_reduce_fusion.2) | copy-start | bytes 3145732
  242.2 26.8 %collective-permute-start.16 = (f32[4,64,256]{2,0,1:T(4,128)S(1)}, f32[4,64,256]{2,0,1:T(4,128)S(1)}, u32[]{:S(2)}, u32[]{:S(2)}) collective-permute-start(f32[4,64,256]{2,0,1:T(4,128)S(1)} %get-tuple-element.42), channel_id=1, source_target_pairs={{0,32},{32,64},{64,96},{96,0},{1,33},{33,65},{65,97},{97,1},{2,34}... | collective-permute-start | bytes 786440 | tf_op jit(solution)/shard_map/ppermute | solution.py:37
  243.6 27.3 %collective-permute-start.17 = (f32[4,64,256]{2,0,1:T(4,128)S(1)}, f32[4,64,256]{2,0,1:T(4,128)}, u32[]{:S(2)}, u32[]{:S(2)}) collective-permute-start(f32[4,64,256]{2,0,1:T(4,128)S(1)} %get-tuple-element.44), channel_id=1, source_target_pairs={{0,64},{32,96},{64,0},{96,32},{1,65},{33,97},{65,1},{97,33},{2,66}... | collective-permute-start | bytes 786440 | tf_op jit(solution)/shard_map/ppermute | solution.py:37
  246.7 24.2 %collective-permute-start.18 = (f32[4,64,256]{2,0,1:T(4,128)S(1)}, f32[4,64,256]{2,0,1:T(4,128)}, u32[]{:S(2)}, u32[]{:S(2)}) collective-permute-start(f32[4,64,256]{2,0,1:T(4,128)S(1)} %get-tuple-element.43), channel_id=1, source_target_pairs={{0,96},{32,0},{64,32},{96,64},{1,97},{33,1},{65,33},{97,65},{2,98}... | collective-permute-start | bytes 786440 | tf_op jit(solution)/shard_map/ppermute | solution.py:37
  256.0 14.7 %copy-start.11 = (s32[8]{0:T(128)S(1)}, s32[8]{0:T(128)}, u32[]{:S(2)}) copy-start(s32[8]{0:T(128)} %param.13) | copy-start | bytes 100
  262.5 1.0 copy-start.6
  264.5 10.3 %collective-permute-start.6 = (f32[4,64,256]{2,0,1:T(4,128)}, f32[4,64,256]{2,0,1:T(4,128)}, u32[]{:S(2)}, u32[]{:S(2)}) collective-permute-start(f32[4,64,256]{2,0,1:T(4,128)} %get-tuple-element.37), channel_id=1, source_target_pairs={{0,32},{32,64},{64,96},{96,0},{1,33},{33,65},{65,97},{97,1},{2,34}... | collective-permute-start | bytes 786440 | tf_op jit(solution)/shard_map/ppermute | solution.py:37
  265.8 11.8 %collective-permute-start.7 = (f32[4,64,256]{2,0,1:T(4,128)}, f32[4,64,256]{2,0,1:T(4,128)}, u32[]{:S(2)}, u32[]{:S(2)}) collective-permute-start(f32[4,64,256]{2,0,1:T(4,128)} %get-tuple-element.39), channel_id=1, source_target_pairs={{0,64},{32,96},{64,0},{96,32},{1,65},{33,97},{65,1},{97,33},{2,66}... | collective-permute-start | bytes 786440 | tf_op jit(solution)/shard_map/ppermute | solution.py:37
  269.0 0.7 copy-start.7
  269.7 8.0 %collective-permute-start.8 = (f32[4,64,256]{2,0,1:T(4,128)}, f32[4,64,256]{2,0,1:T(4,128)}, u32[]{:S(2)}, u32[]{:S(2)}) collective-permute-start(f32[4,64,256]{2,0,1:T(4,128)} %get-tuple-element.38), channel_id=1, source_target_pairs={{0,96},{32,0},{64,32},{96,64},{1,97},{33,1},{65,33},{97,65},{2,98}... | collective-permute-start | bytes 786440 | tf_op jit(solution)/shard_map/ppermute | solution.py:37
  280.6 13.0 %collective-permute-start.9 = (f32[4,64,256]{2,0,1:T(4,128)}, f32[4,64,256]{2,0,1:T(4,128)}, u32[]{:S(2)}, u32[]{:S(2)}) collective-permute-start(f32[4,64,256]{2,0,1:T(4,128)} %get-tuple-element.12), channel_id=1, source_target_pairs={{0,32},{32,64},{64,96},{96,0},{1,33},{33,65},{65,97},{97,1},{2,34}... | collective-permute-start | bytes 786440 | tf_op jit(solution)/shard_map/ppermute | solution.py:43
  282.3 15.0 %collective-permute-start.10 = (f32[4,64,256]{2,0,1:T(4,128)}, f32[4,64,256]{2,0,1:T(4,128)S(1)}, u32[]{:S(2)}, u32[]{:S(2)}) collective-permute-start(f32[4,64,256]{2,0,1:T(4,128)} %get-tuple-element.12), channel_id=1, source_target_pairs={{0,64},{32,96},{64,0},{96,32},{1,65},{33,97},{65,1},{97,33},{2,66}... | collective-permute-start | bytes 786440 | tf_op jit(solution)/shard_map/ppermute | solution.py:43
  284.2 13.7 %collective-permute-start.11 = (f32[4,64,256]{2,0,1:T(4,128)}, f32[4,64,256]{2,0,1:T(4,128)S(1)}, u32[]{:S(2)}, u32[]{:S(2)}) collective-permute-start(f32[4,64,256]{2,0,1:T(4,128)} %get-tuple-element.12), channel_id=1, source_target_pairs={{0,96},{32,0},{64,32},{96,64},{1,97},{33,1},{65,33},{97,65},{2,98}... | collective-permute-start | bytes 786440 | tf_op jit(solution)/shard_map/ppermute | solution.py:43
  285.7 19.2 %collective-permute-start.19 = (f32[4,64,256]{2,0,1:T(4,128)}, f32[4,64,256]{2,0,1:T(4,128)S(1)}, u32[]{:S(2)}, u32[]{:S(2)}) collective-permute-start(f32[4,64,256]{2,0,1:T(4,128)} %get-tuple-element.50), channel_id=1, source_target_pairs={{0,32},{32,64},{64,96},{96,0},{1,33},{33,65},{65,97},{97,1},{2,34}... | collective-permute-start | bytes 786440 | tf_op jit(solution)/shard_map/ppermute | solution.py:43
  286.2 18.7 %collective-permute-start.20 = (f32[4,64,256]{2,0,1:T(4,128)}, f32[4,64,256]{2,0,1:T(4,128)S(1)}, u32[]{:S(2)}, u32[]{:S(2)}) collective-permute-start(f32[4,64,256]{2,0,1:T(4,128)} %get-tuple-element.50), channel_id=1, source_target_pairs={{0,64},{32,96},{64,0},{96,32},{1,65},{33,97},{65,1},{97,33},{2,66}... | collective-permute-start | bytes 786440 | tf_op jit(solution)/shard_map/ppermute | solution.py:43
  293.6 11.4 %collective-permute-start.21 = (f32[4,64,256]{2,0,1:T(4,128)}, f32[4,64,256]{2,0,1:T(4,128)S(1)}, u32[]{:S(2)}, u32[]{:S(2)}) collective-permute-start(f32[4,64,256]{2,0,1:T(4,128)} %get-tuple-element.50), channel_id=1, source_target_pairs={{0,96},{32,0},{64,32},{96,64},{1,97},{33,1},{65,33},{97,65},{2,98}... | collective-permute-start | bytes 786440 | tf_op jit(solution)/shard_map/ppermute | solution.py:43
  298.7 16.2 %collective-permute-start.12 = (f32[15,64,256]{2,1,0:T(8,128)S(1)}, f32[15,64,256]{2,1,0:T(8,128)S(1)}, u32[]{:S(2)}, u32[]{:S(2)}) collective-permute-start(f32[15,64,256]{2,1,0:T(8,128)S(1)} %copy.171), channel_id=1, source_target_pairs={{0,1},{1,2},{2,3},{3,4},{4,5},{5,6},{6,7},{7,8},{8,9},{9,10},{10,1... | collective-permute-start | bytes 2949128 | tf_op jit(solution)/shard_map/ppermute | solution.py:17
  301.2 15.2 %collective-permute-start.13 = (f32[15,64,256]{2,1,0:T(8,128)S(1)}, f32[15,64,256]{2,1,0:T(8,128)S(1)}, u32[]{:S(2)}, u32[]{:S(2)}) collective-permute-start(f32[15,64,256]{2,1,0:T(8,128)S(1)} %copy.172), channel_id=1, source_target_pairs={{1,0},{2,1},{3,2},{4,3},{5,4},{6,5},{7,6},{8,7},{9,8},{10,9},{11,1... | collective-permute-start | bytes 2949128 | tf_op jit(solution)/shard_map/ppermute | solution.py:19
  305.9 18.8 %collective-permute-start.22 = (f32[15,64,256]{2,1,0:T(8,128)S(1)}, f32[15,64,256]{2,1,0:T(8,128)S(1)}, u32[]{:S(2)}, u32[]{:S(2)}) collective-permute-start(f32[15,64,256]{2,1,0:T(8,128)S(1)} %copy.181), channel_id=1, source_target_pairs={{0,1},{1,2},{2,3},{3,4},{4,5},{5,6},{6,7},{7,8},{8,9},{9,10},{10,1... | collective-permute-start | bytes 2949128 | tf_op jit(solution)/shard_map/ppermute | solution.py:17
  308.4 22.2 %collective-permute-start.23 = (f32[15,64,256]{2,1,0:T(8,128)S(1)}, f32[15,64,256]{2,1,0:T(8,128)S(1)}, u32[]{:S(2)}, u32[]{:S(2)}) collective-permute-start(f32[15,64,256]{2,1,0:T(8,128)S(1)} %copy.182), channel_id=1, source_target_pairs={{1,0},{2,1},{3,2},{4,3},{5,4},{6,5},{7,6},{8,7},{9,8},{10,9},{11,1... | collective-permute-start | bytes 2949128 | tf_op jit(solution)/shard_map/ppermute | solution.py:19
  336.9 4.0 copy-start
  347.9 25.9 %collective-permute-start.32 = (f32[2,15,64,256]{3,2,1,0:T(8,128)S(1)}, f32[2,15,64,256]{3,2,1,0:T(8,128)S(1)}, u32[]{:S(2)}, u32[]{:S(2)}) collective-permute-start(f32[2,15,64,256]{3,2,1,0:T(8,128)S(1)} %get-tuple-element.17), channel_id=1, source_target_pairs={{0,1},{1,2},{2,3},{3,4},{4,5},{5,6},{6,7},{7,8},{8,9},{9,10},{10,1... | collective-permute-start | bytes 5898248 | tf_op jit(solution)/shard_map/ppermute | solution.py:17
  349.8 25.8 %collective-permute-start.33 = (f32[2,15,64,256]{3,2,1,0:T(8,128)S(1)}, f32[2,15,64,256]{3,2,1,0:T(8,128)}, u32[]{:S(2)}, u32[]{:S(2)}) collective-permute-start(f32[2,15,64,256]{3,2,1,0:T(8,128)S(1)} %get-tuple-element.18), channel_id=1, source_target_pairs={{1,0},{2,1},{3,2},{4,3},{5,4},{6,5},{7,6},{8,7},{9,8},{10,9},{11,1... | collective-permute-start | bytes 5898248 | tf_op jit(solution)/shard_map/ppermute | solution.py:19
  358.1 36.8 %collective-permute-start.24 = (f32[2,15,64,256]{3,2,1,0:T(8,128)}, f32[2,15,64,256]{3,2,1,0:T(8,128)S(1)}, u32[]{:S(2)}, u32[]{:S(2)}) collective-permute-start(f32[2,15,64,256]{3,2,1,0:T(8,128)} %get-tuple-element.15), channel_id=1, source_target_pairs={{0,1},{1,2},{2,3},{3,4},{4,5},{5,6},{6,7},{7,8},{8,9},{9,10},{10,1... | collective-permute-start | bytes 5898248 | tf_op jit(solution)/shard_map/ppermute | solution.py:17
  360.0 36.8 %collective-permute-start.25 = (f32[2,15,64,256]{3,2,1,0:T(8,128)}, f32[2,15,64,256]{3,2,1,0:T(8,128)S(1)}, u32[]{:S(2)}, u32[]{:S(2)}) collective-permute-start(f32[2,15,64,256]{3,2,1,0:T(8,128)} %get-tuple-element.16), channel_id=1, source_target_pairs={{1,0},{2,1},{3,2},{4,3},{5,4},{6,5},{7,6},{8,7},{9,8},{10,9},{11,1... | collective-permute-start | bytes 5898248 | tf_op jit(solution)/shard_map/ppermute | solution.py:19
  384.8 24.7 %collective-permute-start.34 = (f32[4,64,256]{2,0,1:T(4,128)S(1)}, f32[4,64,256]{2,0,1:T(4,128)S(1)}, u32[]{:S(2)}, u32[]{:S(2)}) collective-permute-start(f32[4,64,256]{2,0,1:T(4,128)S(1)} %get-tuple-element.32), channel_id=1, source_target_pairs={{0,32},{32,64},{64,96},{96,0},{1,33},{33,65},{65,97},{97,1},{2,34}... | collective-permute-start | bytes 786440 | tf_op jit(solution)/shard_map/ppermute | solution.py:37
  386.7 22.9 %collective-permute-start.35 = (f32[4,64,256]{2,0,1:T(4,128)S(1)}, f32[4,64,256]{2,0,1:T(4,128)S(1)}, u32[]{:S(2)}, u32[]{:S(2)}) collective-permute-start(f32[4,64,256]{2,0,1:T(4,128)S(1)} %get-tuple-element.34), channel_id=1, source_target_pairs={{0,64},{32,96},{64,0},{96,32},{1,65},{33,97},{65,1},{97,33},{2,66}... | collective-permute-start | bytes 786440 | tf_op jit(solution)/shard_map/ppermute | solution.py:37
  390.1 19.5 %collective-permute-start.36 = (f32[4,64,256]{2,0,1:T(4,128)S(1)}, f32[4,64,256]{2,0,1:T(4,128)S(1)}, u32[]{:S(2)}, u32[]{:S(2)}) collective-permute-start(f32[4,64,256]{2,0,1:T(4,128)S(1)} %get-tuple-element.33), channel_id=1, source_target_pairs={{0,96},{32,0},{64,32},{96,64},{1,97},{33,1},{65,33},{97,65},{2,98}... | collective-permute-start | bytes 786440 | tf_op jit(solution)/shard_map/ppermute | solution.py:37
  404.3 8.2 %collective-permute-start.26 = (f32[4,64,256]{2,0,1:T(4,128)S(1)}, f32[4,64,256]{2,0,1:T(4,128)S(1)}, u32[]{:S(2)}, u32[]{:S(2)}) collective-permute-start(f32[4,64,256]{2,0,1:T(4,128)S(1)} %get-tuple-element.29), channel_id=1, source_target_pairs={{0,32},{32,64},{64,96},{96,0},{1,33},{33,65},{65,97},{97,1},{2,34}... | collective-permute-start | bytes 786440 | tf_op jit(solution)/shard_map/ppermute | solution.py:37
  406.2 13.0 %collective-permute-start.27 = (f32[4,64,256]{2,0,1:T(4,128)S(1)}, f32[4,64,256]{2,0,1:T(4,128)S(1)}, u32[]{:S(2)}, u32[]{:S(2)}) collective-permute-start(f32[4,64,256]{2,0,1:T(4,128)S(1)} %get-tuple-element.31), channel_id=1, source_target_pairs={{0,64},{32,96},{64,0},{96,32},{1,65},{33,97},{65,1},{97,33},{2,66}... | collective-permute-start | bytes 786440 | tf_op jit(solution)/shard_map/ppermute | solution.py:37
  409.6 10.5 %collective-permute-start.28 = (f32[4,64,256]{2,0,1:T(4,128)S(1)}, f32[4,64,256]{2,0,1:T(4,128)S(1)}, u32[]{:S(2)}, u32[]{:S(2)}) collective-permute-start(f32[4,64,256]{2,0,1:T(4,128)S(1)} %get-tuple-element.30), channel_id=1, source_target_pairs={{0,96},{32,0},{64,32},{96,64},{1,97},{33,1},{65,33},{97,65},{2,98}... | collective-permute-start | bytes 786440 | tf_op jit(solution)/shard_map/ppermute | solution.py:37
  420.6 10.2 %collective-permute-start.29 = (f32[4,64,256]{2,0,1:T(4,128)S(1)}, f32[4,64,256]{2,0,1:T(4,128)S(1)}, u32[]{:S(2)}, u32[]{:S(2)}) collective-permute-start(f32[4,64,256]{2,0,1:T(4,128)S(1)} %get-tuple-element.8), channel_id=1, source_target_pairs={{0,32},{32,64},{64,96},{96,0},{1,33},{33,65},{65,97},{97,1},{2,34}... | collective-permute-start | bytes 786440 | tf_op jit(solution)/shard_map/ppermute | solution.py:43
  423.2 15.5 %collective-permute-start.30 = (f32[4,64,256]{2,0,1:T(4,128)S(1)}, f32[4,64,256]{2,0,1:T(4,128)S(1)}, u32[]{:S(2)}, u32[]{:S(2)}) collective-permute-start(f32[4,64,256]{2,0,1:T(4,128)S(1)} %get-tuple-element.8), channel_id=1, source_target_pairs={{0,64},{32,96},{64,0},{96,32},{1,65},{33,97},{65,1},{97,33},{2,66}... | collective-permute-start | bytes 786440 | tf_op jit(solution)/shard_map/ppermute | solution.py:43
  425.8 12.9 %collective-permute-start.31 = (f32[4,64,256]{2,0,1:T(4,128)S(1)}, f32[4,64,256]{2,0,1:T(4,128)S(1)}, u32[]{:S(2)}, u32[]{:S(2)}) collective-permute-start(f32[4,64,256]{2,0,1:T(4,128)S(1)} %get-tuple-element.8), channel_id=1, source_target_pairs={{0,96},{32,0},{64,32},{96,64},{1,97},{33,1},{65,33},{97,65},{2,98}... | collective-permute-start | bytes 786440 | tf_op jit(solution)/shard_map/ppermute | solution.py:43
  425.9 16.1 %collective-permute-start.37 = (f32[4,64,256]{2,0,1:T(4,128)S(1)}, f32[4,64,256]{2,0,1:T(4,128)S(1)}, u32[]{:S(2)}, u32[]{:S(2)}) collective-permute-start(f32[4,64,256]{2,0,1:T(4,128)S(1)} %get-tuple-element.48), channel_id=1, source_target_pairs={{0,32},{32,64},{64,96},{96,0},{1,33},{33,65},{65,97},{97,1},{2,34}... | collective-permute-start | bytes 786440 | tf_op jit(solution)/shard_map/ppermute | solution.py:43
  427.9 21.7 %collective-permute-start.38 = (f32[4,64,256]{2,0,1:T(4,128)S(1)}, f32[4,64,256]{2,0,1:T(4,128)S(1)}, u32[]{:S(2)}, u32[]{:S(2)}) collective-permute-start(f32[4,64,256]{2,0,1:T(4,128)S(1)} %get-tuple-element.48), channel_id=1, source_target_pairs={{0,64},{32,96},{64,0},{96,32},{1,65},{33,97},{65,1},{97,33},{2,66}... | collective-permute-start | bytes 786440 | tf_op jit(solution)/shard_map/ppermute | solution.py:43
  430.9 18.7 %collective-permute-start.39 = (f32[4,64,256]{2,0,1:T(4,128)S(1)}, f32[4,64,256]{2,0,1:T(4,128)S(1)}, u32[]{:S(2)}, u32[]{:S(2)}) collective-permute-start(f32[4,64,256]{2,0,1:T(4,128)S(1)} %get-tuple-element.48), channel_id=1, source_target_pairs={{0,96},{32,0},{64,32},{96,64},{1,97},{33,1},{65,33},{97,65},{2,98}... | collective-permute-start | bytes 786440 | tf_op jit(solution)/shard_map/ppermute | solution.py:43

commit v5 on v2

--- a/solution.py
+++ b/solution.py
@@ -74,47 +74,36 @@
     nz_cells = observed.shape[4]
     per_group = view_span.shape[0]
     per_block = view_count.shape[0]
-    capacity = max(1, slot_count // blocks)
     block_x = per_block * planes
     reach = psf_taps.shape[-1] // 2
     sources = observed[0]
     dest_list = route_dest[0]
     pos_list = route_pos[0]
-    slot_index = jnp.arange(slot_count, dtype=jnp.int32)
-    earlier = (dest_list[:, None] == dest_list[None, :]) & (
-        slot_index[None, :] < slot_index[:, None]
+    block_ids = jnp.arange(blocks, dtype=jnp.int32)
+    sends = dest_list[None, :] == block_ids[:, None]
+    has_slot = jnp.any(sends, axis=1)
+    slot_of = jnp.argmax(sends, axis=1)
+    outgoing = jnp.where(
+        has_slot[:, None, None, None], jnp.take(sources, slot_of, axis=0), 0.0
     )
-    rank_in_dest = jnp.sum(earlier.astype(jnp.int32), axis=1)
-    target = jnp.where(dest_list >= 0, dest_list * capacity + rank_in_dest, blocks * capacity)
-    outgoing = (
-        jnp.zeros((blocks * capacity, planes, ny_cells, nz_cells), jnp.float32)
-        .at[target]
-        .set(sources, mode="drop")
-    )
-    out_pos = (
-        jnp.full((blocks * capacity,), -1.0, jnp.float32)
-        .at[target]
-        .set(pos_list.astype(jnp.float32), mode="drop")
-    )
+    out_pos = jnp.where(has_slot, jnp.take(pos_list, slot_of).astype(jnp.float32), -1.0)
     arrived, arrived_pos = (
         lax.all_to_all(
-            outgoing.reshape(blocks, capacity, planes, ny_cells, nz_cells),
+            outgoing.reshape(blocks, 1, planes, ny_cells, nz_cells),
             "block",
             split_axis=0,
             concat_axis=0,
             tiled=True,
         ),
-        lax.all_to_all(
-            out_pos.reshape(blocks, capacity), "block", split_axis=0, concat_axis=0, tiled=True
-        ),
+        lax.all_to_all(out_pos.reshape(blocks, 1), "block", split_axis=0, concat_axis=0, tiled=True),
     )
+    arrived = arrived.reshape(blocks, planes, ny_cells, nz_cells)
     places = arrived_pos.reshape(-1).astype(jnp.int32)
-    places = jnp.where(places >= 0, places, per_group * per_block)
-    placed = (
-        jnp.zeros((per_group * per_block, planes, ny_cells, nz_cells), jnp.float32)
-        .at[places]
-        .set(arrived.reshape(-1, planes, ny_cells, nz_cells), mode="drop")
-    )
+    position_ids = jnp.arange(per_group * per_block, dtype=jnp.int32)
+    holds = places[None, :] == position_ids[:, None]
+    found = jnp.any(holds, axis=1)
+    source_of = jnp.argmax(holds, axis=1)
+    placed = jnp.where(found[:, None, None, None], jnp.take(arrived, source_of, axis=0), 0.0)
     obs_views = placed.reshape(per_group, block_x, ny_cells, nz_cells)
     brick_index = lax.axis_index("block") * per_block + jnp.arange(per_block, dtype=jnp.int32)
     span_first = view_span[:, 0:1]

time: 450 us -> 440 us (0.978)
  local copies, waits for them, and re-layouts: 54 us -> 32.3 us
  other arithmetic: 7.81 us -> 17.1 us
    scatter x3 -> x0, local copies, waits for them, and re-layouts: 21.9 us -> none  [the longest x1 13.6 us: on_device(): placed = jnp.zeros((per_group * per_block, planes, ny_cells, nz_cells), j...]
    gather x0 -> x3, local copies, waits for them, and re-layouts: none -> 13.5 us  [the longest x1 6.55 us: on_device(): jnp.take(sources, slot_of, axis=0)]
    select_n x2 -> x4, other arithmetic: 0.67 us -> 8.65 us  [the longest x1 8.63 us: on_device(): jnp.where(has_slot[:, None, None, None], jnp.take(sources, slot_of, axis=...]
    broadcast_in_dim x2 -> x6, local copies, waits for them, and re-layouts: 6.88 us -> 0.51 us  [the longest x3 0.25 us: on_device(): jnp.take(arrived, source_of, axis=0)]
    unnamed x26 -> x30, local copies, waits for them, and re-layouts: 15.2 us -> 9.4 us
    ppermute x16, waiting for transfers between devices: 57.2 us -> 62.5 us  [with_halo(): lax.ppermute(tail, axis, [(i, (i + 1) % count) for i in range(ends)])]
  transfers between devices with their start and end apart: 82 -> 82, of which waited for: 20 -> 17; matrix products, arithmetic and copies ran while one was open for 23% -> 23% of each run, Pallas kernels for 0% -> 0%
where the time goes in v5:
time: 440 us; the launch traced here: 434 us
  starting transfers between devices  213 us (48%)
  matrix products  85.3 us (19%)
  waiting for transfers between devices  84.4 us (19%)
  local copies, waits for them, and re-layouts  32.3 us (7%)
  other arithmetic  17.1 us (4%)
    ppermute x16, starting transfers between devices, with_halo(): lax.ppermute(head, axis, [((i + 1) % count, i) for i in range(ends)])  94.3 us
    ppermute x16, waiting for transfers between devices, with_halo(): lax.ppermute(tail, axis, [(i, (i + 1) % count) for i in range(ends)])  62.5 us
    ppermute x24, starting transfers between devices, view_sum_update(): lax.ppermute(updated, 'view', [(i, (i + shift) % count) for i in range(co...  35.7 us
    ppermute x16, starting transfers between devices, with_halo(): lax.ppermute(tail, axis, [(i, (i + 1) % count) for i in range(ends)])  34.9 us
    ppermute x24, starting transfers between devices, view_sum_update(): lax.ppermute(sent, 'view', [(i, (i + shift) % count) for i in range(count)])  32.8 us
    dot_general x8, matrix products, backward_chunk(): corrected = jnp.einsum('vwyz,vwx->vxyz', rimmed, adj_x, precision=highest)  26.4 us
    dot_general x8, matrix products, forward_chunk(): return jnp.einsum('vxyz,vzq->vxyq', along_x, mat_z, precision=highest)  13.5 us
    dot_general x8, matrix products, forward_chunk(): along_x = jnp.einsum('wyz,vwx->vxyz', padded, fwd_x, precision=highest)  12.5 us
  transfers between devices with their start and end apart: 82, of which 17 were waited for; matrix products, arithmetic and copies ran while one was open for 23% of the time, Pallas kernels for 0%

profile of v5, /device:TPU:64, one launch (start us, length us, event | category | flops | bytes accessed | tf_op | source)
XLA Modules:
  0.0 433.9 jit_solution(1577673134612414401)
XLA Ops:
  3.5 7.6 %all-to-all-start = ((f32[32,1,1]{2,1,0:T(1,128)}), f32[32,1,1]{2,1,0:T(1,128)S(1)}, u32[]{:S(2)}, u32[]{:S(2)}) async-start(f32[32,1,1]{2,1,0:T(1,128)} %copy.194), calls=%async_computation | async-start | bytes 32768 | tf_op jit(solution)/shard_map/all_to_all | solution.py:98
  11.1 6.6 %gather_fusion.1 = f32[32,2,128,256]{3,2,1,0:T(8,128)} fusion(f32[16,2,128,256]{3,2,1,0:T(8,128)} %bitcast.132, s32[1024]{0:T(1024)S(1)} %pad_clamp_fusion.1), kind=kCustom, calls=%fused_computation.1 | custom fusion | bytes 16777344 | tf_op jit(solution)/shard_map/jit(_take)/gather | solution.py:87
  17.6 8.6 %fusion = f32[32,1,2,128,256]{4,3,2,1,0:T(8,128)} fusion(f32[32,2,128,256]{3,2,1,0:T(8,128)} %gather_fusion.1, pred[32]{0:T(512)(128)(4,1)S(1)} %get-tuple-element.28, pred[32]{0:T(512)(128)(4,1)S(1)} %fusion.249), kind=kLoop, calls=%fused_computation.4 | loop fusion | flops 4194304 | bytes 16777280 | tf_op jit(solution)/shard_map/jit(_where)/select_n | solution.py:86
  26.2 7.6 %all-to-all-start.1 = ((f32[32,1,2,128,256]{4,3,2,1,0:T(8,128)}), f32[32,1,2,128,256]{4,3,2,1,0:T(8,128)}, u32[]{:S(2)}, u32[]{:S(2)}) async-start(f32[32,1,2,128,256]{4,3,2,1,0:T(8,128)} %fusion), calls=%async_computation.1 | async-start | bytes 16777216 | tf_op jit(solution)/shard_map/all_to_all | solution.py:91
  36.2 2.0 collective-permute-start.4
  39.3 5.6 %collective-permute-start.5 = (f32[15,32,256]{2,0,1:T(8,128)}, f32[15,32,256]{2,0,1:T(8,128)}, u32[]{:S(2)}, u32[]{:S(2)}) collective-permute-start(f32[15,32,256]{2,0,1:T(8,128)} %copy.375), channel_id=1, source_target_pairs={{1,0},{2,1},{3,2},{4,3},{5,4},{6,5},{7,6},{8,7},{9,8},{10,9},{11,1... | collective-permute-start | bytes 1474568 | tf_op jit(solution)/shard_map/ppermute | solution.py:19
  49.0 5.7 %collective-permute-start.3 = (f32[15,32,256]{2,0,1:T(8,128)}, f32[15,32,256]{2,0,1:T(8,128)}, u32[]{:S(2)}, u32[]{:S(2)}) collective-permute-start(f32[15,32,256]{2,0,1:T(8,128)} %copy.372), channel_id=1, source_target_pairs={{1,0},{2,1},{3,2},{4,3},{5,4},{6,5},{7,6},{8,7},{9,8},{10,9},{11,1... | collective-permute-start | bytes 1474568 | tf_op jit(solution)/shard_map/ppermute | solution.py:19
  55.9 2.2 collective-permute-start
  64.6 2.0 fusion.177
  68.6 62.5 %collective-permute-done.4 = f32[15,32,256]{2,0,1:T(8,128)} collective-permute-done((f32[15,32,256]{2,0,1:T(8,128)}, f32[15,32,256]{2,0,1:T(8,128)}, u32[]{:S(2)}, u32[]{:S(2)}) %collective-permute-start.4) | collective-permute-done | bytes 491552 | tf_op jit(solution)/shard_map/ppermute | solution.py:17
  133.0 2.2 collective-permute-done.5
  135.3 5.4 %collective-permute-start.6 = (f32[15,32,256]{2,0,1:T(8,128)}, f32[15,32,256]{2,0,1:T(8,128)S(1)}, u32[]{:S(2)}, u32[]{:S(2)}) collective-permute-start(f32[15,32,256]{2,0,1:T(8,128)} %copy.376), channel_id=1, source_target_pairs={{0,1},{1,2},{2,3},{3,4},{4,5},{5,6},{6,7},{7,8},{8,9},{9,10},{10,1... | collective-permute-start | bytes 1474568 | tf_op jit(solution)/shard_map/ppermute | solution.py:17
  140.6 2.3 fusion.75
  143.0 11.4 %collective-permute-start.7 = (f32[15,32,256]{2,0,1:T(8,128)S(1)}, f32[15,32,256]{2,0,1:T(8,128)S(1)}, u32[]{:S(2)}, u32[]{:S(2)}) collective-permute-start(f32[15,32,256]{2,0,1:T(8,128)S(1)} %copy.378), channel_id=1, source_target_pairs={{1,0},{2,1},{3,2},{4,3},{5,4},{6,5},{7,6},{8,7},{9,8},{10,9},{11,1... | collective-permute-start | bytes 1474568 | tf_op jit(solution)/shard_map/ppermute | solution.py:19
  154.4 2.3 fusion.70
  156.8 2.2 fusion.65
  168.5 5.3 %fusion.2 = f32[2,128,16,256]{3,1,2,0:T(8,128)} fusion(f32[2,128,128,1]{1,2,3,0:T(8,128)S(1)} %copy.267, f32[2,16,32,256]{3,2,1,0:T(8,128)S(1)} %fusion.203, f32[2,16,32,256]{3,2,1,0:T(8,128)S(1)} %fusion.205, f32[2,16,32,256]{3,2,1,0:T(8,128)S(1)} %fusion.207, f32[2,16,32,256]{3,2,1,0:T(8,128)S(1)} %fusion.209), kind=kOutput, calls=%fused_computation.7 | convolution fusion | flops 1613758464 | bytes 8519680 | tf_op jit(solution)/shard_map/vxyz,vyq->vxqz/dot_general | solution.py:145
  173.8 6.3 %gather_fusion.2 = f32[16,2,128,256]{3,2,1,0:T(8,128)} fusion(f32[32,2,128,256]{3,2,1,0:T(8,128)} %bitcast.11, s32[1024]{0:T(1024)S(1)} %pad_clamp_fusion), kind=kCustom, calls=%fused_computation.2 | custom fusion | bytes 8388672 | tf_op jit(solution)/shard_map/jit(_take)/gather | solution.py:106
  180.0 6.9 %fusion.46 = f32[2,16,128,256]{3,2,1,0:T(8,128)S(1)} fusion(f32[2,128,16,256]{3,1,2,0:T(8,128)} %fusion.2, f32[2,16]{1,0:T(2,128)S(1)} %get-tuple-element.90, f32[2,16]{1,0:T(2,128)S(1)} %broadcast_in_dim_reshape.6, pred[2,16]{1,0:T(4,128)(4,1)S(1)} %broadcast_in_dim.95, pred[2,16]{1,0:T(4,128)(4,1)S(1)} %broadcast_in_dim.91, ...), kind=kOutput, calls=%fused_computation.58 | convolution fusion | flops 1615855616 | bytes 12714304 | tf_op jit(solution)/shard_map/vxyz,vqy->vxqz/dot_general | solution.py:147
  189.3 1.9 collective-permute-start.38
  191.3 5.9 %collective-permute-start.39 = (f32[2,15,32,256]{3,2,1,0:T(8,128)S(1)}, f32[2,15,32,256]{3,2,1,0:T(8,128)S(1)}, u32[]{:S(2)}, u32[]{:S(2)}) collective-permute-start(f32[2,15,32,256]{3,2,1,0:T(8,128)S(1)} %get-tuple-element.56), channel_id=1, source_target_pairs={{1,0},{2,1},{3,2},{4,3},{5,4},{6,5},{7,6},{8,7},{9,8},{10,9},{11,1... | collective-permute-start | bytes 2949128 | tf_op jit(solution)/shard_map/ppermute | solution.py:19
  200.5 5.8 %collective-permute-start.19 = (f32[2,15,32,256]{3,2,1,0:T(8,128)S(1)}, f32[2,15,32,256]{3,2,1,0:T(8,128)S(1)}, u32[]{:S(2)}, u32[]{:S(2)}) collective-permute-start(f32[2,15,32,256]{3,2,1,0:T(8,128)S(1)} %get-tuple-element.52), channel_id=1, source_target_pairs={{1,0},{2,1},{3,2},{4,3},{5,4},{6,5},{7,6},{8,7},{9,8},{10,9},{11,1... | collective-permute-start | bytes 2949128 | tf_op jit(solution)/shard_map/ppermute | solution.py:19
  209.8 5.8 %collective-permute-start.9 = (f32[2,15,32,256]{3,2,1,0:T(8,128)S(1)}, f32[2,15,32,256]{3,2,1,0:T(8,128)S(1)}, u32[]{:S(2)}, u32[]{:S(2)}) collective-permute-start(f32[2,15,32,256]{3,2,1,0:T(8,128)S(1)} %get-tuple-element.50), channel_id=1, source_target_pairs={{1,0},{2,1},{3,2},{4,3},{5,4},{6,5},{7,6},{8,7},{9,8},{10,9},{11,1... | collective-permute-start | bytes 2949128 | tf_op jit(solution)/shard_map/ppermute | solution.py:19
  215.6 2.1 collective-permute-start.28
  218.1 3.3 fusion.165
  221.4 5.8 %collective-permute-start.29 = (f32[2,15,32,256]{3,2,1,0:T(8,128)S(1)}, f32[2,15,32,256]{3,2,1,0:T(8,128)S(1)}, u32[]{:S(2)}, u32[]{:S(2)}) collective-permute-start(f32[2,15,32,256]{3,2,1,0:T(8,128)S(1)} %get-tuple-element.54), channel_id=1, source_target_pairs={{1,0},{2,1},{3,2},{4,3},{5,4},{6,5},{7,6},{8,7},{9,8},{10,9},{11,1... | collective-permute-start | bytes 2949128 | tf_op jit(solution)/shard_map/ppermute | solution.py:19
  229.3 3.3 fusion.171
  232.8 3.0 collective-permute-start.41
  237.9 3.3 fusion.174
  248.1 2.1 collective-permute-done.20
  250.7 3.3 fusion.168
  255.7 2.8 collective-permute-start.32
  259.0 2.8 collective-permute-start.14
  264.6 2.1 collective-permute-start.24
  267.4 2.9 collective-permute-start.25
  273.0 2.3 collective-permute-start.35
  276.3 2.4 collective-permute-start.44
  278.8 2.8 collective-permute-start.45
  283.6 5.8 %collective-permute-start.17 = (f32[15,32,256]{2,0,1:T(8,128)S(1)}, f32[15,32,256]{2,0,1:T(8,128)S(1)}, u32[]{:S(2)}, u32[]{:S(2)}) collective-permute-start(f32[15,32,256]{2,0,1:T(8,128)S(1)} %get-tuple-element.70), channel_id=1, source_target_pairs={{1,0},{2,1},{3,2},{4,3},{5,4},{6,5},{7,6},{8,7},{9,8},{10,9},{11,1... | collective-permute-start | bytes 1474568 | tf_op jit(solution)/shard_map/ppermute | solution.py:19
  291.5 5.8 %collective-permute-start.27 = (f32[15,32,256]{2,0,1:T(8,128)S(1)}, f32[15,32,256]{2,0,1:T(8,128)S(1)}, u32[]{:S(2)}, u32[]{:S(2)}) collective-permute-start(f32[15,32,256]{2,0,1:T(8,128)S(1)} %get-tuple-element.75), channel_id=1, source_target_pairs={{1,0},{2,1},{3,2},{4,3},{5,4},{6,5},{7,6},{8,7},{9,8},{10,9},{11,1... | collective-permute-start | bytes 1474568 | tf_op jit(solution)/shard_map/ppermute | solution.py:19
  299.4 5.8 %collective-permute-start.37 = (f32[15,32,256]{2,0,1:T(8,128)S(1)}, f32[15,32,256]{2,0,1:T(8,128)S(1)}, u32[]{:S(2)}, u32[]{:S(2)}) collective-permute-start(f32[15,32,256]{2,0,1:T(8,128)S(1)} %get-tuple-element.80), channel_id=1, source_target_pairs={{1,0},{2,1},{3,2},{4,3},{5,4},{6,5},{7,6},{8,7},{9,8},{10,9},{11,1... | collective-permute-start | bytes 1474568 | tf_op jit(solution)/shard_map/ppermute | solution.py:19
  309.9 6.0 %collective-permute-start.47 = (f32[15,32,256]{2,0,1:T(8,128)S(1)}, f32[15,32,256]{2,0,1:T(8,128)S(1)}, u32[]{:S(2)}, u32[]{:S(2)}) collective-permute-start(f32[15,32,256]{2,0,1:T(8,128)S(1)} %get-tuple-element.85), channel_id=1, source_target_pairs={{1,0},{2,1},{3,2},{4,3},{5,4},{6,5},{7,6},{8,7},{9,8},{10,9},{11,1... | collective-permute-start | bytes 1474568 | tf_op jit(solution)/shard_map/ppermute | solution.py:19
  325.2 4.2 fusion.10
  329.4 4.5 %fusion.49 = f32[2,16,128,256]{3,2,1,0:T(8,128)S(1)} fusion(f32[2,128,16,256]{3,1,2,0:T(8,128)S(1)} %fusion.10, f32[2,16]{1,0:T(2,128)S(1)} %get-tuple-element.90, f32[2,16]{1,0:T(2,128)S(1)} %broadcast_in_dim_reshape.6, pred[2,16]{1,0:T(4,128)(4,1)S(1)} %broadcast_in_dim.95, pred[2,16]{1,0:T(4,128)(4,1)S(1)} %broadcast_in_dim.91, ...), kind=kOutput, calls=%fused_computation.59 | convolution fusion | flops 1615855616 | bytes 12714304 | tf_op jit(solution)/shard_map/vxyz,vqy->vxqz/dot_general | solution.py:147
  338.2 5.9 %collective-permute-start.65 = (f32[2,15,32,256]{3,2,1,0:T(8,128)S(1)}, f32[2,15,32,256]{3,2,1,0:T(8,128)S(1)}, u32[]{:S(2)}, u32[]{:S(2)}) collective-permute-start(f32[2,15,32,256]{3,2,1,0:T(8,128)S(1)} %get-tuple-element.46), channel_id=1, source_target_pairs={{1,0},{2,1},{3,2},{4,3},{5,4},{6,5},{7,6},{8,7},{9,8},{10,9},{11,1... | collective-permute-start | bytes 2949128 | tf_op jit(solution)/shard_map/ppermute | solution.py:19
  347.4 5.8 %collective-permute-start.73 = (f32[2,15,32,256]{3,2,1,0:T(8,128)S(1)}, f32[2,15,32,256]{3,2,1,0:T(8,128)S(1)}, u32[]{:S(2)}, u32[]{:S(2)}) collective-permute-start(f32[2,15,32,256]{3,2,1,0:T(8,128)S(1)} %get-tuple-element.48), channel_id=1, source_target_pairs={{1,0},{2,1},{3,2},{4,3},{5,4},{6,5},{7,6},{8,7},{9,8},{10,9},{11,1... | collective-permute-start | bytes 2949128 | tf_op jit(solution)/shard_map/ppermute | solution.py:19
  356.7 5.8 %collective-permute-start.49 = (f32[2,15,32,256]{3,2,1,0:T(8,128)S(1)}, f32[2,15,32,256]{3,2,1,0:T(8,128)S(1)}, u32[]{:S(2)}, u32[]{:S(2)}) collective-permute-start(f32[2,15,32,256]{3,2,1,0:T(8,128)S(1)} %get-tuple-element.42), channel_id=1, source_target_pairs={{1,0},{2,1},{3,2},{4,3},{5,4},{6,5},{7,6},{8,7},{9,8},{10,9},{11,1... | collective-permute-start | bytes 2949128 | tf_op jit(solution)/shard_map/ppermute | solution.py:19
  362.5 2.1 collective-permute-start.56
  365.0 3.3 fusion.156
  368.3 5.8 %collective-permute-start.57 = (f32[2,15,32,256]{3,2,1,0:T(8,128)S(1)}, f32[2,15,32,256]{3,2,1,0:T(8,128)S(1)}, u32[]{:S(2)}, u32[]{:S(2)}) collective-permute-start(f32[2,15,32,256]{3,2,1,0:T(8,128)S(1)} %get-tuple-element.44), channel_id=1, source_target_pairs={{1,0},{2,1},{3,2},{4,3},{5,4},{6,5},{7,6},{8,7},{9,8},{10,9},{11,1... | collective-permute-start | bytes 2949128 | tf_op jit(solution)/shard_map/ppermute | solution.py:19
  374.7 3.3 fusion.153
  379.9 2.8 collective-permute-start.68
  383.1 3.3 fusion.162
  389.5 2.0 collective-permute-start.76
  393.5 2.4 collective-permute-done.74
  395.9 3.3 fusion.159
  399.3 2.1 collective-permute-start.58
  401.4 2.8 collective-permute-start.60
  404.8 2.8 collective-permute-start.54
  410.4 2.0 collective-permute-start.61
  412.4 3.1 collective-permute-start.62
  415.5 2.1 collective-permute-start.69
  426.9 2.7 collective-permute-done.77
  431.1 2.5 copy.258
  (265 shorter events, 116.1 us)
Async XLA Ops:
  3.5 22.8 %all-to-all-start = ((f32[32,1,1]{2,1,0:T(1,128)}), f32[32,1,1]{2,1,0:T(1,128)S(1)}, u32[]{:S(2)}, u32[]{:S(2)}) async-start(f32[32,1,1]{2,1,0:T(1,128)} %copy.194), calls=%async_computation | async-start | bytes 32768 | tf_op jit(solution)/shard_map/all_to_all | solution.py:98
  26.2 147.5 %all-to-all-start.1 = ((f32[32,1,2,128,256]{4,3,2,1,0:T(8,128)}), f32[32,1,2,128,256]{4,3,2,1,0:T(8,128)}, u32[]{:S(2)}, u32[]{:S(2)}) async-start(f32[32,1,2,128,256]{4,3,2,1,0:T(8,128)} %fusion), calls=%async_computation.1 | async-start | bytes 16777216 | tf_op jit(solution)/shard_map/all_to_all | solution.py:91
  36.2 94.9 %collective-permute-start.4 = (f32[15,32,256]{2,0,1:T(8,128)}, f32[15,32,256]{2,0,1:T(8,128)}, u32[]{:S(2)}, u32[]{:S(2)}) collective-permute-start(f32[15,32,256]{2,0,1:T(8,128)} %copy.373), channel_id=1, source_target_pairs={{0,1},{1,2},{2,3},{3,4},{4,5},{5,6},{6,7},{7,8},{8,9},{9,10},{10,1... | collective-permute-start | bytes 1474568 | tf_op jit(solution)/shard_map/ppermute | solution.py:17
  39.3 96.0 %collective-permute-start.5 = (f32[15,32,256]{2,0,1:T(8,128)}, f32[15,32,256]{2,0,1:T(8,128)}, u32[]{:S(2)}, u32[]{:S(2)}) collective-permute-start(f32[15,32,256]{2,0,1:T(8,128)} %copy.375), channel_id=1, source_target_pairs={{1,0},{2,1},{3,2},{4,3},{5,4},{6,5},{7,6},{8,7},{9,8},{10,9},{11,1... | collective-permute-start | bytes 1474568 | tf_op jit(solution)/shard_map/ppermute | solution.py:19
  46.0 97.0 %collective-permute-start.2 = (f32[15,32,256]{2,0,1:T(8,128)}, f32[15,32,256]{2,0,1:T(8,128)}, u32[]{:S(2)}, u32[]{:S(2)}) collective-permute-start(f32[15,32,256]{2,0,1:T(8,128)} %copy.370), channel_id=1, source_target_pairs={{0,1},{1,2},{2,3},{3,4},{4,5},{5,6},{6,7},{7,8},{8,9},{9,10},{10,1... | collective-permute-start | bytes 1474568 | tf_op jit(solution)/shard_map/ppermute | solution.py:17
  49.0 105.4 %collective-permute-start.3 = (f32[15,32,256]{2,0,1:T(8,128)}, f32[15,32,256]{2,0,1:T(8,128)}, u32[]{:S(2)}, u32[]{:S(2)}) collective-permute-start(f32[15,32,256]{2,0,1:T(8,128)} %copy.372), channel_id=1, source_target_pairs={{1,0},{2,1},{3,2},{4,3},{5,4},{6,5},{7,6},{8,7},{9,8},{10,9},{11,1... | collective-permute-start | bytes 1474568 | tf_op jit(solution)/shard_map/ppermute | solution.py:19
  55.9 100.9 %collective-permute-start = (f32[15,32,256]{2,0,1:T(8,128)}, f32[15,32,256]{2,0,1:T(8,128)}, u32[]{:S(2)}, u32[]{:S(2)}) collective-permute-start(f32[15,32,256]{2,0,1:T(8,128)} %copy.368), channel_id=1, source_target_pairs={{0,1},{1,2},{2,3},{3,4},{4,5},{5,6},{6,7},{7,8},{8,9},{9,10},{10,1... | collective-permute-start | bytes 1474568 | tf_op jit(solution)/shard_map/ppermute | solution.py:17
  131.1 25.6 %collective-permute-start.1 = (f32[15,32,256]{2,0,1:T(8,128)}, f32[15,32,256]{2,0,1:T(8,128)S(1)}, u32[]{:S(2)}, u32[]{:S(2)}) collective-permute-start(f32[15,32,256]{2,0,1:T(8,128)} %copy.369), channel_id=1, source_target_pairs={{1,0},{2,1},{3,2},{4,3},{5,4},{6,5},{7,6},{8,7},{9,8},{10,9},{11,1... | collective-permute-start | bytes 1474568 | tf_op jit(solution)/shard_map/ppermute | solution.py:19
  135.3 23.7 %collective-permute-start.6 = (f32[15,32,256]{2,0,1:T(8,128)}, f32[15,32,256]{2,0,1:T(8,128)S(1)}, u32[]{:S(2)}, u32[]{:S(2)}) collective-permute-start(f32[15,32,256]{2,0,1:T(8,128)} %copy.376), channel_id=1, source_target_pairs={{0,1},{1,2},{2,3},{3,4},{4,5},{5,6},{6,7},{7,8},{8,9},{9,10},{10,1... | collective-permute-start | bytes 1474568 | tf_op jit(solution)/shard_map/ppermute | solution.py:17
  143.0 17.6 %collective-permute-start.7 = (f32[15,32,256]{2,0,1:T(8,128)S(1)}, f32[15,32,256]{2,0,1:T(8,128)S(1)}, u32[]{:S(2)}, u32[]{:S(2)}) collective-permute-start(f32[15,32,256]{2,0,1:T(8,128)S(1)} %copy.378), channel_id=1, source_target_pairs={{1,0},{2,1},{3,2},{4,3},{5,4},{6,5},{7,6},{8,7},{9,8},{10,9},{11,1... | collective-permute-start | bytes 1474568 | tf_op jit(solution)/shard_map/ppermute | solution.py:19
  189.3 20.5 %collective-permute-start.38 = (f32[2,15,32,256]{3,2,1,0:T(8,128)S(1)}, f32[2,15,32,256]{3,2,1,0:T(8,128)S(1)}, u32[]{:S(2)}, u32[]{:S(2)}) collective-permute-start(f32[2,15,32,256]{3,2,1,0:T(8,128)S(1)} %get-tuple-element.55), channel_id=1, source_target_pairs={{0,1},{1,2},{2,3},{3,4},{4,5},{5,6},{6,7},{7,8},{8,9},{9,10},{10,1... | collective-permute-start | bytes 2949128 | tf_op jit(solution)/shard_map/ppermute | solution.py:17
  191.3 24.3 %collective-permute-start.39 = (f32[2,15,32,256]{3,2,1,0:T(8,128)S(1)}, f32[2,15,32,256]{3,2,1,0:T(8,128)S(1)}, u32[]{:S(2)}, u32[]{:S(2)}) collective-permute-start(f32[2,15,32,256]{3,2,1,0:T(8,128)S(1)} %get-tuple-element.56), channel_id=1, source_target_pairs={{1,0},{2,1},{3,2},{4,3},{5,4},{6,5},{7,6},{8,7},{9,8},{10,9},{11,1... | collective-permute-start | bytes 2949128 | tf_op jit(solution)/shard_map/ppermute | solution.py:19
  198.5 22.9 %collective-permute-start.18 = (f32[2,15,32,256]{3,2,1,0:T(8,128)S(1)}, f32[2,15,32,256]{3,2,1,0:T(8,128)S(1)}, u32[]{:S(2)}, u32[]{:S(2)}) collective-permute-start(f32[2,15,32,256]{3,2,1,0:T(8,128)S(1)} %get-tuple-element.51), channel_id=1, source_target_pairs={{0,1},{1,2},{2,3},{3,4},{4,5},{5,6},{6,7},{7,8},{8,9},{9,10},{10,1... | collective-permute-start | bytes 2949128 | tf_op jit(solution)/shard_map/ppermute | solution.py:17
  200.5 26.8 %collective-permute-start.19 = (f32[2,15,32,256]{3,2,1,0:T(8,128)S(1)}, f32[2,15,32,256]{3,2,1,0:T(8,128)S(1)}, u32[]{:S(2)}, u32[]{:S(2)}) collective-permute-start(f32[2,15,32,256]{3,2,1,0:T(8,128)S(1)} %get-tuple-element.52), channel_id=1, source_target_pairs={{1,0},{2,1},{3,2},{4,3},{5,4},{6,5},{7,6},{8,7},{9,8},{10,9},{11,1... | collective-permute-start | bytes 2949128 | tf_op jit(solution)/shard_map/ppermute | solution.py:19
  207.6 25.2 %collective-permute-start.8 = (f32[2,15,32,256]{3,2,1,0:T(8,128)S(1)}, f32[2,15,32,256]{3,2,1,0:T(8,128)S(1)}, u32[]{:S(2)}, u32[]{:S(2)}) collective-permute-start(f32[2,15,32,256]{3,2,1,0:T(8,128)S(1)} %get-tuple-element.49), channel_id=1, source_target_pairs={{0,1},{1,2},{2,3},{3,4},{4,5},{5,6},{6,7},{7,8},{8,9},{9,10},{10,1... | collective-permute-start | bytes 2949128 | tf_op jit(solution)/shard_map/ppermute | solution.py:17
  209.8 26.0 %collective-permute-start.9 = (f32[2,15,32,256]{3,2,1,0:T(8,128)S(1)}, f32[2,15,32,256]{3,2,1,0:T(8,128)S(1)}, u32[]{:S(2)}, u32[]{:S(2)}) collective-permute-start(f32[2,15,32,256]{3,2,1,0:T(8,128)S(1)} %get-tuple-element.50), channel_id=1, source_target_pairs={{1,0},{2,1},{3,2},{4,3},{5,4},{6,5},{7,6},{8,7},{9,8},{10,9},{11,1... | collective-permute-start | bytes 2949128 | tf_op jit(solution)/shard_map/ppermute | solution.py:19
  215.6 25.6 %collective-permute-start.28 = (f32[2,15,32,256]{3,2,1,0:T(8,128)S(1)}, f32[2,15,32,256]{3,2,1,0:T(8,128)S(1)}, u32[]{:S(2)}, u32[]{:S(2)}) collective-permute-start(f32[2,15,32,256]{3,2,1,0:T(8,128)S(1)} %get-tuple-element.53), channel_id=1, source_target_pairs={{0,1},{1,2},{2,3},{3,4},{4,5},{5,6},{6,7},{7,8},{8,9},{9,10},{10,1... | collective-permute-start | bytes 2949128 | tf_op jit(solution)/shard_map/ppermute | solution.py:17
  221.4 20.5 %collective-permute-start.29 = (f32[2,15,32,256]{3,2,1,0:T(8,128)S(1)}, f32[2,15,32,256]{3,2,1,0:T(8,128)S(1)}, u32[]{:S(2)}, u32[]{:S(2)}) collective-permute-start(f32[2,15,32,256]{3,2,1,0:T(8,128)S(1)} %get-tuple-element.54), channel_id=1, source_target_pairs={{1,0},{2,1},{3,2},{4,3},{5,4},{6,5},{7,6},{8,7},{9,8},{10,9},{11,1... | collective-permute-start | bytes 2949128 | tf_op jit(solution)/shard_map/ppermute | solution.py:19
  227.3 16.8 %collective-permute-start.40 = (f32[4,32,256]{2,0,1:T(4,128)S(1)}, f32[4,32,256]{2,0,1:T(4,128)S(1)}, u32[]{:S(2)}, u32[]{:S(2)}) collective-permute-start(f32[4,32,256]{2,0,1:T(4,128)S(1)} %get-tuple-element.86), channel_id=1, source_target_pairs={{0,32},{32,64},{64,96},{96,0},{1,33},{33,65},{65,97},{97,1},{2,34}... | collective-permute-start | bytes 393224 | tf_op jit(solution)/shard_map/ppermute | solution.py:37
  232.8 12.5 %collective-permute-start.41 = (f32[4,32,256]{2,0,1:T(4,128)S(1)}, f32[4,32,256]{2,0,1:T(4,128)S(1)}, u32[]{:S(2)}, u32[]{:S(2)}) collective-permute-start(f32[4,32,256]{2,0,1:T(4,128)S(1)} %get-tuple-element.88), channel_id=1, source_target_pairs={{0,64},{32,96},{64,0},{96,32},{1,65},{33,97},{65,1},{97,33},{2,66}... | collective-permute-start | bytes 393224 | tf_op jit(solution)/shard_map/ppermute | solution.py:37
  235.7 10.4 %collective-permute-start.42 = (f32[4,32,256]{2,0,1:T(4,128)S(1)}, f32[4,32,256]{2,0,1:T(4,128)S(1)}, u32[]{:S(2)}, u32[]{:S(2)}) collective-permute-start(f32[4,32,256]{2,0,1:T(4,128)S(1)} %get-tuple-element.87), channel_id=1, source_target_pairs={{0,96},{32,0},{64,32},{96,64},{1,97},{33,1},{65,33},{97,65},{2,98}... | collective-permute-start | bytes 393224 | tf_op jit(solution)/shard_map/ppermute | solution.py:37
  241.9 12.1 %collective-permute-start.21 = (f32[4,32,256]{2,0,1:T(4,128)S(1)}, f32[4,32,256]{2,0,1:T(4,128)S(1)}, u32[]{:S(2)}, u32[]{:S(2)}) collective-permute-start(f32[4,32,256]{2,0,1:T(4,128)S(1)} %get-tuple-element.78), channel_id=1, source_target_pairs={{0,64},{32,96},{64,0},{96,32},{1,65},{33,97},{65,1},{97,33},{2,66}... | collective-permute-start | bytes 393224 | tf_op jit(solution)/shard_map/ppermute | solution.py:37
  244.1 11.6 %collective-permute-start.22 = (f32[4,32,256]{2,0,1:T(4,128)S(1)}, f32[4,32,256]{2,0,1:T(4,128)S(1)}, u32[]{:S(2)}, u32[]{:S(2)}) collective-permute-start(f32[4,32,256]{2,0,1:T(4,128)S(1)} %get-tuple-element.77), channel_id=1, source_target_pairs={{0,96},{32,0},{64,32},{96,64},{1,97},{33,1},{65,33},{97,65},{2,98}... | collective-permute-start | bytes 393224 | tf_op jit(solution)/shard_map/ppermute | solution.py:37
  245.3 10.4 %collective-permute-start.10 = (f32[4,32,256]{2,0,1:T(4,128)S(1)}, f32[4,32,256]{2,0,1:T(4,128)S(1)}, u32[]{:S(2)}, u32[]{:S(2)}) collective-permute-start(f32[4,32,256]{2,0,1:T(4,128)S(1)} %get-tuple-element.71), channel_id=1, source_target_pairs={{0,32},{32,64},{64,96},{96,0},{1,33},{33,65},{65,97},{97,1},{2,34}... | collective-permute-start | bytes 393224 | tf_op jit(solution)/shard_map/ppermute | solution.py:37
  246.2 12.3 %collective-permute-start.11 = (f32[4,32,256]{2,0,1:T(4,128)S(1)}, f32[4,32,256]{2,0,1:T(4,128)S(1)}, u32[]{:S(2)}, u32[]{:S(2)}) collective-permute-start(f32[4,32,256]{2,0,1:T(4,128)S(1)} %get-tuple-element.73), channel_id=1, source_target_pairs={{0,64},{32,96},{64,0},{96,32},{1,65},{33,97},{65,1},{97,33},{2,66}... | collective-permute-start | bytes 393224 | tf_op jit(solution)/shard_map/ppermute | solution.py:37
  259.0 11.3 %collective-permute-start.14 = (f32[4,32,256]{2,0,1:T(4,128)S(1)}, f32[4,32,256]{2,0,1:T(4,128)S(1)}, u32[]{:S(2)}, u32[]{:S(2)}) collective-permute-start(f32[4,32,256]{2,0,1:T(4,128)S(1)} %get-tuple-element.20), channel_id=1, source_target_pairs={{0,64},{32,96},{64,0},{96,32},{1,65},{33,97},{65,1},{97,33},{2,66}... | collective-permute-start | bytes 393224 | tf_op jit(solution)/shard_map/ppermute | solution.py:43
  263.7 9.3 %collective-permute-start.23 = (f32[4,32,256]{2,0,1:T(4,128)S(1)}, f32[4,32,256]{2,0,1:T(4,128)S(1)}, u32[]{:S(2)}, u32[]{:S(2)}) collective-permute-start(f32[4,32,256]{2,0,1:T(4,128)S(1)} %get-tuple-element.96), channel_id=1, source_target_pairs={{0,32},{32,64},{64,96},{96,0},{1,33},{33,65},{65,97},{97,1},{2,34}... | collective-permute-start | bytes 393224 | tf_op jit(solution)/shard_map/ppermute | solution.py:43
  264.6 10.6 %collective-permute-start.24 = (f32[4,32,256]{2,0,1:T(4,128)S(1)}, f32[4,32,256]{2,0,1:T(4,128)S(1)}, u32[]{:S(2)}, u32[]{:S(2)}) collective-permute-start(f32[4,32,256]{2,0,1:T(4,128)S(1)} %get-tuple-element.96), channel_id=1, source_target_pairs={{0,64},{32,96},{64,0},{96,32},{1,65},{33,97},{65,1},{97,33},{2,66}... | collective-permute-start | bytes 393224 | tf_op jit(solution)/shard_map/ppermute | solution.py:43
  270.5 11.2 %collective-permute-start.34 = (f32[4,32,256]{2,0,1:T(4,128)S(1)}, f32[4,32,256]{2,0,1:T(4,128)S(1)}, u32[]{:S(2)}, u32[]{:S(2)}) collective-permute-start(f32[4,32,256]{2,0,1:T(4,128)S(1)} %get-tuple-element.24), channel_id=1, source_target_pairs={{0,64},{32,96},{64,0},{96,32},{1,65},{33,97},{65,1},{97,33},{2,66}... | collective-permute-start | bytes 393224 | tf_op jit(solution)/shard_map/ppermute | solution.py:43
  273.0 10.6 %collective-permute-start.35 = (f32[4,32,256]{2,0,1:T(4,128)S(1)}, f32[4,32,256]{2,0,1:T(4,128)S(1)}, u32[]{:S(2)}, u32[]{:S(2)}) collective-permute-start(f32[4,32,256]{2,0,1:T(4,128)S(1)} %get-tuple-element.24), channel_id=1, source_target_pairs={{0,96},{32,0},{64,32},{96,64},{1,97},{33,1},{65,33},{97,65},{2,98}... | collective-permute-start | bytes 393224 | tf_op jit(solution)/shard_map/ppermute | solution.py:43
  275.3 14.2 %collective-permute-start.43 = (f32[4,32,256]{2,0,1:T(4,128)S(1)}, f32[4,32,256]{2,0,1:T(4,128)S(1)}, u32[]{:S(2)}, u32[]{:S(2)}) collective-permute-start(f32[4,32,256]{2,0,1:T(4,128)S(1)} %get-tuple-element.98), channel_id=1, source_target_pairs={{0,32},{32,64},{64,96},{96,0},{1,33},{33,65},{65,97},{97,1},{2,34}... | collective-permute-start | bytes 393224 | tf_op jit(solution)/shard_map/ppermute | solution.py:43
  276.3 15.2 %collective-permute-start.44 = (f32[4,32,256]{2,0,1:T(4,128)S(1)}, f32[4,32,256]{2,0,1:T(4,128)S(1)}, u32[]{:S(2)}, u32[]{:S(2)}) collective-permute-start(f32[4,32,256]{2,0,1:T(4,128)S(1)} %get-tuple-element.98), channel_id=1, source_target_pairs={{0,64},{32,96},{64,0},{96,32},{1,65},{33,97},{65,1},{97,33},{2,66}... | collective-permute-start | bytes 393224 | tf_op jit(solution)/shard_map/ppermute | solution.py:43
  278.8 18.5 %collective-permute-start.45 = (f32[4,32,256]{2,0,1:T(4,128)S(1)}, f32[4,32,256]{2,0,1:T(4,128)S(1)}, u32[]{:S(2)}, u32[]{:S(2)}) collective-permute-start(f32[4,32,256]{2,0,1:T(4,128)S(1)} %get-tuple-element.98), channel_id=1, source_target_pairs={{0,96},{32,0},{64,32},{96,64},{1,97},{33,1},{65,33},{97,65},{2,98}... | collective-permute-start | bytes 393224 | tf_op jit(solution)/shard_map/ppermute | solution.py:43
  281.6 17.8 %collective-permute-start.16 = (f32[15,32,256]{2,0,1:T(8,128)S(1)}, f32[15,32,256]{2,0,1:T(8,128)S(1)}, u32[]{:S(2)}, u32[]{:S(2)}) collective-permute-start(f32[15,32,256]{2,0,1:T(8,128)S(1)} %get-tuple-element.69), channel_id=1, source_target_pairs={{0,1},{1,2},{2,3},{3,4},{4,5},{5,6},{6,7},{7,8},{8,9},{9,10},{10,1... | collective-permute-start | bytes 1474568 | tf_op jit(solution)/shard_map/ppermute | solution.py:17
  283.6 21.5 %collective-permute-start.17 = (f32[15,32,256]{2,0,1:T(8,128)S(1)}, f32[15,32,256]{2,0,1:T(8,128)S(1)}, u32[]{:S(2)}, u32[]{:S(2)}) collective-permute-start(f32[15,32,256]{2,0,1:T(8,128)S(1)} %get-tuple-element.70), channel_id=1, source_target_pairs={{1,0},{2,1},{3,2},{4,3},{5,4},{6,5},{7,6},{8,7},{9,8},{10,9},{11,1... | collective-permute-start | bytes 1474568 | tf_op jit(solution)/shard_map/ppermute | solution.py:19
  289.5 20.4 %collective-permute-start.26 = (f32[15,32,256]{2,0,1:T(8,128)S(1)}, f32[15,32,256]{2,0,1:T(8,128)S(1)}, u32[]{:S(2)}, u32[]{:S(2)}) collective-permute-start(f32[15,32,256]{2,0,1:T(8,128)S(1)} %get-tuple-element.74), channel_id=1, source_target_pairs={{0,1},{1,2},{2,3},{3,4},{4,5},{5,6},{6,7},{7,8},{8,9},{9,10},{10,1... | collective-permute-start | bytes 1474568 | tf_op jit(solution)/shard_map/ppermute | solution.py:17
  291.5 24.4 %collective-permute-start.27 = (f32[15,32,256]{2,0,1:T(8,128)S(1)}, f32[15,32,256]{2,0,1:T(8,128)S(1)}, u32[]{:S(2)}, u32[]{:S(2)}) collective-permute-start(f32[15,32,256]{2,0,1:T(8,128)S(1)} %get-tuple-element.75), channel_id=1, source_target_pairs={{1,0},{2,1},{3,2},{4,3},{5,4},{6,5},{7,6},{8,7},{9,8},{10,9},{11,1... | collective-permute-start | bytes 1474568 | tf_op jit(solution)/shard_map/ppermute | solution.py:19
  297.3 21.4 %collective-permute-start.36 = (f32[15,32,256]{2,0,1:T(8,128)S(1)}, f32[15,32,256]{2,0,1:T(8,128)S(1)}, u32[]{:S(2)}, u32[]{:S(2)}) collective-permute-start(f32[15,32,256]{2,0,1:T(8,128)S(1)} %get-tuple-element.79), channel_id=1, source_target_pairs={{0,1},{1,2},{2,3},{3,4},{4,5},{5,6},{6,7},{7,8},{8,9},{9,10},{10,1... | collective-permute-start | bytes 1474568 | tf_op jit(solution)/shard_map/ppermute | solution.py:17
  299.4 19.4 %collective-permute-start.37 = (f32[15,32,256]{2,0,1:T(8,128)S(1)}, f32[15,32,256]{2,0,1:T(8,128)S(1)}, u32[]{:S(2)}, u32[]{:S(2)}) collective-permute-start(f32[15,32,256]{2,0,1:T(8,128)S(1)} %get-tuple-element.80), channel_id=1, source_target_pairs={{1,0},{2,1},{3,2},{4,3},{5,4},{6,5},{7,6},{8,7},{9,8},{10,9},{11,1... | collective-permute-start | bytes 1474568 | tf_op jit(solution)/shard_map/ppermute | solution.py:19
  305.2 16.4 %collective-permute-start.46 = (f32[15,32,256]{2,0,1:T(8,128)S(1)}, f32[15,32,256]{2,0,1:T(8,128)S(1)}, u32[]{:S(2)}, u32[]{:S(2)}) collective-permute-start(f32[15,32,256]{2,0,1:T(8,128)S(1)} %get-tuple-element.84), channel_id=1, source_target_pairs={{0,1},{1,2},{2,3},{3,4},{4,5},{5,6},{6,7},{7,8},{8,9},{9,10},{10,1... | collective-permute-start | bytes 1474568 | tf_op jit(solution)/shard_map/ppermute | solution.py:17
  309.9 12.4 %collective-permute-start.47 = (f32[15,32,256]{2,0,1:T(8,128)S(1)}, f32[15,32,256]{2,0,1:T(8,128)S(1)}, u32[]{:S(2)}, u32[]{:S(2)}) collective-permute-start(f32[15,32,256]{2,0,1:T(8,128)S(1)} %get-tuple-element.85), channel_id=1, source_target_pairs={{1,0},{2,1},{3,2},{4,3},{5,4},{6,5},{7,6},{8,7},{9,8},{10,9},{11,1... | collective-permute-start | bytes 1474568 | tf_op jit(solution)/shard_map/ppermute | solution.py:19
  336.3 20.4 %collective-permute-start.64 = (f32[2,15,32,256]{3,2,1,0:T(8,128)S(1)}, f32[2,15,32,256]{3,2,1,0:T(8,128)S(1)}, u32[]{:S(2)}, u32[]{:S(2)}) collective-permute-start(f32[2,15,32,256]{3,2,1,0:T(8,128)S(1)} %get-tuple-element.45), channel_id=1, source_target_pairs={{0,1},{1,2},{2,3},{3,4},{4,5},{5,6},{6,7},{7,8},{8,9},{9,10},{10,1... | collective-permute-start | bytes 2949128 | tf_op jit(solution)/shard_map/ppermute | solution.py:17
  338.2 24.3 %collective-permute-start.65 = (f32[2,15,32,256]{3,2,1,0:T(8,128)S(1)}, f32[2,15,32,256]{3,2,1,0:T(8,128)S(1)}, u32[]{:S(2)}, u32[]{:S(2)}) collective-permute-start(f32[2,15,32,256]{3,2,1,0:T(8,128)S(1)} %get-tuple-element.46), channel_id=1, source_target_pairs={{1,0},{2,1},{3,2},{4,3},{5,4},{6,5},{7,6},{8,7},{9,8},{10,9},{11,1... | collective-permute-start | bytes 2949128 | tf_op jit(solution)/shard_map/ppermute | solution.py:19
  345.5 22.8 %collective-permute-start.72 = (f32[2,15,32,256]{3,2,1,0:T(8,128)S(1)}, f32[2,15,32,256]{3,2,1,0:T(8,128)S(1)}, u32[]{:S(2)}, u32[]{:S(2)}) collective-permute-start(f32[2,15,32,256]{3,2,1,0:T(8,128)S(1)} %get-tuple-element.47), channel_id=1, source_target_pairs={{0,1},{1,2},{2,3},{3,4},{4,5},{5,6},{6,7},{7,8},{8,9},{9,10},{10,1... | collective-permute-start | bytes 2949128 | tf_op jit(solution)/shard_map/ppermute | solution.py:17
  347.4 26.8 %collective-permute-start.73 = (f32[2,15,32,256]{3,2,1,0:T(8,128)S(1)}, f32[2,15,32,256]{3,2,1,0:T(8,128)S(1)}, u32[]{:S(2)}, u32[]{:S(2)}) collective-permute-start(f32[2,15,32,256]{3,2,1,0:T(8,128)S(1)} %get-tuple-element.48), channel_id=1, source_target_pairs={{1,0},{2,1},{3,2},{4,3},{5,4},{6,5},{7,6},{8,7},{9,8},{10,9},{11,1... | collective-permute-start | bytes 2949128 | tf_op jit(solution)/shard_map/ppermute | solution.py:19
  354.5 23.5 %collective-permute-start.48 = (f32[2,15,32,256]{3,2,1,0:T(8,128)S(1)}, f32[2,15,32,256]{3,2,1,0:T(8,128)S(1)}, u32[]{:S(2)}, u32[]{:S(2)}) collective-permute-start(f32[2,15,32,256]{3,2,1,0:T(8,128)S(1)} %get-tuple-element.41), channel_id=1, source_target_pairs={{0,1},{1,2},{2,3},{3,4},{4,5},{5,6},{6,7},{7,8},{8,9},{9,10},{10,1... | collective-permute-start | bytes 2949128 | tf_op jit(solution)/shard_map/ppermute | solution.py:17
  356.7 23.2 %collective-permute-start.49 = (f32[2,15,32,256]{3,2,1,0:T(8,128)S(1)}, f32[2,15,32,256]{3,2,1,0:T(8,128)S(1)}, u32[]{:S(2)}, u32[]{:S(2)}) collective-permute-start(f32[2,15,32,256]{3,2,1,0:T(8,128)S(1)} %get-tuple-element.42), channel_id=1, source_target_pairs={{1,0},{2,1},{3,2},{4,3},{5,4},{6,5},{7,6},{8,7},{9,8},{10,9},{11,1... | collective-permute-start | bytes 2949128 | tf_op jit(solution)/shard_map/ppermute | solution.py:19
  362.5 23.9 %collective-permute-start.56 = (f32[2,15,32,256]{3,2,1,0:T(8,128)S(1)}, f32[2,15,32,256]{3,2,1,0:T(8,128)S(1)}, u32[]{:S(2)}, u32[]{:S(2)}) collective-permute-start(f32[2,15,32,256]{3,2,1,0:T(8,128)S(1)} %get-tuple-element.43), channel_id=1, source_target_pairs={{0,1},{1,2},{2,3},{3,4},{4,5},{5,6},{6,7},{7,8},{8,9},{9,10},{10,1... | collective-permute-start | bytes 2949128 | tf_op jit(solution)/shard_map/ppermute | solution.py:17
  368.3 19.0 %collective-permute-start.57 = (f32[2,15,32,256]{3,2,1,0:T(8,128)S(1)}, f32[2,15,32,256]{3,2,1,0:T(8,128)S(1)}, u32[]{:S(2)}, u32[]{:S(2)}) collective-permute-start(f32[2,15,32,256]{3,2,1,0:T(8,128)S(1)} %get-tuple-element.44), channel_id=1, source_target_pairs={{1,0},{2,1},{3,2},{4,3},{5,4},{6,5},{7,6},{8,7},{9,8},{10,9},{11,1... | collective-permute-start | bytes 2949128 | tf_op jit(solution)/shard_map/ppermute | solution.py:19
  374.2 15.4 %collective-permute-start.66 = (f32[4,32,256]{2,0,1:T(4,128)S(1)}, f32[4,32,256]{2,0,1:T(4,128)S(1)}, u32[]{:S(2)}, u32[]{:S(2)}) collective-permute-start(f32[4,32,256]{2,0,1:T(4,128)S(1)} %get-tuple-element.63), channel_id=1, source_target_pairs={{0,32},{32,64},{64,96},{96,0},{1,33},{33,65},{65,97},{97,1},{2,34}... | collective-permute-start | bytes 393224 | tf_op jit(solution)/shard_map/ppermute | solution.py:37
  378.1 13.4 %collective-permute-start.67 = (f32[4,32,256]{2,0,1:T(4,128)S(1)}, f32[4,32,256]{2,0,1:T(4,128)S(1)}, u32[]{:S(2)}, u32[]{:S(2)}) collective-permute-start(f32[4,32,256]{2,0,1:T(4,128)S(1)} %get-tuple-element.65), channel_id=1, source_target_pairs={{0,64},{32,96},{64,0},{96,32},{1,65},{33,97},{65,1},{97,33},{2,66}... | collective-permute-start | bytes 393224 | tf_op jit(solution)/shard_map/ppermute | solution.py:37
  379.9 11.8 %collective-permute-start.68 = (f32[4,32,256]{2,0,1:T(4,128)S(1)}, f32[4,32,256]{2,0,1:T(4,128)S(1)}, u32[]{:S(2)}, u32[]{:S(2)}) collective-permute-start(f32[4,32,256]{2,0,1:T(4,128)S(1)} %get-tuple-element.64), channel_id=1, source_target_pairs={{0,96},{32,0},{64,32},{96,64},{1,97},{33,1},{65,33},{97,65},{2,98}... | collective-permute-start | bytes 393224 | tf_op jit(solution)/shard_map/ppermute | solution.py:37
  386.4 9.5 %collective-permute-start.74 = (f32[4,32,256]{2,0,1:T(4,128)S(1)}, f32[4,32,256]{2,0,1:T(4,128)S(1)}, u32[]{:S(2)}, u32[]{:S(2)}) collective-permute-start(f32[4,32,256]{2,0,1:T(4,128)S(1)} %get-tuple-element.66), channel_id=1, source_target_pairs={{0,32},{32,64},{64,96},{96,0},{1,33},{33,65},{65,97},{97,1},{2,34}... | collective-permute-start | bytes 393224 | tf_op jit(solution)/shard_map/ppermute | solution.py:37
  387.3 12.0 %collective-permute-start.75 = (f32[4,32,256]{2,0,1:T(4,128)S(1)}, f32[4,32,256]{2,0,1:T(4,128)S(1)}, u32[]{:S(2)}, u32[]{:S(2)}) collective-permute-start(f32[4,32,256]{2,0,1:T(4,128)S(1)} %get-tuple-element.68), channel_id=1, source_target_pairs={{0,64},{32,96},{64,0},{96,32},{1,65},{33,97},{65,1},{97,33},{2,66}... | collective-permute-start | bytes 393224 | tf_op jit(solution)/shard_map/ppermute | solution.py:37
  389.5 11.9 %collective-permute-start.76 = (f32[4,32,256]{2,0,1:T(4,128)S(1)}, f32[4,32,256]{2,0,1:T(4,128)S(1)}, u32[]{:S(2)}, u32[]{:S(2)}) collective-permute-start(f32[4,32,256]{2,0,1:T(4,128)S(1)} %get-tuple-element.67), channel_id=1, source_target_pairs={{0,96},{32,0},{64,32},{96,64},{1,97},{33,1},{65,33},{97,65},{2,98}... | collective-permute-start | bytes 393224 | tf_op jit(solution)/shard_map/ppermute | solution.py:37
  391.5 9.9 %collective-permute-start.50 = (f32[4,32,256]{2,0,1:T(4,128)S(1)}, f32[4,32,256]{2,0,1:T(4,128)S(1)}, u32[]{:S(2)}, u32[]{:S(2)}) collective-permute-start(f32[4,32,256]{2,0,1:T(4,128)S(1)} %get-tuple-element.57), channel_id=1, source_target_pairs={{0,32},{32,64},{64,96},{96,0},{1,33},{33,65},{65,97},{97,1},{2,34}... | collective-permute-start | bytes 393224 | tf_op jit(solution)/shard_map/ppermute | solution.py:37
  391.6 12.6 %collective-permute-start.51 = (f32[4,32,256]{2,0,1:T(4,128)S(1)}, f32[4,32,256]{2,0,1:T(4,128)S(1)}, u32[]{:S(2)}, u32[]{:S(2)}) collective-permute-start(f32[4,32,256]{2,0,1:T(4,128)S(1)} %get-tuple-element.59), channel_id=1, source_target_pairs={{0,64},{32,96},{64,0},{96,32},{1,65},{33,97},{65,1},{97,33},{2,66}... | collective-permute-start | bytes 393224 | tf_op jit(solution)/shard_map/ppermute | solution.py:37
  404.7 10.8 %collective-permute-start.53 = (f32[4,32,256]{2,0,1:T(4,128)S(1)}, f32[4,32,256]{2,0,1:T(4,128)S(1)}, u32[]{:S(2)}, u32[]{:S(2)}) collective-permute-start(f32[4,32,256]{2,0,1:T(4,128)S(1)} %get-tuple-element.12), channel_id=1, source_target_pairs={{0,32},{32,64},{64,96},{96,0},{1,33},{33,65},{65,97},{97,1},{2,34}... | collective-permute-start | bytes 393224 | tf_op jit(solution)/shard_map/ppermute | solution.py:43
  404.8 10.8 %collective-permute-start.54 = (f32[4,32,256]{2,0,1:T(4,128)S(1)}, f32[4,32,256]{2,0,1:T(4,128)S(1)}, u32[]{:S(2)}, u32[]{:S(2)}) collective-permute-start(f32[4,32,256]{2,0,1:T(4,128)S(1)} %get-tuple-element.12), channel_id=1, source_target_pairs={{0,64},{32,96},{64,0},{96,32},{1,65},{33,97},{65,1},{97,33},{2,66}... | collective-permute-start | bytes 393224 | tf_op jit(solution)/shard_map/ppermute | solution.py:43
  407.6 10.1 %collective-permute-start.55 = (f32[4,32,256]{2,0,1:T(4,128)S(1)}, f32[4,32,256]{2,0,1:T(4,128)S(1)}, u32[]{:S(2)}, u32[]{:S(2)}) collective-permute-start(f32[4,32,256]{2,0,1:T(4,128)S(1)} %get-tuple-element.12), channel_id=1, source_target_pairs={{0,96},{32,0},{64,32},{96,64},{1,97},{33,1},{65,33},{97,65},{2,98}... | collective-permute-start | bytes 393224 | tf_op jit(solution)/shard_map/ppermute | solution.py:43
  410.4 9.4 %collective-permute-start.61 = (f32[4,32,256]{2,0,1:T(4,128)S(1)}, f32[4,32,256]{2,0,1:T(4,128)S(1)}, u32[]{:S(2)}, u32[]{:S(2)}) collective-permute-start(f32[4,32,256]{2,0,1:T(4,128)S(1)} %get-tuple-element.14), channel_id=1, source_target_pairs={{0,32},{32,64},{64,96},{96,0},{1,33},{33,65},{65,97},{97,1},{2,34}... | collective-permute-start | bytes 393224 | tf_op jit(solution)/shard_map/ppermute | solution.py:43
  412.4 9.7 %collective-permute-start.62 = (f32[4,32,256]{2,0,1:T(4,128)S(1)}, f32[4,32,256]{2,0,1:T(4,128)S(1)}, u32[]{:S(2)}, u32[]{:S(2)}) collective-permute-start(f32[4,32,256]{2,0,1:T(4,128)S(1)} %get-tuple-element.14), channel_id=1, source_target_pairs={{0,64},{32,96},{64,0},{96,32},{1,65},{33,97},{65,1},{97,33},{2,66}... | collective-permute-start | bytes 393224 | tf_op jit(solution)/shard_map/ppermute | solution.py:43
  415.5 9.4 %collective-permute-start.69 = (f32[4,32,256]{2,0,1:T(4,128)S(1)}, f32[4,32,256]{2,0,1:T(4,128)S(1)}, u32[]{:S(2)}, u32[]{:S(2)}) collective-permute-start(f32[4,32,256]{2,0,1:T(4,128)S(1)} %get-tuple-element.94), channel_id=1, source_target_pairs={{0,32},{32,64},{64,96},{96,0},{1,33},{33,65},{65,97},{97,1},{2,34}... | collective-permute-start | bytes 393224 | tf_op jit(solution)/shard_map/ppermute | solution.py:43
  417.6 9.2 %collective-permute-start.70 = (f32[4,32,256]{2,0,1:T(4,128)S(1)}, f32[4,32,256]{2,0,1:T(4,128)S(1)}, u32[]{:S(2)}, u32[]{:S(2)}) collective-permute-start(f32[4,32,256]{2,0,1:T(4,128)S(1)} %get-tuple-element.94), channel_id=1, source_target_pairs={{0,64},{32,96},{64,0},{96,32},{1,65},{33,97},{65,1},{97,33},{2,66}... | collective-permute-start | bytes 393224 | tf_op jit(solution)/shard_map/ppermute | solution.py:43
  (27 other events, 176.1 us)

commit v6 on v5

--- a/solution.py
+++ b/solution.py
@@ -81,24 +81,23 @@
     pos_list = route_pos[0]
     block_ids = jnp.arange(blocks, dtype=jnp.int32)
     sends = dest_list[None, :] == block_ids[:, None]
-    has_slot = jnp.any(sends, axis=1)
     slot_of = jnp.argmax(sends, axis=1)
-    outgoing = jnp.where(
-        has_slot[:, None, None, None], jnp.take(sources, slot_of, axis=0), 0.0
-    )
-    out_pos = jnp.where(has_slot, jnp.take(pos_list, slot_of).astype(jnp.float32), -1.0)
-    arrived, arrived_pos = (
-        lax.all_to_all(
-            outgoing.reshape(blocks, 1, planes, ny_cells, nz_cells),
-            "block",
-            split_axis=0,
-            concat_axis=0,
-            tiled=True,
-        ),
-        lax.all_to_all(out_pos.reshape(blocks, 1), "block", split_axis=0, concat_axis=0, tiled=True),
+    outgoing = jnp.take(sources, slot_of, axis=0)
+    tables = lax.all_gather(jnp.stack([dest_list, pos_list]), "block")
+    arrived = lax.all_to_all(
+        outgoing.reshape(blocks, 1, planes, ny_cells, nz_cells),
+        "block",
+        split_axis=0,
+        concat_axis=0,
+        tiled=True,
     )
     arrived = arrived.reshape(blocks, planes, ny_cells, nz_cells)
-    places = arrived_pos.reshape(-1).astype(jnp.int32)
+    to_me = tables[:, 0, :] == lax.axis_index("block")
+    places = jnp.where(
+        jnp.any(to_me, axis=1),
+        jnp.take_along_axis(tables[:, 1, :], jnp.argmax(to_me, axis=1)[:, None], axis=1)[:, 0],
+        -1,
+    )
     position_ids = jnp.arange(per_group * per_block, dtype=jnp.int32)
     holds = places[None, :] == position_ids[:, None]
     found = jnp.any(holds, axis=1)

time: 440 us -> 459 us (1.043)
  blocking collectives: 0 us -> 23.1 us
  starting transfers between devices: 213 us -> 204 us
  local copies, waits for them, and re-layouts: 32.3 us -> 37.5 us
    all_gather x0 -> x1, blocking collectives: none -> 23.1 us  [on_device(): tables = lax.all_gather(jnp.stack([dest_list, pos_list]), 'block')]
    all_to_all x1 -> x0, starting transfers between devices: 7.59 us -> none  [on_device(): lax.all_to_all(out_pos.reshape(blocks, 1), 'block', split_axis=0, concat_...]
    unnamed x30, local copies, waits for them, and re-layouts: 9.4 us -> 14.2 us
    ppermute x16, waiting for transfers between devices: 62.5 us -> 57.8 us  [with_halo(): lax.ppermute(tail, axis, [(i, (i + 1) % count) for i in range(ends)])]
  transfers between devices with their start and end apart: 82 -> 81, of which waited for: 17 -> 17; matrix products, arithmetic and copies ran while one was open for 23% -> 20% of each run, Pallas kernels for 0% -> 0%
where the time goes in v6:
time: 459 us; the launch traced here: 450 us
  starting transfers between devices  204 us (44%)
  matrix products  85.7 us (19%)
  waiting for transfers between devices  80.8 us (18%)
  local copies, waits for them, and re-layouts  37.5 us (8%)
  blocking collectives  23.1 us (5%)
  other arithmetic  16.4 us (4%)
    ppermute x16, starting transfers between devices, with_halo(): lax.ppermute(head, axis, [((i + 1) % count, i) for i in range(ends)])  93.6 us
    ppermute x16, waiting for transfers between devices, with_halo(): lax.ppermute(tail, axis, [(i, (i + 1) % count) for i in range(ends)])  57.8 us
    ppermute x24, starting transfers between devices, view_sum_update(): lax.ppermute(updated, 'view', [(i, (i + shift) % count) for i in range(co...  35.6 us
    ppermute x16, starting transfers between devices, with_halo(): lax.ppermute(tail, axis, [(i, (i + 1) % count) for i in range(ends)])  35.1 us
    ppermute x24, starting transfers between devices, view_sum_update(): lax.ppermute(sent, 'view', [(i, (i + shift) % count) for i in range(count)])  32.8 us
    dot_general x8, matrix products, backward_chunk(): corrected = jnp.einsum('vwyz,vwx->vxyz', rimmed, adj_x, precision=highest)  26.4 us
    all_gather x1, blocking collectives, on_device(): tables = lax.all_gather(jnp.stack([dest_list, pos_list]), 'block')  23.1 us
    unnamed x30, local copies, waits for them, and re-layouts  14.2 us
  transfers between devices with their start and end apart: 81, of which 17 were waited for; matrix products, arithmetic and copies ran while one was open for 20% of the time, Pallas kernels for 0%

profile of v6, /device:TPU:64, one launch (start us, length us, event | category | flops | bytes accessed | tf_op | source)
XLA Modules:
  0.0 449.6 jit_solution(15444858538146262550)
XLA Ops:
  0.7 23.1 %all-gather.1 = s32[32,2,16]{2,1,0:T(2,128)S(1)} all-gather(s32[1,2,16]{2,1,0:T(2,128)S(1)} %add_bitcast_fusion), channel_id=2, replica_groups=mesh['view'=4,'block'=32] {'block'}, dimensions={0}, use_global_device_ids=true | all-gather | bytes 4224 | tf_op jit(solution)/shard_map/all_gather | solution.py:86
  26.5 6.5 %gather_fusion = f32[32,2,128,256]{3,2,1,0:T(8,128)} fusion(f32[16,2,128,256]{3,2,1,0:T(8,128)} %bitcast.140, s32[1024]{0:T(1024)S(1)} %pad_clamp_fusion.1), kind=kCustom, calls=%fused_computation | custom fusion | bytes 16777344 | tf_op jit(solution)/shard_map/jit(_take)/gather | solution.py:85
  33.0 8.2 %bitcast_select_fusion = f32[32,1,2,128,256]{4,3,2,1,0:T(8,128)} fusion(f32[32,2,128,256]{3,2,1,0:T(8,128)} %gather_fusion, pred[32]{0:T(512)(128)(4,1)S(1)} %compare_and_fusion), kind=kLoop, calls=%fused_computation.3 | loop fusion | flops 2097152 | bytes 16777248 | tf_op jit(solution)/shard_map/jit(_take)/select_n | solution.py:85
  41.2 7.0 %all-to-all-start = ((f32[32,1,2,128,256]{4,3,2,1,0:T(8,128)}), f32[32,1,2,128,256]{4,3,2,1,0:T(8,128)}, u32[]{:S(2)}, u32[]{:S(2)}) async-start(f32[32,1,2,128,256]{4,3,2,1,0:T(8,128)} %bitcast_select_fusion), calls=%async_computation | async-start | bytes 16777216 | tf_op jit(solution)/shard_map/all_to_all | solution.py:87
  50.7 2.0 collective-permute-start.4
  53.8 5.6 %collective-permute-start.5 = (f32[15,32,256]{2,0,1:T(8,128)}, f32[15,32,256]{2,0,1:T(8,128)}, u32[]{:S(2)}, u32[]{:S(2)}) collective-permute-start(f32[15,32,256]{2,0,1:T(8,128)} %copy.315), channel_id=1, source_target_pairs={{1,0},{2,1},{3,2},{4,3},{5,4},{6,5},{7,6},{8,7},{9,8},{10,9},{11,1... | collective-permute-start | bytes 1474568 | tf_op jit(solution)/shard_map/ppermute | solution.py:19
  63.6 5.7 %collective-permute-start.3 = (f32[15,32,256]{2,0,1:T(8,128)}, f32[15,32,256]{2,0,1:T(8,128)}, u32[]{:S(2)}, u32[]{:S(2)}) collective-permute-start(f32[15,32,256]{2,0,1:T(8,128)} %copy.312), channel_id=1, source_target_pairs={{1,0},{2,1},{3,2},{4,3},{5,4},{6,5},{7,6},{8,7},{9,8},{10,9},{11,1... | collective-permute-start | bytes 1474568 | tf_op jit(solution)/shard_map/ppermute | solution.py:19
  74.1 2.0 fusion.176
  80.0 2.1 copy.309
  82.4 2.1 copy.316
  84.5 2.1 copy.318
  87.8 57.7 %collective-permute-done.4 = f32[15,32,256]{2,0,1:T(8,128)} collective-permute-done((f32[15,32,256]{2,0,1:T(8,128)}, f32[15,32,256]{2,0,1:T(8,128)}, u32[]{:S(2)}, u32[]{:S(2)}) %collective-permute-start.4) | collective-permute-done | bytes 491552 | tf_op jit(solution)/shard_map/ppermute | solution.py:17
  147.5 2.2 collective-permute-done.5
  149.7 5.8 %collective-permute-start.6 = (f32[15,32,256]{2,0,1:T(8,128)}, f32[15,32,256]{2,0,1:T(8,128)S(1)}, u32[]{:S(2)}, u32[]{:S(2)}) collective-permute-start(f32[15,32,256]{2,0,1:T(8,128)} %copy.316), channel_id=1, source_target_pairs={{0,1},{1,2},{2,3},{3,4},{4,5},{5,6},{6,7},{7,8},{8,9},{9,10},{10,1... | collective-permute-start | bytes 1474568 | tf_op jit(solution)/shard_map/ppermute | solution.py:17
  155.5 2.3 fusion.74
  157.9 10.9 %collective-permute-start.7 = (f32[15,32,256]{2,0,1:T(8,128)}, f32[15,32,256]{2,0,1:T(8,128)S(1)}, u32[]{:S(2)}, u32[]{:S(2)}) collective-permute-start(f32[15,32,256]{2,0,1:T(8,128)} %copy.318), channel_id=1, source_target_pairs={{1,0},{2,1},{3,2},{4,3},{5,4},{6,5},{7,6},{8,7},{9,8},{10,9},{11,1... | collective-permute-start | bytes 1474568 | tf_op jit(solution)/shard_map/ppermute | solution.py:19
  168.8 2.3 fusion.69
  171.1 2.2 fusion.64
  173.3 2.4 collective-permute-done.7
  183.6 5.3 %fusion.1 = f32[2,128,16,256]{3,1,2,0:T(8,128)} fusion(f32[2,128,128,1]{1,2,3,0:T(8,128)S(1)} %copy.205, f32[2,16,32,256]{3,2,1,0:T(8,128)S(1)} %fusion.202, f32[2,16,32,256]{3,2,1,0:T(8,128)S(1)} %fusion.204, f32[2,16,32,256]{3,2,1,0:T(8,128)S(1)} %fusion.206, f32[2,16,32,256]{3,2,1,0:T(8,128)S(1)} %fusion.208), kind=kOutput, calls=%fused_computation.6 | convolution fusion | flops 1613758464 | bytes 8519680 | tf_op jit(solution)/shard_map/vxyz,vyq->vxqz/dot_general | solution.py:144
  188.9 6.2 %gather_fusion.1 = f32[16,2,128,256]{3,2,1,0:T(8,128)} fusion(f32[32,2,128,256]{3,2,1,0:T(8,128)} %bitcast.15, s32[1024]{0:T(1024)S(1)} %pad_clamp_fusion), kind=kCustom, calls=%fused_computation.1 | custom fusion | bytes 8388672 | tf_op jit(solution)/shard_map/jit(_take)/gather | solution.py:105
  195.2 6.9 %fusion.45 = f32[2,16,128,256]{3,2,1,0:T(8,128)S(1)} fusion(f32[2,128,16,256]{3,1,2,0:T(8,128)} %fusion.1, f32[2,16]{1,0:T(2,128)S(1)} %get-tuple-element.94, f32[2,16]{1,0:T(2,128)S(1)} %broadcast_in_dim_reshape.6, pred[2,16]{1,0:T(4,128)(4,1)S(1)} %broadcast_in_dim.80, pred[2,16]{1,0:T(4,128)(4,1)S(1)} %broadcast_in_dim.76, ...), kind=kOutput, calls=%fused_computation.57 | convolution fusion | flops 1615855616 | bytes 12714304 | tf_op jit(solution)/shard_map/vxyz,vqy->vxqz/dot_general | solution.py:146
  206.3 5.8 %collective-permute-start.39 = (f32[2,15,32,256]{3,2,1,0:T(8,128)S(1)}, f32[2,15,32,256]{3,2,1,0:T(8,128)S(1)}, u32[]{:S(2)}, u32[]{:S(2)}) collective-permute-start(f32[2,15,32,256]{3,2,1,0:T(8,128)S(1)} %get-tuple-element.58), channel_id=1, source_target_pairs={{1,0},{2,1},{3,2},{4,3},{5,4},{6,5},{7,6},{8,7},{9,8},{10,9},{11,1... | collective-permute-start | bytes 2949128 | tf_op jit(solution)/shard_map/ppermute | solution.py:19
  215.4 5.8 %collective-permute-start.19 = (f32[2,15,32,256]{3,2,1,0:T(8,128)S(1)}, f32[2,15,32,256]{3,2,1,0:T(8,128)S(1)}, u32[]{:S(2)}, u32[]{:S(2)}) collective-permute-start(f32[2,15,32,256]{3,2,1,0:T(8,128)S(1)} %get-tuple-element.54), channel_id=1, source_target_pairs={{1,0},{2,1},{3,2},{4,3},{5,4},{6,5},{7,6},{8,7},{9,8},{10,9},{11,1... | collective-permute-start | bytes 2949128 | tf_op jit(solution)/shard_map/ppermute | solution.py:19
  224.7 5.8 %collective-permute-start.9 = (f32[2,15,32,256]{3,2,1,0:T(8,128)S(1)}, f32[2,15,32,256]{3,2,1,0:T(8,128)S(1)}, u32[]{:S(2)}, u32[]{:S(2)}) collective-permute-start(f32[2,15,32,256]{3,2,1,0:T(8,128)S(1)} %get-tuple-element.52), channel_id=1, source_target_pairs={{1,0},{2,1},{3,2},{4,3},{5,4},{6,5},{7,6},{8,7},{9,8},{10,9},{11,1... | collective-permute-start | bytes 2949128 | tf_op jit(solution)/shard_map/ppermute | solution.py:19
  230.5 2.1 collective-permute-start.28
  233.0 3.3 fusion.164
  236.3 5.8 %collective-permute-start.29 = (f32[2,15,32,256]{3,2,1,0:T(8,128)S(1)}, f32[2,15,32,256]{3,2,1,0:T(8,128)S(1)}, u32[]{:S(2)}, u32[]{:S(2)}) collective-permute-start(f32[2,15,32,256]{3,2,1,0:T(8,128)S(1)} %get-tuple-element.56), channel_id=1, source_target_pairs={{1,0},{2,1},{3,2},{4,3},{5,4},{6,5},{7,6},{8,7},{9,8},{10,9},{11,1... | collective-permute-start | bytes 2949128 | tf_op jit(solution)/shard_map/ppermute | solution.py:19
  244.3 3.3 fusion.170
  247.7 3.0 collective-permute-start.41
  252.8 3.3 fusion.173
  263.0 2.0 collective-permute-done.20
  265.6 3.3 fusion.167
  270.6 2.8 collective-permute-start.32
  273.9 2.8 collective-permute-start.14
  279.6 2.1 collective-permute-start.24
  282.3 2.9 collective-permute-start.25
  287.9 2.2 collective-permute-start.35
  291.2 2.4 collective-permute-start.44
  293.7 2.8 collective-permute-start.45
  298.5 5.8 %collective-permute-start.17 = (f32[15,32,256]{2,0,1:T(8,128)S(1)}, f32[15,32,256]{2,0,1:T(8,128)S(1)}, u32[]{:S(2)}, u32[]{:S(2)}) collective-permute-start(f32[15,32,256]{2,0,1:T(8,128)S(1)} %get-tuple-element.72), channel_id=1, source_target_pairs={{1,0},{2,1},{3,2},{4,3},{5,4},{6,5},{7,6},{8,7},{9,8},{10,9},{11,1... | collective-permute-start | bytes 1474568 | tf_op jit(solution)/shard_map/ppermute | solution.py:19
  306.4 5.8 %collective-permute-start.27 = (f32[15,32,256]{2,0,1:T(8,128)S(1)}, f32[15,32,256]{2,0,1:T(8,128)S(1)}, u32[]{:S(2)}, u32[]{:S(2)}) collective-permute-start(f32[15,32,256]{2,0,1:T(8,128)S(1)} %get-tuple-element.77), channel_id=1, source_target_pairs={{1,0},{2,1},{3,2},{4,3},{5,4},{6,5},{7,6},{8,7},{9,8},{10,9},{11,1... | collective-permute-start | bytes 1474568 | tf_op jit(solution)/shard_map/ppermute | solution.py:19
  314.3 5.8 %collective-permute-start.37 = (f32[15,32,256]{2,0,1:T(8,128)S(1)}, f32[15,32,256]{2,0,1:T(8,128)S(1)}, u32[]{:S(2)}, u32[]{:S(2)}) collective-permute-start(f32[15,32,256]{2,0,1:T(8,128)S(1)} %get-tuple-element.82), channel_id=1, source_target_pairs={{1,0},{2,1},{3,2},{4,3},{5,4},{6,5},{7,6},{8,7},{9,8},{10,9},{11,1... | collective-permute-start | bytes 1474568 | tf_op jit(solution)/shard_map/ppermute | solution.py:19
  324.9 6.0 %collective-permute-start.47 = (f32[15,32,256]{2,0,1:T(8,128)S(1)}, f32[15,32,256]{2,0,1:T(8,128)S(1)}, u32[]{:S(2)}, u32[]{:S(2)}) collective-permute-start(f32[15,32,256]{2,0,1:T(8,128)S(1)} %get-tuple-element.87), channel_id=1, source_target_pairs={{1,0},{2,1},{3,2},{4,3},{5,4},{6,5},{7,6},{8,7},{9,8},{10,9},{11,1... | collective-permute-start | bytes 1474568 | tf_op jit(solution)/shard_map/ppermute | solution.py:19
  340.1 4.5 %fusion.9 = f32[2,128,16,256]{3,1,2,0:T(8,128)S(1)} fusion(f32[2,128,128,1]{1,2,3,0:T(8,128)S(1)} %copy.205, f32[2,16,32,256]{3,2,1,0:T(8,128)S(1)} %fusion.194, f32[2,16,32,256]{3,2,1,0:T(8,128)S(1)} %fusion.196, f32[2,16,32,256]{3,2,1,0:T(8,128)S(1)} %fusion.198, f32[2,16,32,256]{3,2,1,0:T(8,128)S(1)} %fusion.200), kind=kOutput, calls=%fused_computation.14 | convolution fusion | flops 1613758464 | bytes 8519680 | tf_op jit(solution)/shard_map/vxyz,vyq->vxqz/dot_general | solution.py:144
  344.6 4.8 %fusion.48 = f32[2,16,128,256]{3,2,1,0:T(8,128)S(1)} fusion(f32[2,128,16,256]{3,1,2,0:T(8,128)S(1)} %fusion.9, f32[2,16]{1,0:T(2,128)S(1)} %get-tuple-element.94, f32[2,16]{1,0:T(2,128)S(1)} %broadcast_in_dim_reshape.6, pred[2,16]{1,0:T(4,128)(4,1)S(1)} %broadcast_in_dim.80, pred[2,16]{1,0:T(4,128)(4,1)S(1)} %broadcast_in_dim.76, ...), kind=kOutput, calls=%fused_computation.58 | convolution fusion | flops 1615855616 | bytes 12714304 | tf_op jit(solution)/shard_map/vxyz,vqy->vxqz/dot_general | solution.py:146
  353.7 5.9 %collective-permute-start.65 = (f32[2,15,32,256]{3,2,1,0:T(8,128)S(1)}, f32[2,15,32,256]{3,2,1,0:T(8,128)S(1)}, u32[]{:S(2)}, u32[]{:S(2)}) collective-permute-start(f32[2,15,32,256]{3,2,1,0:T(8,128)S(1)} %get-tuple-element.48), channel_id=1, source_target_pairs={{1,0},{2,1},{3,2},{4,3},{5,4},{6,5},{7,6},{8,7},{9,8},{10,9},{11,1... | collective-permute-start | bytes 2949128 | tf_op jit(solution)/shard_map/ppermute | solution.py:19
  362.9 5.8 %collective-permute-start.73 = (f32[2,15,32,256]{3,2,1,0:T(8,128)S(1)}, f32[2,15,32,256]{3,2,1,0:T(8,128)S(1)}, u32[]{:S(2)}, u32[]{:S(2)}) collective-permute-start(f32[2,15,32,256]{3,2,1,0:T(8,128)S(1)} %get-tuple-element.50), channel_id=1, source_target_pairs={{1,0},{2,1},{3,2},{4,3},{5,4},{6,5},{7,6},{8,7},{9,8},{10,9},{11,1... | collective-permute-start | bytes 2949128 | tf_op jit(solution)/shard_map/ppermute | solution.py:19
  372.2 5.8 %collective-permute-start.49 = (f32[2,15,32,256]{3,2,1,0:T(8,128)S(1)}, f32[2,15,32,256]{3,2,1,0:T(8,128)S(1)}, u32[]{:S(2)}, u32[]{:S(2)}) collective-permute-start(f32[2,15,32,256]{3,2,1,0:T(8,128)S(1)} %get-tuple-element.44), channel_id=1, source_target_pairs={{1,0},{2,1},{3,2},{4,3},{5,4},{6,5},{7,6},{8,7},{9,8},{10,9},{11,1... | collective-permute-start | bytes 2949128 | tf_op jit(solution)/shard_map/ppermute | solution.py:19
  378.0 2.1 collective-permute-start.56
  380.5 3.3 fusion.155
  383.8 5.8 %collective-permute-start.57 = (f32[2,15,32,256]{3,2,1,0:T(8,128)S(1)}, f32[2,15,32,256]{3,2,1,0:T(8,128)S(1)}, u32[]{:S(2)}, u32[]{:S(2)}) collective-permute-start(f32[2,15,32,256]{3,2,1,0:T(8,128)S(1)} %get-tuple-element.46), channel_id=1, source_target_pairs={{1,0},{2,1},{3,2},{4,3},{5,4},{6,5},{7,6},{8,7},{9,8},{10,9},{11,1... | collective-permute-start | bytes 2949128 | tf_op jit(solution)/shard_map/ppermute | solution.py:19
  390.2 3.3 fusion.152
  395.4 2.8 collective-permute-start.68
  398.6 3.3 fusion.161
  409.0 2.4 collective-permute-done.74
  411.5 3.3 fusion.158
  414.9 2.1 collective-permute-start.58
  417.0 2.8 collective-permute-start.60
  420.3 2.8 collective-permute-start.54
  427.9 3.1 collective-permute-start.62
  431.1 2.1 collective-permute-start.69
  442.4 2.8 collective-permute-done.77
  446.7 2.5 copy.196
  (268 shorter events, 120.8 us)
Async XLA Ops:
  41.2 147.7 %all-to-all-start = ((f32[32,1,2,128,256]{4,3,2,1,0:T(8,128)}), f32[32,1,2,128,256]{4,3,2,1,0:T(8,128)}, u32[]{:S(2)}, u32[]{:S(2)}) async-start(f32[32,1,2,128,256]{4,3,2,1,0:T(8,128)} %bitcast_select_fusion), calls=%async_computation | async-start | bytes 16777216 | tf_op jit(solution)/shard_map/all_to_all | solution.py:87
  50.7 94.9 %collective-permute-start.4 = (f32[15,32,256]{2,0,1:T(8,128)}, f32[15,32,256]{2,0,1:T(8,128)}, u32[]{:S(2)}, u32[]{:S(2)}) collective-permute-start(f32[15,32,256]{2,0,1:T(8,128)} %copy.313), channel_id=1, source_target_pairs={{0,1},{1,2},{2,3},{3,4},{4,5},{5,6},{6,7},{7,8},{8,9},{9,10},{10,1... | collective-permute-start | bytes 1474568 | tf_op jit(solution)/shard_map/ppermute | solution.py:17
  53.8 95.9 %collective-permute-start.5 = (f32[15,32,256]{2,0,1:T(8,128)}, f32[15,32,256]{2,0,1:T(8,128)}, u32[]{:S(2)}, u32[]{:S(2)}) collective-permute-start(f32[15,32,256]{2,0,1:T(8,128)} %copy.315), channel_id=1, source_target_pairs={{1,0},{2,1},{3,2},{4,3},{5,4},{6,5},{7,6},{8,7},{9,8},{10,9},{11,1... | collective-permute-start | bytes 1474568 | tf_op jit(solution)/shard_map/ppermute | solution.py:19
  60.5 97.3 %collective-permute-start.2 = (f32[15,32,256]{2,0,1:T(8,128)}, f32[15,32,256]{2,0,1:T(8,128)}, u32[]{:S(2)}, u32[]{:S(2)}) collective-permute-start(f32[15,32,256]{2,0,1:T(8,128)} %copy.310), channel_id=1, source_target_pairs={{0,1},{1,2},{2,3},{3,4},{4,5},{5,6},{6,7},{7,8},{8,9},{9,10},{10,1... | collective-permute-start | bytes 1474568 | tf_op jit(solution)/shard_map/ppermute | solution.py:17
  63.6 105.2 %collective-permute-start.3 = (f32[15,32,256]{2,0,1:T(8,128)}, f32[15,32,256]{2,0,1:T(8,128)}, u32[]{:S(2)}, u32[]{:S(2)}) collective-permute-start(f32[15,32,256]{2,0,1:T(8,128)} %copy.312), channel_id=1, source_target_pairs={{1,0},{2,1},{3,2},{4,3},{5,4},{6,5},{7,6},{8,7},{9,8},{10,9},{11,1... | collective-permute-start | bytes 1474568 | tf_op jit(solution)/shard_map/ppermute | solution.py:19
  70.4 100.7 %collective-permute-start = (f32[15,32,256]{2,0,1:T(8,128)}, f32[15,32,256]{2,0,1:T(8,128)}, u32[]{:S(2)}, u32[]{:S(2)}) collective-permute-start(f32[15,32,256]{2,0,1:T(8,128)} %copy.308), channel_id=1, source_target_pairs={{0,1},{1,2},{2,3},{3,4},{4,5},{5,6},{6,7},{7,8},{8,9},{9,10},{10,1... | collective-permute-start | bytes 1474568 | tf_op jit(solution)/shard_map/ppermute | solution.py:17
  145.5 25.6 %collective-permute-start.1 = (f32[15,32,256]{2,0,1:T(8,128)}, f32[15,32,256]{2,0,1:T(8,128)S(1)}, u32[]{:S(2)}, u32[]{:S(2)}) collective-permute-start(f32[15,32,256]{2,0,1:T(8,128)} %copy.309), channel_id=1, source_target_pairs={{1,0},{2,1},{3,2},{4,3},{5,4},{6,5},{7,6},{8,7},{9,8},{10,9},{11,1... | collective-permute-start | bytes 1474568 | tf_op jit(solution)/shard_map/ppermute | solution.py:19
  149.7 23.6 %collective-permute-start.6 = (f32[15,32,256]{2,0,1:T(8,128)}, f32[15,32,256]{2,0,1:T(8,128)S(1)}, u32[]{:S(2)}, u32[]{:S(2)}) collective-permute-start(f32[15,32,256]{2,0,1:T(8,128)} %copy.316), channel_id=1, source_target_pairs={{0,1},{1,2},{2,3},{3,4},{4,5},{5,6},{6,7},{7,8},{8,9},{9,10},{10,1... | collective-permute-start | bytes 1474568 | tf_op jit(solution)/shard_map/ppermute | solution.py:17
  157.9 17.9 %collective-permute-start.7 = (f32[15,32,256]{2,0,1:T(8,128)}, f32[15,32,256]{2,0,1:T(8,128)S(1)}, u32[]{:S(2)}, u32[]{:S(2)}) collective-permute-start(f32[15,32,256]{2,0,1:T(8,128)} %copy.318), channel_id=1, source_target_pairs={{1,0},{2,1},{3,2},{4,3},{5,4},{6,5},{7,6},{8,7},{9,8},{10,9},{11,1... | collective-permute-start | bytes 1474568 | tf_op jit(solution)/shard_map/ppermute | solution.py:19
  204.4 20.3 %collective-permute-start.38 = (f32[2,15,32,256]{3,2,1,0:T(8,128)S(1)}, f32[2,15,32,256]{3,2,1,0:T(8,128)S(1)}, u32[]{:S(2)}, u32[]{:S(2)}) collective-permute-start(f32[2,15,32,256]{3,2,1,0:T(8,128)S(1)} %get-tuple-element.57), channel_id=1, source_target_pairs={{0,1},{1,2},{2,3},{3,4},{4,5},{5,6},{6,7},{7,8},{8,9},{9,10},{10,1... | collective-permute-start | bytes 2949128 | tf_op jit(solution)/shard_map/ppermute | solution.py:17
  206.3 24.1 %collective-permute-start.39 = (f32[2,15,32,256]{3,2,1,0:T(8,128)S(1)}, f32[2,15,32,256]{3,2,1,0:T(8,128)S(1)}, u32[]{:S(2)}, u32[]{:S(2)}) collective-permute-start(f32[2,15,32,256]{3,2,1,0:T(8,128)S(1)} %get-tuple-element.58), channel_id=1, source_target_pairs={{1,0},{2,1},{3,2},{4,3},{5,4},{6,5},{7,6},{8,7},{9,8},{10,9},{11,1... | collective-permute-start | bytes 2949128 | tf_op jit(solution)/shard_map/ppermute | solution.py:19
  213.5 22.8 %collective-permute-start.18 = (f32[2,15,32,256]{3,2,1,0:T(8,128)S(1)}, f32[2,15,32,256]{3,2,1,0:T(8,128)S(1)}, u32[]{:S(2)}, u32[]{:S(2)}) collective-permute-start(f32[2,15,32,256]{3,2,1,0:T(8,128)S(1)} %get-tuple-element.53), channel_id=1, source_target_pairs={{0,1},{1,2},{2,3},{3,4},{4,5},{5,6},{6,7},{7,8},{8,9},{9,10},{10,1... | collective-permute-start | bytes 2949128 | tf_op jit(solution)/shard_map/ppermute | solution.py:17
  215.4 26.8 %collective-permute-start.19 = (f32[2,15,32,256]{3,2,1,0:T(8,128)S(1)}, f32[2,15,32,256]{3,2,1,0:T(8,128)S(1)}, u32[]{:S(2)}, u32[]{:S(2)}) collective-permute-start(f32[2,15,32,256]{3,2,1,0:T(8,128)S(1)} %get-tuple-element.54), channel_id=1, source_target_pairs={{1,0},{2,1},{3,2},{4,3},{5,4},{6,5},{7,6},{8,7},{9,8},{10,9},{11,1... | collective-permute-start | bytes 2949128 | tf_op jit(solution)/shard_map/ppermute | solution.py:19
  222.5 25.2 %collective-permute-start.8 = (f32[2,15,32,256]{3,2,1,0:T(8,128)S(1)}, f32[2,15,32,256]{3,2,1,0:T(8,128)S(1)}, u32[]{:S(2)}, u32[]{:S(2)}) collective-permute-start(f32[2,15,32,256]{3,2,1,0:T(8,128)S(1)} %get-tuple-element.51), channel_id=1, source_target_pairs={{0,1},{1,2},{2,3},{3,4},{4,5},{5,6},{6,7},{7,8},{8,9},{9,10},{10,1... | collective-permute-start | bytes 2949128 | tf_op jit(solution)/shard_map/ppermute | solution.py:17
  224.7 26.0 %collective-permute-start.9 = (f32[2,15,32,256]{3,2,1,0:T(8,128)S(1)}, f32[2,15,32,256]{3,2,1,0:T(8,128)S(1)}, u32[]{:S(2)}, u32[]{:S(2)}) collective-permute-start(f32[2,15,32,256]{3,2,1,0:T(8,128)S(1)} %get-tuple-element.52), channel_id=1, source_target_pairs={{1,0},{2,1},{3,2},{4,3},{5,4},{6,5},{7,6},{8,7},{9,8},{10,9},{11,1... | collective-permute-start | bytes 2949128 | tf_op jit(solution)/shard_map/ppermute | solution.py:19
  230.5 25.6 %collective-permute-start.28 = (f32[2,15,32,256]{3,2,1,0:T(8,128)S(1)}, f32[2,15,32,256]{3,2,1,0:T(8,128)S(1)}, u32[]{:S(2)}, u32[]{:S(2)}) collective-permute-start(f32[2,15,32,256]{3,2,1,0:T(8,128)S(1)} %get-tuple-element.55), channel_id=1, source_target_pairs={{0,1},{1,2},{2,3},{3,4},{4,5},{5,6},{6,7},{7,8},{8,9},{9,10},{10,1... | collective-permute-start | bytes 2949128 | tf_op jit(solution)/shard_map/ppermute | solution.py:17
  236.3 20.5 %collective-permute-start.29 = (f32[2,15,32,256]{3,2,1,0:T(8,128)S(1)}, f32[2,15,32,256]{3,2,1,0:T(8,128)S(1)}, u32[]{:S(2)}, u32[]{:S(2)}) collective-permute-start(f32[2,15,32,256]{3,2,1,0:T(8,128)S(1)} %get-tuple-element.56), channel_id=1, source_target_pairs={{1,0},{2,1},{3,2},{4,3},{5,4},{6,5},{7,6},{8,7},{9,8},{10,9},{11,1... | collective-permute-start | bytes 2949128 | tf_op jit(solution)/shard_map/ppermute | solution.py:19
  242.2 16.8 %collective-permute-start.40 = (f32[4,32,256]{2,0,1:T(4,128)S(1)}, f32[4,32,256]{2,0,1:T(4,128)S(1)}, u32[]{:S(2)}, u32[]{:S(2)}) collective-permute-start(f32[4,32,256]{2,0,1:T(4,128)S(1)} %get-tuple-element.88), channel_id=1, source_target_pairs={{0,32},{32,64},{64,96},{96,0},{1,33},{33,65},{65,97},{97,1},{2,34}... | collective-permute-start | bytes 393224 | tf_op jit(solution)/shard_map/ppermute | solution.py:37
  247.7 12.5 %collective-permute-start.41 = (f32[4,32,256]{2,0,1:T(4,128)S(1)}, f32[4,32,256]{2,0,1:T(4,128)S(1)}, u32[]{:S(2)}, u32[]{:S(2)}) collective-permute-start(f32[4,32,256]{2,0,1:T(4,128)S(1)} %get-tuple-element.90), channel_id=1, source_target_pairs={{0,64},{32,96},{64,0},{96,32},{1,65},{33,97},{65,1},{97,33},{2,66}... | collective-permute-start | bytes 393224 | tf_op jit(solution)/shard_map/ppermute | solution.py:37
  250.7 10.5 %collective-permute-start.42 = (f32[4,32,256]{2,0,1:T(4,128)S(1)}, f32[4,32,256]{2,0,1:T(4,128)S(1)}, u32[]{:S(2)}, u32[]{:S(2)}) collective-permute-start(f32[4,32,256]{2,0,1:T(4,128)S(1)} %get-tuple-element.89), channel_id=1, source_target_pairs={{0,96},{32,0},{64,32},{96,64},{1,97},{33,1},{65,33},{97,65},{2,98}... | collective-permute-start | bytes 393224 | tf_op jit(solution)/shard_map/ppermute | solution.py:37
  256.9 12.1 %collective-permute-start.21 = (f32[4,32,256]{2,0,1:T(4,128)S(1)}, f32[4,32,256]{2,0,1:T(4,128)S(1)}, u32[]{:S(2)}, u32[]{:S(2)}) collective-permute-start(f32[4,32,256]{2,0,1:T(4,128)S(1)} %get-tuple-element.80), channel_id=1, source_target_pairs={{0,64},{32,96},{64,0},{96,32},{1,65},{33,97},{65,1},{97,33},{2,66}... | collective-permute-start | bytes 393224 | tf_op jit(solution)/shard_map/ppermute | solution.py:37
  259.1 11.5 %collective-permute-start.22 = (f32[4,32,256]{2,0,1:T(4,128)S(1)}, f32[4,32,256]{2,0,1:T(4,128)S(1)}, u32[]{:S(2)}, u32[]{:S(2)}) collective-permute-start(f32[4,32,256]{2,0,1:T(4,128)S(1)} %get-tuple-element.79), channel_id=1, source_target_pairs={{0,96},{32,0},{64,32},{96,64},{1,97},{33,1},{65,33},{97,65},{2,98}... | collective-permute-start | bytes 393224 | tf_op jit(solution)/shard_map/ppermute | solution.py:37
  260.2 10.4 %collective-permute-start.10 = (f32[4,32,256]{2,0,1:T(4,128)S(1)}, f32[4,32,256]{2,0,1:T(4,128)S(1)}, u32[]{:S(2)}, u32[]{:S(2)}) collective-permute-start(f32[4,32,256]{2,0,1:T(4,128)S(1)} %get-tuple-element.73), channel_id=1, source_target_pairs={{0,32},{32,64},{64,96},{96,0},{1,33},{33,65},{65,97},{97,1},{2,34}... | collective-permute-start | bytes 393224 | tf_op jit(solution)/shard_map/ppermute | solution.py:37
  261.2 12.2 %collective-permute-start.11 = (f32[4,32,256]{2,0,1:T(4,128)S(1)}, f32[4,32,256]{2,0,1:T(4,128)S(1)}, u32[]{:S(2)}, u32[]{:S(2)}) collective-permute-start(f32[4,32,256]{2,0,1:T(4,128)S(1)} %get-tuple-element.75), channel_id=1, source_target_pairs={{0,64},{32,96},{64,0},{96,32},{1,65},{33,97},{65,1},{97,33},{2,66}... | collective-permute-start | bytes 393224 | tf_op jit(solution)/shard_map/ppermute | solution.py:37
  270.6 9.0 %collective-permute-start.32 = (f32[4,32,256]{2,0,1:T(4,128)S(1)}, f32[4,32,256]{2,0,1:T(4,128)S(1)}, u32[]{:S(2)}, u32[]{:S(2)}) collective-permute-start(f32[4,32,256]{2,0,1:T(4,128)S(1)} %get-tuple-element.84), channel_id=1, source_target_pairs={{0,96},{32,0},{64,32},{96,64},{1,97},{33,1},{65,33},{97,65},{2,98}... | collective-permute-start | bytes 393224 | tf_op jit(solution)/shard_map/ppermute | solution.py:37
  273.9 11.3 %collective-permute-start.14 = (f32[4,32,256]{2,0,1:T(4,128)S(1)}, f32[4,32,256]{2,0,1:T(4,128)S(1)}, u32[]{:S(2)}, u32[]{:S(2)}) collective-permute-start(f32[4,32,256]{2,0,1:T(4,128)S(1)} %get-tuple-element.22), channel_id=1, source_target_pairs={{0,64},{32,96},{64,0},{96,32},{1,65},{33,97},{65,1},{97,33},{2,66}... | collective-permute-start | bytes 393224 | tf_op jit(solution)/shard_map/ppermute | solution.py:43
  278.6 9.3 %collective-permute-start.23 = (f32[4,32,256]{2,0,1:T(4,128)S(1)}, f32[4,32,256]{2,0,1:T(4,128)S(1)}, u32[]{:S(2)}, u32[]{:S(2)}) collective-permute-start(f32[4,32,256]{2,0,1:T(4,128)S(1)} %get-tuple-element.100), channel_id=1, source_target_pairs={{0,32},{32,64},{64,96},{96,0},{1,33},{33,65},{65,97},{97,1},{2,34}... | collective-permute-start | bytes 393224 | tf_op jit(solution)/shard_map/ppermute | solution.py:43
  279.6 10.6 %collective-permute-start.24 = (f32[4,32,256]{2,0,1:T(4,128)S(1)}, f32[4,32,256]{2,0,1:T(4,128)S(1)}, u32[]{:S(2)}, u32[]{:S(2)}) collective-permute-start(f32[4,32,256]{2,0,1:T(4,128)S(1)} %get-tuple-element.100), channel_id=1, source_target_pairs={{0,64},{32,96},{64,0},{96,32},{1,65},{33,97},{65,1},{97,33},{2,66}... | collective-permute-start | bytes 393224 | tf_op jit(solution)/shard_map/ppermute | solution.py:43
  285.4 11.2 %collective-permute-start.34 = (f32[4,32,256]{2,0,1:T(4,128)S(1)}, f32[4,32,256]{2,0,1:T(4,128)S(1)}, u32[]{:S(2)}, u32[]{:S(2)}) collective-permute-start(f32[4,32,256]{2,0,1:T(4,128)S(1)} %get-tuple-element.26), channel_id=1, source_target_pairs={{0,64},{32,96},{64,0},{96,32},{1,65},{33,97},{65,1},{97,33},{2,66}... | collective-permute-start | bytes 393224 | tf_op jit(solution)/shard_map/ppermute | solution.py:43
  287.9 10.6 %collective-permute-start.35 = (f32[4,32,256]{2,0,1:T(4,128)S(1)}, f32[4,32,256]{2,0,1:T(4,128)S(1)}, u32[]{:S(2)}, u32[]{:S(2)}) collective-permute-start(f32[4,32,256]{2,0,1:T(4,128)S(1)} %get-tuple-element.26), channel_id=1, source_target_pairs={{0,96},{32,0},{64,32},{96,64},{1,97},{33,1},{65,33},{97,65},{2,98}... | collective-permute-start | bytes 393224 | tf_op jit(solution)/shard_map/ppermute | solution.py:43
  290.2 14.2 %collective-permute-start.43 = (f32[4,32,256]{2,0,1:T(4,128)S(1)}, f32[4,32,256]{2,0,1:T(4,128)S(1)}, u32[]{:S(2)}, u32[]{:S(2)}) collective-permute-start(f32[4,32,256]{2,0,1:T(4,128)S(1)} %get-tuple-element.102), channel_id=1, source_target_pairs={{0,32},{32,64},{64,96},{96,0},{1,33},{33,65},{65,97},{97,1},{2,34}... | collective-permute-start | bytes 393224 | tf_op jit(solution)/shard_map/ppermute | solution.py:43
  291.2 15.2 %collective-permute-start.44 = (f32[4,32,256]{2,0,1:T(4,128)S(1)}, f32[4,32,256]{2,0,1:T(4,128)S(1)}, u32[]{:S(2)}, u32[]{:S(2)}) collective-permute-start(f32[4,32,256]{2,0,1:T(4,128)S(1)} %get-tuple-element.102), channel_id=1, source_target_pairs={{0,64},{32,96},{64,0},{96,32},{1,65},{33,97},{65,1},{97,33},{2,66}... | collective-permute-start | bytes 393224 | tf_op jit(solution)/shard_map/ppermute | solution.py:43
  293.7 18.5 %collective-permute-start.45 = (f32[4,32,256]{2,0,1:T(4,128)S(1)}, f32[4,32,256]{2,0,1:T(4,128)S(1)}, u32[]{:S(2)}, u32[]{:S(2)}) collective-permute-start(f32[4,32,256]{2,0,1:T(4,128)S(1)} %get-tuple-element.102), channel_id=1, source_target_pairs={{0,96},{32,0},{64,32},{96,64},{1,97},{33,1},{65,33},{97,65},{2,98}... | collective-permute-start | bytes 393224 | tf_op jit(solution)/shard_map/ppermute | solution.py:43
  296.6 17.8 %collective-permute-start.16 = (f32[15,32,256]{2,0,1:T(8,128)S(1)}, f32[15,32,256]{2,0,1:T(8,128)S(1)}, u32[]{:S(2)}, u32[]{:S(2)}) collective-permute-start(f32[15,32,256]{2,0,1:T(8,128)S(1)} %get-tuple-element.71), channel_id=1, source_target_pairs={{0,1},{1,2},{2,3},{3,4},{4,5},{5,6},{6,7},{7,8},{8,9},{9,10},{10,1... | collective-permute-start | bytes 1474568 | tf_op jit(solution)/shard_map/ppermute | solution.py:17
  298.5 21.5 %collective-permute-start.17 = (f32[15,32,256]{2,0,1:T(8,128)S(1)}, f32[15,32,256]{2,0,1:T(8,128)S(1)}, u32[]{:S(2)}, u32[]{:S(2)}) collective-permute-start(f32[15,32,256]{2,0,1:T(8,128)S(1)} %get-tuple-element.72), channel_id=1, source_target_pairs={{1,0},{2,1},{3,2},{4,3},{5,4},{6,5},{7,6},{8,7},{9,8},{10,9},{11,1... | collective-permute-start | bytes 1474568 | tf_op jit(solution)/shard_map/ppermute | solution.py:19
  304.5 20.4 %collective-permute-start.26 = (f32[15,32,256]{2,0,1:T(8,128)S(1)}, f32[15,32,256]{2,0,1:T(8,128)S(1)}, u32[]{:S(2)}, u32[]{:S(2)}) collective-permute-start(f32[15,32,256]{2,0,1:T(8,128)S(1)} %get-tuple-element.76), channel_id=1, source_target_pairs={{0,1},{1,2},{2,3},{3,4},{4,5},{5,6},{6,7},{7,8},{8,9},{9,10},{10,1... | collective-permute-start | bytes 1474568 | tf_op jit(solution)/shard_map/ppermute | solution.py:17
  306.4 24.4 %collective-permute-start.27 = (f32[15,32,256]{2,0,1:T(8,128)S(1)}, f32[15,32,256]{2,0,1:T(8,128)S(1)}, u32[]{:S(2)}, u32[]{:S(2)}) collective-permute-start(f32[15,32,256]{2,0,1:T(8,128)S(1)} %get-tuple-element.77), channel_id=1, source_target_pairs={{1,0},{2,1},{3,2},{4,3},{5,4},{6,5},{7,6},{8,7},{9,8},{10,9},{11,1... | collective-permute-start | bytes 1474568 | tf_op jit(solution)/shard_map/ppermute | solution.py:19
  312.3 21.4 %collective-permute-start.36 = (f32[15,32,256]{2,0,1:T(8,128)S(1)}, f32[15,32,256]{2,0,1:T(8,128)S(1)}, u32[]{:S(2)}, u32[]{:S(2)}) collective-permute-start(f32[15,32,256]{2,0,1:T(8,128)S(1)} %get-tuple-element.81), channel_id=1, source_target_pairs={{0,1},{1,2},{2,3},{3,4},{4,5},{5,6},{6,7},{7,8},{8,9},{9,10},{10,1... | collective-permute-start | bytes 1474568 | tf_op jit(solution)/shard_map/ppermute | solution.py:17
  314.3 19.3 %collective-permute-start.37 = (f32[15,32,256]{2,0,1:T(8,128)S(1)}, f32[15,32,256]{2,0,1:T(8,128)S(1)}, u32[]{:S(2)}, u32[]{:S(2)}) collective-permute-start(f32[15,32,256]{2,0,1:T(8,128)S(1)} %get-tuple-element.82), channel_id=1, source_target_pairs={{1,0},{2,1},{3,2},{4,3},{5,4},{6,5},{7,6},{8,7},{9,8},{10,9},{11,1... | collective-permute-start | bytes 1474568 | tf_op jit(solution)/shard_map/ppermute | solution.py:19
  320.1 16.4 %collective-permute-start.46 = (f32[15,32,256]{2,0,1:T(8,128)S(1)}, f32[15,32,256]{2,0,1:T(8,128)S(1)}, u32[]{:S(2)}, u32[]{:S(2)}) collective-permute-start(f32[15,32,256]{2,0,1:T(8,128)S(1)} %get-tuple-element.86), channel_id=1, source_target_pairs={{0,1},{1,2},{2,3},{3,4},{4,5},{5,6},{6,7},{7,8},{8,9},{9,10},{10,1... | collective-permute-start | bytes 1474568 | tf_op jit(solution)/shard_map/ppermute | solution.py:17
  324.9 12.4 %collective-permute-start.47 = (f32[15,32,256]{2,0,1:T(8,128)S(1)}, f32[15,32,256]{2,0,1:T(8,128)S(1)}, u32[]{:S(2)}, u32[]{:S(2)}) collective-permute-start(f32[15,32,256]{2,0,1:T(8,128)S(1)} %get-tuple-element.87), channel_id=1, source_target_pairs={{1,0},{2,1},{3,2},{4,3},{5,4},{6,5},{7,6},{8,7},{9,8},{10,9},{11,1... | collective-permute-start | bytes 1474568 | tf_op jit(solution)/shard_map/ppermute | solution.py:19
  351.8 20.4 %collective-permute-start.64 = (f32[2,15,32,256]{3,2,1,0:T(8,128)S(1)}, f32[2,15,32,256]{3,2,1,0:T(8,128)S(1)}, u32[]{:S(2)}, u32[]{:S(2)}) collective-permute-start(f32[2,15,32,256]{3,2,1,0:T(8,128)S(1)} %get-tuple-element.47), channel_id=1, source_target_pairs={{0,1},{1,2},{2,3},{3,4},{4,5},{5,6},{6,7},{7,8},{8,9},{9,10},{10,1... | collective-permute-start | bytes 2949128 | tf_op jit(solution)/shard_map/ppermute | solution.py:17
  353.7 24.3 %collective-permute-start.65 = (f32[2,15,32,256]{3,2,1,0:T(8,128)S(1)}, f32[2,15,32,256]{3,2,1,0:T(8,128)S(1)}, u32[]{:S(2)}, u32[]{:S(2)}) collective-permute-start(f32[2,15,32,256]{3,2,1,0:T(8,128)S(1)} %get-tuple-element.48), channel_id=1, source_target_pairs={{1,0},{2,1},{3,2},{4,3},{5,4},{6,5},{7,6},{8,7},{9,8},{10,9},{11,1... | collective-permute-start | bytes 2949128 | tf_op jit(solution)/shard_map/ppermute | solution.py:19
  361.0 22.8 %collective-permute-start.72 = (f32[2,15,32,256]{3,2,1,0:T(8,128)S(1)}, f32[2,15,32,256]{3,2,1,0:T(8,128)S(1)}, u32[]{:S(2)}, u32[]{:S(2)}) collective-permute-start(f32[2,15,32,256]{3,2,1,0:T(8,128)S(1)} %get-tuple-element.49), channel_id=1, source_target_pairs={{0,1},{1,2},{2,3},{3,4},{4,5},{5,6},{6,7},{7,8},{8,9},{9,10},{10,1... | collective-permute-start | bytes 2949128 | tf_op jit(solution)/shard_map/ppermute | solution.py:17
  362.9 26.8 %collective-permute-start.73 = (f32[2,15,32,256]{3,2,1,0:T(8,128)S(1)}, f32[2,15,32,256]{3,2,1,0:T(8,128)S(1)}, u32[]{:S(2)}, u32[]{:S(2)}) collective-permute-start(f32[2,15,32,256]{3,2,1,0:T(8,128)S(1)} %get-tuple-element.50), channel_id=1, source_target_pairs={{1,0},{2,1},{3,2},{4,3},{5,4},{6,5},{7,6},{8,7},{9,8},{10,9},{11,1... | collective-permute-start | bytes 2949128 | tf_op jit(solution)/shard_map/ppermute | solution.py:19
  370.1 23.5 %collective-permute-start.48 = (f32[2,15,32,256]{3,2,1,0:T(8,128)S(1)}, f32[2,15,32,256]{3,2,1,0:T(8,128)S(1)}, u32[]{:S(2)}, u32[]{:S(2)}) collective-permute-start(f32[2,15,32,256]{3,2,1,0:T(8,128)S(1)} %get-tuple-element.43), channel_id=1, source_target_pairs={{0,1},{1,2},{2,3},{3,4},{4,5},{5,6},{6,7},{7,8},{8,9},{9,10},{10,1... | collective-permute-start | bytes 2949128 | tf_op jit(solution)/shard_map/ppermute | solution.py:17
  372.2 23.1 %collective-permute-start.49 = (f32[2,15,32,256]{3,2,1,0:T(8,128)S(1)}, f32[2,15,32,256]{3,2,1,0:T(8,128)S(1)}, u32[]{:S(2)}, u32[]{:S(2)}) collective-permute-start(f32[2,15,32,256]{3,2,1,0:T(8,128)S(1)} %get-tuple-element.44), channel_id=1, source_target_pairs={{1,0},{2,1},{3,2},{4,3},{5,4},{6,5},{7,6},{8,7},{9,8},{10,9},{11,1... | collective-permute-start | bytes 2949128 | tf_op jit(solution)/shard_map/ppermute | solution.py:19
  378.0 23.9 %collective-permute-start.56 = (f32[2,15,32,256]{3,2,1,0:T(8,128)S(1)}, f32[2,15,32,256]{3,2,1,0:T(8,128)S(1)}, u32[]{:S(2)}, u32[]{:S(2)}) collective-permute-start(f32[2,15,32,256]{3,2,1,0:T(8,128)S(1)} %get-tuple-element.45), channel_id=1, source_target_pairs={{0,1},{1,2},{2,3},{3,4},{4,5},{5,6},{6,7},{7,8},{8,9},{9,10},{10,1... | collective-permute-start | bytes 2949128 | tf_op jit(solution)/shard_map/ppermute | solution.py:17
  383.8 19.0 %collective-permute-start.57 = (f32[2,15,32,256]{3,2,1,0:T(8,128)S(1)}, f32[2,15,32,256]{3,2,1,0:T(8,128)S(1)}, u32[]{:S(2)}, u32[]{:S(2)}) collective-permute-start(f32[2,15,32,256]{3,2,1,0:T(8,128)S(1)} %get-tuple-element.46), channel_id=1, source_target_pairs={{1,0},{2,1},{3,2},{4,3},{5,4},{6,5},{7,6},{8,7},{9,8},{10,9},{11,1... | collective-permute-start | bytes 2949128 | tf_op jit(solution)/shard_map/ppermute | solution.py:19
  389.7 15.4 %collective-permute-start.66 = (f32[4,32,256]{2,0,1:T(4,128)S(1)}, f32[4,32,256]{2,0,1:T(4,128)S(1)}, u32[]{:S(2)}, u32[]{:S(2)}) collective-permute-start(f32[4,32,256]{2,0,1:T(4,128)S(1)} %get-tuple-element.65), channel_id=1, source_target_pairs={{0,32},{32,64},{64,96},{96,0},{1,33},{33,65},{65,97},{97,1},{2,34}... | collective-permute-start | bytes 393224 | tf_op jit(solution)/shard_map/ppermute | solution.py:37
  393.6 13.4 %collective-permute-start.67 = (f32[4,32,256]{2,0,1:T(4,128)S(1)}, f32[4,32,256]{2,0,1:T(4,128)S(1)}, u32[]{:S(2)}, u32[]{:S(2)}) collective-permute-start(f32[4,32,256]{2,0,1:T(4,128)S(1)} %get-tuple-element.67), channel_id=1, source_target_pairs={{0,64},{32,96},{64,0},{96,32},{1,65},{33,97},{65,1},{97,33},{2,66}... | collective-permute-start | bytes 393224 | tf_op jit(solution)/shard_map/ppermute | solution.py:37
  395.4 11.8 %collective-permute-start.68 = (f32[4,32,256]{2,0,1:T(4,128)S(1)}, f32[4,32,256]{2,0,1:T(4,128)S(1)}, u32[]{:S(2)}, u32[]{:S(2)}) collective-permute-start(f32[4,32,256]{2,0,1:T(4,128)S(1)} %get-tuple-element.66), channel_id=1, source_target_pairs={{0,96},{32,0},{64,32},{96,64},{1,97},{33,1},{65,33},{97,65},{2,98}... | collective-permute-start | bytes 393224 | tf_op jit(solution)/shard_map/ppermute | solution.py:37
  401.9 9.5 %collective-permute-start.74 = (f32[4,32,256]{2,0,1:T(4,128)S(1)}, f32[4,32,256]{2,0,1:T(4,128)S(1)}, u32[]{:S(2)}, u32[]{:S(2)}) collective-permute-start(f32[4,32,256]{2,0,1:T(4,128)S(1)} %get-tuple-element.68), channel_id=1, source_target_pairs={{0,32},{32,64},{64,96},{96,0},{1,33},{33,65},{65,97},{97,1},{2,34}... | collective-permute-start | bytes 393224 | tf_op jit(solution)/shard_map/ppermute | solution.py:37
  402.9 12.0 %collective-permute-start.75 = (f32[4,32,256]{2,0,1:T(4,128)S(1)}, f32[4,32,256]{2,0,1:T(4,128)S(1)}, u32[]{:S(2)}, u32[]{:S(2)}) collective-permute-start(f32[4,32,256]{2,0,1:T(4,128)S(1)} %get-tuple-element.70), channel_id=1, source_target_pairs={{0,64},{32,96},{64,0},{96,32},{1,65},{33,97},{65,1},{97,33},{2,66}... | collective-permute-start | bytes 393224 | tf_op jit(solution)/shard_map/ppermute | solution.py:37
  405.1 11.9 %collective-permute-start.76 = (f32[4,32,256]{2,0,1:T(4,128)S(1)}, f32[4,32,256]{2,0,1:T(4,128)S(1)}, u32[]{:S(2)}, u32[]{:S(2)}) collective-permute-start(f32[4,32,256]{2,0,1:T(4,128)S(1)} %get-tuple-element.69), channel_id=1, source_target_pairs={{0,96},{32,0},{64,32},{96,64},{1,97},{33,1},{65,33},{97,65},{2,98}... | collective-permute-start | bytes 393224 | tf_op jit(solution)/shard_map/ppermute | solution.py:37
  407.0 9.9 %collective-permute-start.50 = (f32[4,32,256]{2,0,1:T(4,128)S(1)}, f32[4,32,256]{2,0,1:T(4,128)S(1)}, u32[]{:S(2)}, u32[]{:S(2)}) collective-permute-start(f32[4,32,256]{2,0,1:T(4,128)S(1)} %get-tuple-element.59), channel_id=1, source_target_pairs={{0,32},{32,64},{64,96},{96,0},{1,33},{33,65},{65,97},{97,1},{2,34}... | collective-permute-start | bytes 393224 | tf_op jit(solution)/shard_map/ppermute | solution.py:37
  407.2 12.6 %collective-permute-start.51 = (f32[4,32,256]{2,0,1:T(4,128)S(1)}, f32[4,32,256]{2,0,1:T(4,128)S(1)}, u32[]{:S(2)}, u32[]{:S(2)}) collective-permute-start(f32[4,32,256]{2,0,1:T(4,128)S(1)} %get-tuple-element.61), channel_id=1, source_target_pairs={{0,64},{32,96},{64,0},{96,32},{1,65},{33,97},{65,1},{97,33},{2,66}... | collective-permute-start | bytes 393224 | tf_op jit(solution)/shard_map/ppermute | solution.py:37
  420.2 10.8 %collective-permute-start.53 = (f32[4,32,256]{2,0,1:T(4,128)S(1)}, f32[4,32,256]{2,0,1:T(4,128)S(1)}, u32[]{:S(2)}, u32[]{:S(2)}) collective-permute-start(f32[4,32,256]{2,0,1:T(4,128)S(1)} %get-tuple-element.14), channel_id=1, source_target_pairs={{0,32},{32,64},{64,96},{96,0},{1,33},{33,65},{65,97},{97,1},{2,34}... | collective-permute-start | bytes 393224 | tf_op jit(solution)/shard_map/ppermute | solution.py:43
  420.3 10.8 %collective-permute-start.54 = (f32[4,32,256]{2,0,1:T(4,128)S(1)}, f32[4,32,256]{2,0,1:T(4,128)S(1)}, u32[]{:S(2)}, u32[]{:S(2)}) collective-permute-start(f32[4,32,256]{2,0,1:T(4,128)S(1)} %get-tuple-element.14), channel_id=1, source_target_pairs={{0,64},{32,96},{64,0},{96,32},{1,65},{33,97},{65,1},{97,33},{2,66}... | collective-permute-start | bytes 393224 | tf_op jit(solution)/shard_map/ppermute | solution.py:43
  423.1 10.1 %collective-permute-start.55 = (f32[4,32,256]{2,0,1:T(4,128)S(1)}, f32[4,32,256]{2,0,1:T(4,128)S(1)}, u32[]{:S(2)}, u32[]{:S(2)}) collective-permute-start(f32[4,32,256]{2,0,1:T(4,128)S(1)} %get-tuple-element.14), channel_id=1, source_target_pairs={{0,96},{32,0},{64,32},{96,64},{1,97},{33,1},{65,33},{97,65},{2,98}... | collective-permute-start | bytes 393224 | tf_op jit(solution)/shard_map/ppermute | solution.py:43
  425.9 9.4 %collective-permute-start.61 = (f32[4,32,256]{2,0,1:T(4,128)S(1)}, f32[4,32,256]{2,0,1:T(4,128)S(1)}, u32[]{:S(2)}, u32[]{:S(2)}) collective-permute-start(f32[4,32,256]{2,0,1:T(4,128)S(1)} %get-tuple-element.16), channel_id=1, source_target_pairs={{0,32},{32,64},{64,96},{96,0},{1,33},{33,65},{65,97},{97,1},{2,34}... | collective-permute-start | bytes 393224 | tf_op jit(solution)/shard_map/ppermute | solution.py:43
  427.9 9.7 %collective-permute-start.62 = (f32[4,32,256]{2,0,1:T(4,128)S(1)}, f32[4,32,256]{2,0,1:T(4,128)S(1)}, u32[]{:S(2)}, u32[]{:S(2)}) collective-permute-start(f32[4,32,256]{2,0,1:T(4,128)S(1)} %get-tuple-element.16), channel_id=1, source_target_pairs={{0,64},{32,96},{64,0},{96,32},{1,65},{33,97},{65,1},{97,33},{2,66}... | collective-permute-start | bytes 393224 | tf_op jit(solution)/shard_map/ppermute | solution.py:43
  431.1 9.4 %collective-permute-start.69 = (f32[4,32,256]{2,0,1:T(4,128)S(1)}, f32[4,32,256]{2,0,1:T(4,128)S(1)}, u32[]{:S(2)}, u32[]{:S(2)}) collective-permute-start(f32[4,32,256]{2,0,1:T(4,128)S(1)} %get-tuple-element.98), channel_id=1, source_target_pairs={{0,32},{32,64},{64,96},{96,0},{1,33},{33,65},{65,97},{97,1},{2,34}... | collective-permute-start | bytes 393224 | tf_op jit(solution)/shard_map/ppermute | solution.py:43
  433.2 9.1 %collective-permute-start.70 = (f32[4,32,256]{2,0,1:T(4,128)S(1)}, f32[4,32,256]{2,0,1:T(4,128)S(1)}, u32[]{:S(2)}, u32[]{:S(2)}) collective-permute-start(f32[4,32,256]{2,0,1:T(4,128)S(1)} %get-tuple-element.98), channel_id=1, source_target_pairs={{0,64},{32,96},{64,0},{96,32},{1,65},{33,97},{65,1},{97,33},{2,66}... | collective-permute-start | bytes 393224 | tf_op jit(solution)/shard_map/ppermute | solution.py:43
  (25 other events, 231.3 us)
